TPU v7x, 32 devices: a whole 2x2x4 slice. The times are simulated.
32 devices in a mesh: videos: 2 (over y), group: 16 (over z, x, core).
Axes of the slice: x: 2, y: 2, z: 4, core: 2. Of those that a mesh axis runs over, the one named last changes fastest.
Arguments:
- queries: bfloat16 [4096, 3072], P(('videos', 'group')), parts along dimension 0, may hold values from -90 to 90
- fresh_keys: bfloat16 [4096, 3072], P(('videos', 'group')), parts along dimension 0, may hold values from -8.375 to 8.375
- fresh_values: bfloat16 [4096, 3072], P(('videos', 'group')), parts along dimension 0, may hold values from -6 to 6
- cache_keys: bfloat16 [64, 3072], P(('videos', 'group')), parts along dimension 0, may hold values from -9 to 9
- cache_values: bfloat16 [64, 3072], P(('videos', 'group')), parts along dimension 0, may hold values from -6 to 6
- lengths: int32 [32], P(('videos', 'group')), parts along dimension 0, may hold values from 1 to 128, 1228 in all
- levels: int32 [32], P(('videos', 'group')), parts along dimension 0, may hold values from 0 to 15
- gate_table: float32 [16, 3072], replicated, may hold values from -24 to 24
Outputs:
- modulated: bfloat16 [4096, 3072], P(('videos', 'group')), parts along dimension 0
There are 2 independent parts, one for each index of `videos`. A program takes and returns all parts, laid end to end along the dimension named above; an argument that names none is the same for every part. Nothing has to cross between parts.
Inputs may be any that keep to these rules, and one draw needn't show every extreme that they name: Each video block has 128 slots, the first lengths of them live; the lengths sum to 1228 in each video; in every draw some block is full.
All inputs are finite; a program needn't handle non-finite values.
Results may differ from a plain program's by a relative error of at most 0.0045.
Values may be sent and summed in bfloat16 or wider, within the bound.
No kernel may reach another device: no remote copies, remote signals or barrier semaphores. Data moves between devices by JAX's collectives and lax.ppermute only.
A program may use at most 64 MiB of HBM per device.

v0:
```python
import math

import jax
import jax.numpy as jnp
from jax import lax
from jax.sharding import PartitionSpec as P

HEAD_DIM = 128
WIN = 4


def passed_along(x, axis, by):
    size = lax.axis_size(axis)
    pairs = [(i, i + by) for i in range(size) if 0 <= i + by < size]
    return lax.ppermute(x, axis, pairs)


def attend_block(carry_state, query_heads, key_block, value_block, live_mask):
    running_max, denominator, accumulated = carry_state
    head_count = query_heads.shape[1]
    head_depth = query_heads.shape[2]
    key_heads = key_block.reshape(key_block.shape[0], head_count, head_depth)
    value_heads = value_block.reshape(value_block.shape[0], head_count, head_depth)
    scores = jnp.einsum("thd,khd->htk", query_heads, key_heads, preferred_element_type=jnp.float32)
    scores = scores * (1.0 / math.sqrt(head_depth))
    scores = jnp.where(live_mask[None, None, :], scores, -jnp.inf)
    new_max = jnp.maximum(running_max, jnp.max(scores, axis=2))
    rescale = jnp.exp(running_max - new_max)
    probabilities = jnp.exp(scores - new_max[:, :, None])
    denominator = denominator * rescale + jnp.sum(probabilities, axis=2)
    weights = probabilities.astype(jnp.bfloat16)
    product = jnp.einsum("htk,khd->thd", weights, value_heads, preferred_element_type=jnp.float32)
    accumulated = accumulated * jnp.transpose(rescale)[:, :, None] + product
    return (new_max, denominator, accumulated)


def body(queries, fresh_keys, fresh_values, cache_keys, cache_values, lengths, levels, gate_table):
    row_count, feat_width = queries.shape
    head_depth = HEAD_DIM
    head_count = feat_width // head_depth
    query_heads = queries.reshape(row_count, head_count, head_depth)
    slot_index = jnp.arange(row_count, dtype=jnp.int32)
    window_span = WIN
    key_slabs = [fresh_keys]
    value_slabs = [fresh_values]
    length_slabs = [lengths]
    current = (fresh_keys, fresh_values, lengths)
    for offset in range(1, window_span):
        current = passed_along((current[0], current[1], current[2]), "group", 1)
        key_slabs.append(current[0])
        value_slabs.append(current[1])
        length_slabs.append(current[2])
    key_stack = jnp.stack(key_slabs, 0)
    value_stack = jnp.stack(value_slabs, 0)
    length_stack = jnp.concatenate(length_slabs, 0)
    live_stack = slot_index[None, :] < length_stack[:, None]
    initial = (
        jnp.full((head_count, row_count), -jnp.inf, jnp.float32),
        jnp.zeros((head_count, row_count), jnp.float32),
        jnp.zeros((row_count, head_count, head_depth), jnp.float32),
    )
    carry_state = initial
    key_block = key_stack.reshape(-1, feat_width)
    value_block = value_stack.reshape(-1, feat_width)
    live_mask = live_stack.reshape(-1)
    carry_state = attend_block(carry_state, query_heads, key_block, value_block, live_mask)
    shard_piece = (
        lax.all_gather(cache_keys, "group", axis=0, tiled=True),
        lax.all_gather(cache_values, "group", axis=0, tiled=True),
    )
    live_mask = jnp.ones((shard_piece[0].shape[0],), jnp.bool_)
    final_state = attend_block(carry_state, query_heads, shard_piece[0], shard_piece[1], live_mask)
    running_max, denominator, accumulated = final_state
    attended = (accumulated / jnp.transpose(denominator)[:, :, None]).reshape(row_count, feat_width)
    level_index = jnp.arange(gate_table.shape[0], dtype=jnp.int32)
    onehot = (level_index[None, :] == levels[:, None]).astype(jnp.float32)
    gate_row = jnp.dot(onehot, gate_table, precision=lax.Precision.HIGHEST)
    modulated = jnp.where((slot_index < lengths[0])[:, None], attended * gate_row, 0.0)
    return modulated.astype(jnp.bfloat16)


def solution(mesh):
    return jax.shard_map(
        body,
        mesh=mesh,
        in_specs=(
            P(("videos", "group"), None),
            P(("videos", "group"), None),
            P(("videos", "group"), None),
            P(("videos", "group"), None),
            P(("videos", "group"), None),
            P(("videos", "group")),
            P(("videos", "group")),
            P(),
        ),
        out_specs=P(("videos", "group"), None),
        check_vma=False,
    )
```

profile of v0, /device:TPU:15, one launch (start us, length us, event | category | flops | bytes accessed | tf_op | source)
XLA Modules:
  0.0 115.3 jit_solution(9058750961986023422)
XLA Ops:
  0.0 0.0 copy-start
  0.0 0.0 copy-start.1
  0.0 3.9 %collective-permute-start.3 = (bf16[128,3072]{1,0:T(8,128)(2,1)}, bf16[128,3072]{1,0:T(8,128)(2,1)S(1)}, u32[]{:S(2)}, u32[]{:S(2)}) collective-permute-start(bf16[128,3072]{1,0:T(8,128)(2,1)} %param.9), channel_id=1, source_target_pairs={{0,1},{1,2},{2,3},{3,4},{4,5},{5,6},{6,7},{7,8},{8,9},{9,10},{10,1... | collective-permute-start | bytes 2359304 | tf_op jit(solution)/shard_map/ppermute | solution.py:15
  3.9 1.9 %collective-permute-start.6 = (bf16[128,3072]{1,0:T(8,128)(2,1)}, bf16[128,3072]{1,0:T(8,128)(2,1)S(1)}, u32[]{:S(2)}, u32[]{:S(2)}) collective-permute-start(bf16[128,3072]{1,0:T(8,128)(2,1)} %param.10), channel_id=1, source_target_pairs={{0,1},{1,2},{2,3},{3,4},{4,5},{5,6},{6,7},{7,8},{8,9},{9,10},{10,1... | collective-permute-start | bytes 2359304 | tf_op jit(solution)/shard_map/ppermute | solution.py:15
  5.8 7.3 %collective-permute-done.3 = bf16[128,3072]{1,0:T(8,128)(2,1)S(1)} collective-permute-done((bf16[128,3072]{1,0:T(8,128)(2,1)}, bf16[128,3072]{1,0:T(8,128)(2,1)S(1)}, u32[]{:S(2)}, u32[]{:S(2)}) %collective-permute-start.3) | collective-permute-done | bytes 786464 | tf_op jit(solution)/shard_map/ppermute | solution.py:15
  13.1 5.2 %collective-permute-start.4 = (bf16[128,3072]{1,0:T(8,128)(2,1)S(1)}, bf16[128,3072]{1,0:T(8,128)(2,1)}, u32[]{:S(2)}, u32[]{:S(2)}) collective-permute-start(bf16[128,3072]{1,0:T(8,128)(2,1)S(1)} %collective-permute-done.3), channel_id=1, source_target_pairs={{0,1},{1,2},{2,3},{3,4},{4,5},{5,6},{6,7},{7,8},{8,9},{9,10},{10,1... | collective-permute-start | bytes 2359304 | tf_op jit(solution)/shard_map/ppermute | solution.py:15
  18.3 3.2 %collective-permute-done.6 = bf16[128,3072]{1,0:T(8,128)(2,1)S(1)} collective-permute-done((bf16[128,3072]{1,0:T(8,128)(2,1)}, bf16[128,3072]{1,0:T(8,128)(2,1)S(1)}, u32[]{:S(2)}, u32[]{:S(2)}) %collective-permute-start.6) | collective-permute-done | bytes 786464 | tf_op jit(solution)/shard_map/ppermute | solution.py:15
  21.5 5.2 %collective-permute-start.7 = (bf16[128,3072]{1,0:T(8,128)(2,1)S(1)}, bf16[128,3072]{1,0:T(8,128)(2,1)}, u32[]{:S(2)}, u32[]{:S(2)}) collective-permute-start(bf16[128,3072]{1,0:T(8,128)(2,1)S(1)} %collective-permute-done.6), channel_id=1, source_target_pairs={{0,1},{1,2},{2,3},{3,4},{4,5},{5,6},{6,7},{7,8},{8,9},{9,10},{10,1... | collective-permute-start | bytes 2359304 | tf_op jit(solution)/shard_map/ppermute | solution.py:15
  26.7 1.9 %collective-permute-start = (s32[1]{0:T(128)}, s32[1]{0:T(128)}, u32[]{:S(2)}, u32[]{:S(2)}) collective-permute-start(s32[1]{0:T(128)} %param.13), channel_id=1, source_target_pairs={{0,1},{1,2},{2,3},{3,4},{4,5},{5,6},{6,7},{7,8},{8,9},{9,10},{10,1... | collective-permute-start | bytes 20 | tf_op jit(solution)/shard_map/ppermute | solution.py:15
  29.9 20.5 %all-gather = bf16[16,2,3072]{2,1,0:T(2,128)(2,1)S(1)} all-gather(bf16[1,2,3072]{2,1,0:T(2,128)(2,1)} %bitcast.97), channel_id=1, replica_groups=mesh['videos'=2,'group'=16] {'group'}, dimensions={0}, use_global_device_ids=true | all-gather | bytes 208896 | tf_op jit(solution)/shard_map/all_gather | solution.py:68
  50.4 0.8 reshape.50
  51.2 1.7 %fusion.34 = f32[1,3072]{1,0:T(1,128)} fusion(f32[16,3072]{1,0:T(8,128)} %param.15, s32[]{:T(128)} %bitcast.86), kind=kOutput, calls=%fused_computation.43 | convolution fusion | flops 589840 | bytes 208900 | tf_op jit(solution)/shard_map/dot_general | solution.py:77
  52.9 0.0 collective-permute-done.4
  53.0 2.0 %collective-permute-start.5 = (bf16[128,3072]{1,0:T(8,128)(2,1)}, bf16[128,3072]{1,0:T(8,128)(2,1)}, u32[]{:S(2)}, u32[]{:S(2)}) collective-permute-start(bf16[128,3072]{1,0:T(8,128)(2,1)} %collective-permute-done.4), channel_id=1, source_target_pairs={{0,1},{1,2},{2,3},{3,4},{4,5},{5,6},{6,7},{7,8},{8,9},{9,10},{10,1... | collective-permute-start | bytes 2359304 | tf_op jit(solution)/shard_map/ppermute | solution.py:15
  55.0 0.0 copy-done
  55.0 1.5 %fusion.42 = (f32[24,128]{1,0:T(8,128)S(1)}, f32[24,128,32]{1,2,0:T(8,128)S(1)}) fusion(bf16[32,24,128]{2,1,0:T(8,128)(2,1)} %reshape.50, bf16[128,3072]{1,0:T(8,128)(2,1)S(1)} %copy-done), kind=kOutput, calls=%fused_computation.52 | convolution fusion | flops 25359360 | bytes 1388544 | tf_op jit(solution)/shard_map/thd,khd->htk/dot_general | solution.py:24
  56.5 0.0 collective-permute-done.7
  56.5 2.1 %collective-permute-start.8 = (bf16[128,3072]{1,0:T(8,128)(2,1)}, bf16[128,3072]{1,0:T(8,128)(2,1)}, u32[]{:S(2)}, u32[]{:S(2)}) collective-permute-start(bf16[128,3072]{1,0:T(8,128)(2,1)} %collective-permute-done.7), channel_id=1, source_target_pairs={{0,1},{1,2},{2,3},{3,4},{4,5},{5,6},{6,7},{7,8},{8,9},{9,10},{10,1... | collective-permute-start | bytes 2359304 | tf_op jit(solution)/shard_map/ppermute | solution.py:15
  58.6 29.4 %all-gather.1 = bf16[16,2,3072]{2,1,0:T(2,128)(2,1)} all-gather(bf16[1,2,3072]{2,1,0:T(2,128)(2,1)} %bitcast.98), channel_id=1, replica_groups=mesh['videos'=2,'group'=16] {'group'}, dimensions={0}, use_global_device_ids=true | all-gather | bytes 208896 | tf_op jit(solution)/shard_map/all_gather | solution.py:69
  88.0 1.7 %reshape.51 = bf16[32,24,128]{2,1,0:T(8,128)(2,1)} reshape(bf16[16,2,3072]{2,1,0:T(2,128)(2,1)} %all-gather.1) | data formatting | bytes 393216 | tf_op jit(solution)/shard_map/reshape | solution.py:23
  89.7 0.0 collective-permute-done
  89.7 1.9 %collective-permute-start.1 = (s32[1]{0:T(128)}, s32[1]{0:T(128)}, u32[]{:S(2)}, u32[]{:S(2)}) collective-permute-start(s32[1]{0:T(128)} %collective-permute-done), channel_id=1, source_target_pairs={{0,1},{1,2},{2,3},{3,4},{4,5},{5,6},{6,7},{7,8},{8,9},{9,10},{10,1... | collective-permute-start | bytes 20 | tf_op jit(solution)/shard_map/ppermute | solution.py:15
  91.6 1.2 %collective-permute-done.1 = s32[1]{0:T(128)} collective-permute-done((s32[1]{0:T(128)}, s32[1]{0:T(128)}, u32[]{:S(2)}, u32[]{:S(2)}) %collective-permute-start.1) | collective-permute-done | bytes 36 | tf_op jit(solution)/shard_map/ppermute | solution.py:15
  92.8 4.8 %collective-permute-start.2 = (s32[1]{0:T(128)}, s32[1]{0:T(128)}, u32[]{:S(2)}, u32[]{:S(2)}) collective-permute-start(s32[1]{0:T(128)} %collective-permute-done.1), channel_id=1, source_target_pairs={{0,1},{1,2},{2,3},{3,4},{4,5},{5,6},{6,7},{7,8},{8,9},{9,10},{10,1... | collective-permute-start | bytes 20 | tf_op jit(solution)/shard_map/ppermute | solution.py:15
  97.6 0.9 collective-permute-done.2
  98.5 1.9 %pad_add_fusion = s32[4]{0:T(128)S(1)} fusion(s32[1]{0:T(128)} %collective-permute-done.2, s32[1]{0:T(128)} %collective-permute-done.1, s32[1]{0:T(128)} %collective-permute-done, s32[1]{0:T(128)} %copy.61), kind=kLoop, calls=%fused_computation.46 | loop fusion | flops 12 | bytes 32 | tf_op jit(solution)/shard_map/concatenate | solution.py:55
  100.4 0.1 fusion.33
  100.5 0.0 collective-permute-done.5
  100.5 0.0 copy-done.1
  100.5 1.6 %pad_maximum_fusion = bf16[4,128,3072]{2,1,0:T(8,128)(2,1)S(1)} fusion(bf16[1,128,3072]{2,1,0:T(8,128)(2,1)} %bitcast.5, bf16[1,128,3072]{2,1,0:T(8,128)(2,1)} %bitcast.4, bf16[1,128,3072]{2,1,0:T(8,128)(2,1)S(1)} %bitcast.95, bf16[1,128,3072]{2,1,0:T(8,128)(2,1)S(1)} %bitcast.92), kind=kLoop, calls=%fused_computation.7 | loop fusion | flops 4718592 | bytes 6291456 | tf_op jit(solution)/shard_map/stack | solution.py:53
  102.1 0.0 copy-start.2
  102.1 0.9 copy.33
  102.9 0.0 collective-permute-done.8
  103.0 0.3 copy-done.2
  103.2 1.6 %pad_maximum_fusion.1 = bf16[4,128,3072]{2,1,0:T(8,128)(2,1)S(1)} fusion(bf16[1,128,3072]{2,1,0:T(8,128)(2,1)} %bitcast.11, bf16[1,128,3072]{2,1,0:T(8,128)(2,1)} %bitcast.10, bf16[1,128,3072]{2,1,0:T(8,128)(2,1)S(1)} %bitcast.94, bf16[1,128,3072]{2,1,0:T(8,128)(2,1)S(1)} %bitcast.93), kind=kLoop, calls=%fused_computation.8 | loop fusion | flops 4718592 | bytes 6291456 | tf_op jit(solution)/shard_map/stack | solution.py:54
  104.8 0.9 copy.34
  105.6 1.2 %bitcast_reduce_fusion = (f32[24,128]{1,0:T(8,128)S(1)}, f32[24,512,128]{2,1,0:T(8,128)S(1)}) fusion(pred[512]{0:T(512)(128)(4,1)S(1)} %fusion.33, bf16[512,24,128]{2,1,0:T(8,128)(2,1)S(1)} %bitcast.90, bf16[128,3072]{1,0:T(8,128)(2,1)S(1)} %copy-done), kind=kOutput, calls=%fused_computation.1 | convolution fusion | flops 407368704 | bytes 10236416 | tf_op jit(solution)/shard_map/thd,khd->htk/dot_general | solution.py:24
  106.9 0.0 copy-start.3
  106.9 1.4 %fusion.1 = f32[24,128]{1,0:T(8,128)S(1)} fusion(f32[24,512,128]{2,1,0:T(8,128)S(1)} %get-tuple-element.9, f32[24,128]{1,0:T(8,128)S(1)} %get-tuple-element.8, pred[512]{0:T(512)(128)(4,1)S(1)} %fusion.33), kind=kLoop, calls=%fused_computation.4 | loop fusion | flops 6288384 | bytes 6316544 | tf_op jit(solution)/shard_map/reduce_sum | solution.py:30
  108.3 0.1 fusion.22
  108.4 0.0 copy-done.3
  108.4 0.4 fusion.24
  108.8 3.5 %fusion.12 = f32[128,24,128]{0,2,1:T(8,128)} fusion(f32[24,128,128]{1,2,0:T(8,128)S(1)} %fusion.24, f32[24,512,128]{2,1,0:T(8,128)S(1)} %get-tuple-element.9, f32[24,128]{1,0:T(8,128)S(1)} %get-tuple-element.8, pred[512]{0:T(512)(128)(4,1)S(1)} %fusion.33, bf16[512,24,128]{2,1,0:T(8,128)(2,1)S(1)} %bitcast.89, f32[128,24]{0,1:T(8,128)S(1)} %get-tuple-element.5, ...), kind=kOutput, calls=%fused_computation.17 | convolution fusion | flops 410517504 | bytes 12632576 | tf_op jit(solution)/shard_map/htk,khd->thd/dot_general | solution.py:32
  112.3 0.0 copy-start.4
  112.3 1.9 %copy.29 = f32[128,3072]{1,0:T(8,128)S(1)} copy(f32[128,3072]{0,1:T(8,128)} %bitcast.91) | data formatting | bytes 3145728 | tf_op jit(solution)/shard_map/reshape | solution.py:74
  114.2 0.0 copy-done.4
  114.2 1.1 select_convert_fusion
  (3 shorter events, 0.0 us)
Async XLA Ops:
  0.0 55.0 %copy-start = (bf16[128,3072]{1,0:T(8,128)(2,1)S(1)}, bf16[128,3072]{1,0:T(8,128)(2,1)}, u32[]{:S(2)}) copy-start(bf16[128,3072]{1,0:T(8,128)(2,1)} %param.8) | copy-start | bytes 2359300
  0.0 100.5 %copy-start.1 = (bf16[128,3072]{1,0:T(8,128)(2,1)S(1)}, bf16[128,3072]{1,0:T(8,128)(2,1)}, u32[]{:S(2)}) copy-start(bf16[128,3072]{1,0:T(8,128)(2,1)} %param.9) | copy-start | bytes 2359300
  0.0 13.1 %collective-permute-start.3 = (bf16[128,3072]{1,0:T(8,128)(2,1)}, bf16[128,3072]{1,0:T(8,128)(2,1)S(1)}, u32[]{:S(2)}, u32[]{:S(2)}) collective-permute-start(bf16[128,3072]{1,0:T(8,128)(2,1)} %param.9), channel_id=1, source_target_pairs={{0,1},{1,2},{2,3},{3,4},{4,5},{5,6},{6,7},{7,8},{8,9},{9,10},{10,1... | collective-permute-start | bytes 2359304 | tf_op jit(solution)/shard_map/ppermute | solution.py:15
  3.9 17.7 %collective-permute-start.6 = (bf16[128,3072]{1,0:T(8,128)(2,1)}, bf16[128,3072]{1,0:T(8,128)(2,1)S(1)}, u32[]{:S(2)}, u32[]{:S(2)}) collective-permute-start(bf16[128,3072]{1,0:T(8,128)(2,1)} %param.10), channel_id=1, source_target_pairs={{0,1},{1,2},{2,3},{3,4},{4,5},{5,6},{6,7},{7,8},{8,9},{9,10},{10,1... | collective-permute-start | bytes 2359304 | tf_op jit(solution)/shard_map/ppermute | solution.py:15
  13.1 39.9 %collective-permute-start.4 = (bf16[128,3072]{1,0:T(8,128)(2,1)S(1)}, bf16[128,3072]{1,0:T(8,128)(2,1)}, u32[]{:S(2)}, u32[]{:S(2)}) collective-permute-start(bf16[128,3072]{1,0:T(8,128)(2,1)S(1)} %collective-permute-done.3), channel_id=1, source_target_pairs={{0,1},{1,2},{2,3},{3,4},{4,5},{5,6},{6,7},{7,8},{8,9},{9,10},{10,1... | collective-permute-start | bytes 2359304 | tf_op jit(solution)/shard_map/ppermute | solution.py:15
  21.5 35.0 %collective-permute-start.7 = (bf16[128,3072]{1,0:T(8,128)(2,1)S(1)}, bf16[128,3072]{1,0:T(8,128)(2,1)}, u32[]{:S(2)}, u32[]{:S(2)}) collective-permute-start(bf16[128,3072]{1,0:T(8,128)(2,1)S(1)} %collective-permute-done.6), channel_id=1, source_target_pairs={{0,1},{1,2},{2,3},{3,4},{4,5},{5,6},{6,7},{7,8},{8,9},{9,10},{10,1... | collective-permute-start | bytes 2359304 | tf_op jit(solution)/shard_map/ppermute | solution.py:15
  26.7 63.0 %collective-permute-start = (s32[1]{0:T(128)}, s32[1]{0:T(128)}, u32[]{:S(2)}, u32[]{:S(2)}) collective-permute-start(s32[1]{0:T(128)} %param.13), channel_id=1, source_target_pairs={{0,1},{1,2},{2,3},{3,4},{4,5},{5,6},{6,7},{7,8},{8,9},{9,10},{10,1... | collective-permute-start | bytes 20 | tf_op jit(solution)/shard_map/ppermute | solution.py:15
  53.0 47.5 %collective-permute-start.5 = (bf16[128,3072]{1,0:T(8,128)(2,1)}, bf16[128,3072]{1,0:T(8,128)(2,1)}, u32[]{:S(2)}, u32[]{:S(2)}) collective-permute-start(bf16[128,3072]{1,0:T(8,128)(2,1)} %collective-permute-done.4), channel_id=1, source_target_pairs={{0,1},{1,2},{2,3},{3,4},{4,5},{5,6},{6,7},{7,8},{8,9},{9,10},{10,1... | collective-permute-start | bytes 2359304 | tf_op jit(solution)/shard_map/ppermute | solution.py:15
  56.5 46.4 %collective-permute-start.8 = (bf16[128,3072]{1,0:T(8,128)(2,1)}, bf16[128,3072]{1,0:T(8,128)(2,1)}, u32[]{:S(2)}, u32[]{:S(2)}) collective-permute-start(bf16[128,3072]{1,0:T(8,128)(2,1)} %collective-permute-done.7), channel_id=1, source_target_pairs={{0,1},{1,2},{2,3},{3,4},{4,5},{5,6},{6,7},{7,8},{8,9},{9,10},{10,1... | collective-permute-start | bytes 2359304 | tf_op jit(solution)/shard_map/ppermute | solution.py:15
  89.7 3.1 %collective-permute-start.1 = (s32[1]{0:T(128)}, s32[1]{0:T(128)}, u32[]{:S(2)}, u32[]{:S(2)}) collective-permute-start(s32[1]{0:T(128)} %collective-permute-done), channel_id=1, source_target_pairs={{0,1},{1,2},{2,3},{3,4},{4,5},{5,6},{6,7},{7,8},{8,9},{9,10},{10,1... | collective-permute-start | bytes 20 | tf_op jit(solution)/shard_map/ppermute | solution.py:15
  92.8 5.7 %collective-permute-start.2 = (s32[1]{0:T(128)}, s32[1]{0:T(128)}, u32[]{:S(2)}, u32[]{:S(2)}) collective-permute-start(s32[1]{0:T(128)} %collective-permute-done.1), channel_id=1, source_target_pairs={{0,1},{1,2},{2,3},{3,4},{4,5},{5,6},{6,7},{7,8},{8,9},{9,10},{10,1... | collective-permute-start | bytes 20 | tf_op jit(solution)/shard_map/ppermute | solution.py:15
  102.1 1.1 copy-start.2
  106.9 1.5 %copy-start.3 = (bf16[32,24,128]{2,1,0:T(8,128)(2,1)S(1)}, bf16[32,24,128]{2,1,0:T(8,128)(2,1)}, u32[]{:S(2)}) copy-start(bf16[32,24,128]{2,1,0:T(8,128)(2,1)} %reshape.51) | copy-start | bytes 589828
  112.3 1.9 %copy-start.4 = (f32[1,3072]{1,0:T(1,128)S(1)}, f32[1,3072]{1,0:T(1,128)}, u32[]{:S(2)}) copy-start(f32[1,3072]{1,0:T(1,128)} %fusion.34) | copy-start | bytes 36868
where the time goes:
time: 118 us; the launch traced here: 115 us
  blocking collectives  49.9 us (42%)
  starting transfers between devices  28.8 us (24%)
  waiting for transfers between devices  12.6 us (11%)
  matrix products  8.34 us (7%)
  other arithmetic  7.73 us (7%)
  local copies, waits for them, and re-layouts  6.4 us (5%)
  between operations  1.54 us (1%)
    all_gather x1, blocking collectives, body(): lax.all_gather(cache_values, 'group', axis=0, tiled=True)  29.4 us
    ppermute x9, starting transfers between devices, passed_along(): return lax.ppermute(x, axis, pairs)  28.8 us
    all_gather x1, blocking collectives, body(): lax.all_gather(cache_keys, 'group', axis=0, tiled=True)  20.5 us
    ppermute x9, waiting for transfers between devices, passed_along(): return lax.ppermute(x, axis, pairs)  12.6 us
    dot_general x2, matrix products, attend_block(): jnp.einsum('htk,khd->thd', weights, value_heads, preferred_element_type=j...  3.95 us
    dot_general x2, matrix products, attend_block(): jnp.einsum('thd,khd->htk', query_heads, key_heads, preferred_element_type...  2.68 us
  transfers between devices with their start and end apart: 9, of which 4 were waited for; matrix products, arithmetic and copies ran while one was open for 9% of the time, Pallas kernels for 0%

commit v1 on v0

--- a/solution.py
+++ b/solution.py
@@ -7,12 +7,6 @@
 
 HEAD_DIM = 128
 WIN = 4
-
-
-def passed_along(x, axis, by):
-    size = lax.axis_size(axis)
-    pairs = [(i, i + by) for i in range(size) if 0 <= i + by < size]
-    return lax.ppermute(x, axis, pairs)
 
 
 def attend_block(carry_state, query_heads, key_block, value_block, live_mask):
@@ -38,38 +32,48 @@
     row_count, feat_width = queries.shape
     head_depth = HEAD_DIM
     head_count = feat_width // head_depth
+    size = lax.axis_size("group")
+    me = lax.axis_index("group")
     query_heads = queries.reshape(row_count, head_count, head_depth)
     slot_index = jnp.arange(row_count, dtype=jnp.int32)
-    window_span = WIN
-    key_slabs = [fresh_keys]
-    value_slabs = [fresh_values]
-    length_slabs = [lengths]
-    current = (fresh_keys, fresh_values, lengths)
-    for offset in range(1, window_span):
-        current = passed_along((current[0], current[1], current[2]), "group", 1)
-        key_slabs.append(current[0])
-        value_slabs.append(current[1])
-        length_slabs.append(current[2])
-    key_stack = jnp.stack(key_slabs, 0)
-    value_stack = jnp.stack(value_slabs, 0)
-    length_stack = jnp.concatenate(length_slabs, 0)
-    live_stack = slot_index[None, :] < length_stack[:, None]
+
+    cache_rows = cache_keys.shape[0]
+    length_row = jnp.zeros((1, feat_width), jnp.bfloat16).at[0, 0].set(lengths[0].astype(jnp.bfloat16))
+    packed = jnp.concatenate([cache_keys, cache_values, length_row], 0)
+    gathered = lax.all_gather(packed, "group", axis=0, tiled=False)
+    all_cache_keys = gathered[:, :cache_rows].reshape(-1, feat_width)
+    all_cache_values = gathered[:, cache_rows:2 * cache_rows].reshape(-1, feat_width)
+    all_lengths = gathered[:, 2 * cache_rows, 0].astype(jnp.int32)
+
+    kv = jnp.stack([fresh_keys, fresh_values], 0)
+    pairs_two = [(i, i + 2) for i in range(size - 2)]
+    pairs_mixed = [(i, i + 1) for i in range(0, size - 1, 2)] + [(i, i + 3) for i in range(1, size - 3, 2)]
+    from_two = lax.ppermute(kv, "group", pairs_two)
+    from_mixed = lax.ppermute(kv, "group", pairs_mixed)
+    pairs_swap = [(i, i ^ 1) for i in range(size)]
+    from_swap = lax.ppermute(from_two, "group", pairs_swap)
+
+    odd = (me % 2) == 1
+    offset_mixed = jnp.where(odd, 1, 3)
+    offset_swap = jnp.where(odd, 3, 1)
+
+    def length_at(offset):
+        source = me - offset
+        return jnp.where(source >= 0, all_lengths[jnp.maximum(source, 0)], 0)
+
+    block_lengths = jnp.stack([lengths[0], length_at(offset_mixed), length_at(2), length_at(offset_swap)])
+    key_block = jnp.concatenate([fresh_keys, from_mixed[0], from_two[0], from_swap[0]], 0)
+    value_block = jnp.concatenate([fresh_values, from_mixed[1], from_two[1], from_swap[1]], 0)
+    live_mask = (slot_index[None, :] < block_lengths[:, None]).reshape(-1)
+
     initial = (
         jnp.full((head_count, row_count), -jnp.inf, jnp.float32),
         jnp.zeros((head_count, row_count), jnp.float32),
         jnp.zeros((row_count, head_count, head_depth), jnp.float32),
     )
-    carry_state = initial
-    key_block = key_stack.reshape(-1, feat_width)
-    value_block = value_stack.reshape(-1, feat_width)
-    live_mask = live_stack.reshape(-1)
-    carry_state = attend_block(carry_state, query_heads, key_block, value_block, live_mask)
-    shard_piece = (
-        lax.all_gather(cache_keys, "group", axis=0, tiled=True),
-        lax.all_gather(cache_values, "group", axis=0, tiled=True),
-    )
-    live_mask = jnp.ones((shard_piece[0].shape[0],), jnp.bool_)
-    final_state = attend_block(carry_state, query_heads, shard_piece[0], shard_piece[1], live_mask)
+    carry_state = attend_block(initial, query_heads, key_block, value_block, live_mask)
+    cache_live = jnp.ones((all_cache_keys.shape[0],), jnp.bool_)
+    final_state = attend_block(carry_state, query_heads, all_cache_keys, all_cache_values, cache_live)
     running_max, denominator, accumulated = final_state
     attended = (accumulated / jnp.transpose(denominator)[:, :, None]).reshape(row_count, feat_width)
     level_index = jnp.arange(gate_table.shape[0], dtype=jnp.int32)

time: 118 us -> 106 us (0.90)
  the two profiles are of different devices: /device:TPU:15 before, /device:TPU:0 now
where the time goes in v1:
time: 106 us; the launch traced here: 105 us
  blocking collectives  59.6 us (56%)
  local copies, waits for them, and re-layouts  18 us (17%)
  matrix products  9.9 us (9%)
  starting transfers between devices  9.07 us (9%)
  other arithmetic  4.76 us (4%)
  between operations  4.02 us (4%)
    all_gather x1, blocking collectives, body(): gathered = lax.all_gather(packed, 'group', axis=0, tiled=False)  59.6 us
    ppermute x1, starting transfers between devices, body(): from_two = lax.ppermute(kv, 'group', pairs_two)  6.04 us
    dot_general x2, matrix products, attend_block(): jnp.einsum('thd,khd->htk', query_heads, key_heads, preferred_element_type...  5.12 us
    concatenate x4, local copies, waits for them, and re-layouts, body(): jnp.concatenate([fresh_keys, from_mixed[0], from_two[0], from_swap[0]], 0)  4.76 us
    dot_general x2, matrix products, attend_block(): jnp.einsum('htk,khd->thd', weights, value_heads, preferred_element_type=j...  3.68 us
    unnamed x14, local copies, waits for them, and re-layouts  3.23 us
    ppermute x1, starting transfers between devices, body(): from_mixed = lax.ppermute(kv, 'group', pairs_mixed)  2.61 us
    slice x1, local copies, waits for them, and re-layouts, body(): from_mixed[1]  2.37 us
  transfers between devices with their start and end apart: 3, of which 0 were waited for; matrix products, arithmetic and copies ran while one was open for 11% of the time, Pallas kernels for 0%

profile of v1, /device:TPU:0, one launch (start us, length us, event | category | flops | bytes accessed | tf_op | source)
XLA Modules:
  0.0 105.4 jit_solution(311849105212902045)
XLA Ops:
  0.0 0.0 copy-start
  0.0 0.0 copy-start.4
  0.0 0.0 copy-start.5
  0.0 1.6 %copy.33 = bf16[128,3072]{0,1:T(8,128)(2,1)S(1)} copy(bf16[128,3072]{1,0:T(8,128)(2,1)} %param.12) | data formatting | bytes 1572864 | tf_op args[2]
  1.6 1.5 %copy.31 = bf16[128,3072]{0,1:T(8,128)(2,1)S(1)} copy(bf16[128,3072]{1,0:T(8,128)(2,1)} %param.11) | data formatting | bytes 1572864 | tf_op args[1]
  3.1 1.3 %pad_maximum_fusion = bf16[2,128,3072]{1,2,0:T(8,128)(2,1)} fusion(bf16[1,128,3072]{1,2,0:T(8,128)(2,1)S(1)} %bitcast.95, bf16[1,128,3072]{1,2,0:T(8,128)(2,1)S(1)} %bitcast.93), kind=kLoop, calls=%fused_computation.26 | loop fusion | flops 786432 | bytes 3145728 | tf_op jit(solution)/shard_map/stack | solution.py:48
  4.4 6.0 %collective-permute-start.1 = (bf16[2,128,3072]{1,2,0:T(8,128)(2,1)}, bf16[2,128,3072]{1,2,0:T(8,128)(2,1)}, u32[]{:S(2)}, u32[]{:S(2)}) collective-permute-start(bf16[2,128,3072]{1,2,0:T(8,128)(2,1)} %pad_maximum_fusion), channel_id=1, source_target_pairs={{0,2},{1,3},{2,4},{3,5},{4,6},{5,7},{6,8},{7,9},{8,10},{9,11},{10,... | collective-permute-start | bytes 4718600 | tf_op jit(solution)/shard_map/ppermute | solution.py:51
  10.5 2.6 %collective-permute-start = (bf16[2,128,3072]{1,2,0:T(8,128)(2,1)}, bf16[2,128,3072]{1,2,0:T(8,128)(2,1)}, u32[]{:S(2)}, u32[]{:S(2)}) collective-permute-start(bf16[2,128,3072]{1,2,0:T(8,128)(2,1)} %pad_maximum_fusion), channel_id=1, source_target_pairs={{0,1},{2,3},{4,5},{6,7},{8,9},{10,11},{12,13},{14,15},{1,4},{3,6},... | collective-permute-start | bytes 4718600 | tf_op jit(solution)/shard_map/ppermute | solution.py:52
  13.1 0.6 compare_reduce_fusion
  15.0 0.0 copy-done.4
  15.0 0.0 copy-done.5
  15.1 59.6 %all-gather.1 = bf16[16,5,3072]{2,1,0:T(8,128)(2,1)S(1)} all-gather(bf16[1,5,3072]{2,1,0:T(8,128)(2,1)S(1)} %fusion.44), channel_id=2, replica_groups=mesh['videos'=2,'group'=16] {'group'}, dimensions={0}, use_global_device_ids=true | all-gather | bytes 522240 | tf_op jit(solution)/shard_map/all_gather | solution.py:43
  74.8 0.5 constant_dynamic-slice_fusion.2
  77.1 0.3 fusion.63
  77.4 0.1 pad_add_fusion
  77.5 0.1 reshape_reshape.6
  77.6 0.1 reshape_reshape.7
  77.8 1.2 %copy.34 = bf16[128,24,128]{2,0,1:T(8,128)(2,1)} copy(bf16[128,24,128]{0,2,1:T(8,128)(2,1)S(1)} %bitcast.94) | data formatting | bytes 1572864 | tf_op jit(solution)/shard_map/concatenate | solution.py:65
  79.6 0.1 fusion.49
  79.7 1.1 %fusion.50 = f32[1,3072]{1,0:T(1,128)S(1)} fusion(f32[16,3072]{1,0:T(8,128)} %param.17, s32[]{:T(128)} %bitcast.92), kind=kOutput, calls=%fused_computation.60 | convolution fusion | flops 589840 | bytes 208900 | tf_op jit(solution)/shard_map/dot_general | solution.py:81
  80.8 0.0 copy-done
  80.8 0.5 fusion.64
  81.3 0.0 collective-permute-done.1
  81.3 0.4 collective-permute-start.2
  81.8 2.3 %fusion.61 = (bf16[1,128,3072]{1,2,0:T(8,128)(2,1)}, bf16[1,128,3072]{1,2,0:T(8,128)(2,1)S(1)}) fusion(bf16[2,128,3072]{1,2,0:T(8,128)(2,1)} %collective-permute-done.1), kind=kLoop, calls=%fused_computation.76 | loop fusion | bytes 3145728 | tf_op jit(solution)/shard_map/slice | solution.py:66
  84.1 1.2 %copy.36 = bf16[128,24,128]{2,0,1:T(8,128)(2,1)} copy(bf16[128,24,128]{0,2,1:T(8,128)(2,1)S(1)} %bitcast.99) | data formatting | bytes 1572864 | tf_op jit(solution)/shard_map/concatenate | solution.py:65
  85.3 0.0 collective-permute-done
  85.3 2.4 %fusion.60 = (bf16[1,128,3072]{1,2,0:T(8,128)(2,1)}, bf16[1,128,3072]{1,2,0:T(8,128)(2,1)S(1)}) fusion(bf16[2,128,3072]{1,2,0:T(8,128)(2,1)} %collective-permute-done), kind=kLoop, calls=%fused_computation.75 | loop fusion | bytes 3145728 | tf_op jit(solution)/shard_map/slice | solution.py:66
  87.7 1.2 %copy.35 = bf16[128,24,128]{2,0,1:T(8,128)(2,1)} copy(bf16[128,24,128]{0,2,1:T(8,128)(2,1)S(1)} %bitcast.97) | data formatting | bytes 1572864 | tf_op jit(solution)/shard_map/concatenate | solution.py:65
  88.9 0.0 collective-permute-done.2
  88.9 2.4 %fusion.62 = (bf16[1,128,3072]{1,2,0:T(8,128)(2,1)}, bf16[1,128,3072]{1,2,0:T(8,128)(2,1)S(1)}) fusion(bf16[2,128,3072]{1,2,0:T(8,128)(2,1)} %collective-permute-done.2), kind=kLoop, calls=%fused_computation.77 | loop fusion | bytes 3145728 | tf_op jit(solution)/shard_map/slice | solution.py:66
  91.2 1.2 %copy.37 = bf16[128,24,128]{2,0,1:T(8,128)(2,1)} copy(bf16[128,24,128]{0,2,1:T(8,128)(2,1)S(1)} %bitcast.98) | data formatting | bytes 1572864 | tf_op jit(solution)/shard_map/concatenate | solution.py:65
  92.4 4.6 %bitcast_reduce_fusion = (f32[24,128]{1,0:T(8,128)S(1)}, f32[24,512,128]{2,1,0:T(8,128)S(1)}) fusion(pred[512]{0:T(512)(128)(4,1)S(1)} %fusion.49, bf16[128,24,128]{2,0,1:T(8,128)(2,1)} %copy.37, bf16[128,24,128]{2,0,1:T(8,128)(2,1)} %copy.36, bf16[128,24,128]{2,0,1:T(8,128)(2,1)} %copy.35, bf16[128,24,128]{2,0,1:T(8,128)(2,1)} %copy.34, ...), kind=kOutput, calls=%fused_computation.1 | convolution fusion | flops 419951616 | bytes 10236416 | tf_op jit(solution)/shard_map/thd,khd->htk/dot_general | solution.py:18
  97.0 0.1 fusion.35
  97.1 0.4 fusion.37
  97.5 0.0 copy-start.1
  97.5 0.0 copy-start.2
  97.6 0.0 copy-start.3
  97.6 1.4 %fusion.1 = f32[24,128]{1,0:T(8,128)S(1)} fusion(f32[24,512,128]{2,1,0:T(8,128)S(1)} %get-tuple-element.32, f32[24,128]{1,0:T(8,128)S(1)} %get-tuple-element.31, pred[512]{0:T(512)(128)(4,1)S(1)} %fusion.49), kind=kLoop, calls=%fused_computation.4 | loop fusion | flops 6288384 | bytes 6316544 | tf_op jit(solution)/shard_map/reduce_sum | solution.py:24
  99.0 0.0 copy-done.1
  99.0 0.0 copy-done.2
  99.0 0.1 copy-done.3
  99.2 3.3 %fusion.24 = f32[128,24,128]{0,2,1:T(8,128)} fusion(f32[24,128,128]{2,1,0:T(8,128)S(1)} %fusion.37, f32[24,512,128]{2,1,0:T(8,128)S(1)} %get-tuple-element.32, f32[24,128]{1,0:T(8,128)S(1)} %get-tuple-element.31, pred[512]{0:T(512)(128)(4,1)S(1)} %fusion.49, bf16[128,24,128]{0,2,1:T(8,128)(2,1)S(1)} %bitcast.103, bf16[128,24,128]{0,2,1:T(8,128)(2,1)S(1)} %bitcast.101, ...), kind=kOutput, calls=%fused_computation.28 | convolution fusion | flops 423100416 | bytes 12632576 | tf_op jit(solution)/shard_map/htk,khd->thd/dot_general | solution.py:26
  102.4 1.9 %copy.44 = f32[128,3072]{1,0:T(8,128)S(1)} copy(f32[128,3072]{0,1:T(8,128)} %bitcast.100) | data formatting | bytes 3145728 | tf_op jit(solution)/shard_map/reshape | solution.py:78
  104.3 1.1 %select_convert_fusion = bf16[128,3072]{1,0:T(8,128)(2,1)} fusion(f32[128,3072]{1,0:T(8,128)S(1)} %copy.44, f32[3072]{0:T(1024)S(1)} %bitcast.104, pred[128]{0:T(512)(128)(4,1)S(1)} %iota_compare_fusion.2), kind=kLoop, calls=%fused_computation.31 | loop fusion | flops 1179648 | bytes 2371712 | tf_op jit(solution)/shard_map/convert_element_type | solution.py:83
  (5 shorter events, 0.1 us)
Async XLA Ops:
  0.0 80.8 %copy-start = (bf16[128,3072]{1,0:T(8,128)(2,1)S(1)}, bf16[128,3072]{1,0:T(8,128)(2,1)}, u32[]{:S(2)}) copy-start(bf16[128,3072]{1,0:T(8,128)(2,1)} %param.10) | copy-start | bytes 2359300
  0.0 15.0 %copy-start.4 = (bf16[2,3072]{1,0:T(2,128)(2,1)S(1)}, bf16[2,3072]{1,0:T(2,128)(2,1)}, u32[]{:S(2)}) copy-start(bf16[2,3072]{1,0:T(2,128)(2,1)} %param.14) | copy-start | bytes 36868
  0.0 15.0 %copy-start.5 = (bf16[2,3072]{1,0:T(2,128)(2,1)S(1)}, bf16[2,3072]{1,0:T(2,128)(2,1)}, u32[]{:S(2)}) copy-start(bf16[2,3072]{1,0:T(2,128)(2,1)} %param.13) | copy-start | bytes 36868
  4.4 76.9 %collective-permute-start.1 = (bf16[2,128,3072]{1,2,0:T(8,128)(2,1)}, bf16[2,128,3072]{1,2,0:T(8,128)(2,1)}, u32[]{:S(2)}, u32[]{:S(2)}) collective-permute-start(bf16[2,128,3072]{1,2,0:T(8,128)(2,1)} %pad_maximum_fusion), channel_id=1, source_target_pairs={{0,2},{1,3},{2,4},{3,5},{4,6},{5,7},{6,8},{7,9},{8,10},{9,11},{10,... | collective-permute-start | bytes 4718600 | tf_op jit(solution)/shard_map/ppermute | solution.py:51
  10.5 74.9 %collective-permute-start = (bf16[2,128,3072]{1,2,0:T(8,128)(2,1)}, bf16[2,128,3072]{1,2,0:T(8,128)(2,1)}, u32[]{:S(2)}, u32[]{:S(2)}) collective-permute-start(bf16[2,128,3072]{1,2,0:T(8,128)(2,1)} %pad_maximum_fusion), channel_id=1, source_target_pairs={{0,1},{2,3},{4,5},{6,7},{8,9},{10,11},{12,13},{14,15},{1,4},{3,6},... | collective-permute-start | bytes 4718600 | tf_op jit(solution)/shard_map/ppermute | solution.py:52
  81.3 7.6 %collective-permute-start.2 = (bf16[2,128,3072]{1,2,0:T(8,128)(2,1)}, bf16[2,128,3072]{1,2,0:T(8,128)(2,1)}, u32[]{:S(2)}, u32[]{:S(2)}) collective-permute-start(bf16[2,128,3072]{1,2,0:T(8,128)(2,1)} %collective-permute-done.1), channel_id=1, source_target_pairs={{0,1},{1,0},{2,3},{3,2},{4,5},{5,4},{6,7},{7,6},{8,9},{9,8},{10,11... | collective-permute-start | bytes 4718600 | tf_op jit(solution)/shard_map/ppermute | solution.py:54
  97.5 1.5 %copy-start.1 = (bf16[1,128,3072]{1,2,0:T(8,128)(2,1)S(1)}, bf16[1,128,3072]{1,2,0:T(8,128)(2,1)}, u32[]{:S(2)}) copy-start(bf16[1,128,3072]{1,2,0:T(8,128)(2,1)} %get-tuple-element.21) | copy-start | bytes 2359300
  97.5 1.5 %copy-start.2 = (bf16[1,128,3072]{1,2,0:T(8,128)(2,1)S(1)}, bf16[1,128,3072]{1,2,0:T(8,128)(2,1)}, u32[]{:S(2)}) copy-start(bf16[1,128,3072]{1,2,0:T(8,128)(2,1)} %get-tuple-element.19) | copy-start | bytes 2359300
  97.6 1.6 %copy-start.3 = (bf16[1,128,3072]{1,2,0:T(8,128)(2,1)S(1)}, bf16[1,128,3072]{1,2,0:T(8,128)(2,1)}, u32[]{:S(2)}) copy-start(bf16[1,128,3072]{1,2,0:T(8,128)(2,1)} %get-tuple-element.23) | copy-start | bytes 2359300

commit v2 on v1

v2 whole, which is shorter than its diff:
```python
import functools
import math

import jax
import jax.numpy as jnp
from jax import lax
from jax.experimental import pallas as pl
from jax.experimental.pallas import tpu as pltpu
from jax.sharding import PartitionSpec as P

HEAD_DIM = 128
WIN = 4
HEADS_PER_STEP = 4


def attention_kernel(table_ref, q_ref, k0, v0, k1, v1, k2, v2, k3, v3, ck, cv, gate_ref, o_ref, *, heads):
    scale = 1.0 / math.sqrt(HEAD_DIM)
    rows = q_ref.shape[0]
    slot = lax.broadcasted_iota(jnp.int32, (1, rows), 1)
    row = lax.broadcasted_iota(jnp.int32, (rows, 1), 0)
    level = table_ref[4]
    gate = gate_ref[pl.ds(level, 1), :]
    live_row = row < table_ref[0]
    blocks = ((k0, v0), (k1, v1), (k2, v2), (k3, v3))
    dims = (((1,), (1,)), ((), ()))
    for h in range(heads):
        cols = slice(h * HEAD_DIM, (h + 1) * HEAD_DIM)
        q = q_ref[:, cols]
        scores = []
        for j, (k_ref, _) in enumerate(blocks):
            s = lax.dot_general(q, k_ref[:, cols], dims, preferred_element_type=jnp.float32) * scale
            scores.append(jnp.where(slot < table_ref[j], s, -jnp.inf))
        scores.append(lax.dot_general(q, ck[:, cols], dims, preferred_element_type=jnp.float32) * scale)
        row_max = scores[0].max(axis=1, keepdims=True)
        for s in scores[1:]:
            row_max = jnp.maximum(row_max, s.max(axis=1, keepdims=True))
        values = [v_ref for _, v_ref in blocks] + [cv]
        denominator = jnp.zeros((rows, 1), jnp.float32)
        attended = jnp.zeros((rows, HEAD_DIM), jnp.float32)
        for s, v_ref in zip(scores, values):
            p = jnp.exp(s - row_max)
            denominator = denominator + p.sum(axis=1, keepdims=True)
            attended = attended + jnp.dot(p.astype(jnp.bfloat16), v_ref[:, cols], preferred_element_type=jnp.float32)
        attended = attended / denominator
        out = jnp.where(live_row, attended * gate[:, cols], 0.0)
        o_ref[:, cols] = out.astype(o_ref.dtype)


def attend(table, queries, kv_own, kv_a, kv_b, kv_c, cache_keys, cache_values, gate_table):
    rows, feat = queries.shape
    width = HEADS_PER_STEP * HEAD_DIM
    steps = feat // width
    cache_rows = cache_keys.shape[0]
    levels = gate_table.shape[0]
    row_block = pl.BlockSpec((rows, width), lambda h, t: (0, h))
    k_block = pl.BlockSpec((None, rows, width), lambda h, t: (0, 0, h))
    v_block = pl.BlockSpec((None, rows, width), lambda h, t: (1, 0, h))
    cache_block = pl.BlockSpec((cache_rows, width), lambda h, t: (0, h))
    gate_block = pl.BlockSpec((levels, width), lambda h, t: (0, h))
    grid_spec = pltpu.PrefetchScalarGridSpec(
        num_scalar_prefetch=1,
        grid=(steps,),
        in_specs=[row_block, k_block, v_block, k_block, v_block, k_block, v_block, k_block, v_block,
                  cache_block, cache_block, gate_block],
        out_specs=row_block,
    )
    keys = 4 * rows + cache_rows
    cost = pl.CostEstimate(
        flops=4 * rows * keys * feat,
        transcendentals=rows * keys * (feat // HEAD_DIM),
        bytes_accessed=2 * (2 * rows * feat + 8 * rows * feat + 2 * cache_rows * feat) + 4 * levels * feat,
    )
    return pl.pallas_call(
        functools.partial(attention_kernel, heads=HEADS_PER_STEP),
        out_shape=jax.ShapeDtypeStruct((rows, feat), jnp.bfloat16),
        grid_spec=grid_spec,
        cost_estimate=cost,
    )(table, queries, kv_own, kv_own, kv_a, kv_a, kv_b, kv_b, kv_c, kv_c, cache_keys, cache_values, gate_table)


def body(queries, fresh_keys, fresh_values, cache_keys, cache_values, lengths, levels, gate_table):
    row_count, feat_width = queries.shape
    size = lax.axis_size("group")
    me = lax.axis_index("group")

    cache_rows = cache_keys.shape[0]
    length_row = jnp.zeros((1, feat_width), jnp.bfloat16).at[0, 0].set(lengths[0].astype(jnp.bfloat16))
    packed = jnp.concatenate([cache_keys, cache_values, length_row], 0)
    gathered = lax.all_gather(packed, "group", axis=0, tiled=False)
    all_cache_keys = gathered[:, :cache_rows].reshape(-1, feat_width)
    all_cache_values = gathered[:, cache_rows:2 * cache_rows].reshape(-1, feat_width)
    all_lengths = gathered[:, 2 * cache_rows, 0].astype(jnp.int32)

    kv = jnp.stack([fresh_keys, fresh_values], 0)
    pairs_two = [(i, i + 2) for i in range(size - 2)]
    pairs_mixed = [(i, i + 1) for i in range(0, size - 1, 2)] + [(i, i + 3) for i in range(1, size - 3, 2)]
    from_two = lax.ppermute(kv, "group", pairs_two)
    from_mixed = lax.ppermute(kv, "group", pairs_mixed)
    pairs_swap = [(i, i ^ 1) for i in range(size)]
    from_swap = lax.ppermute(from_two, "group", pairs_swap)

    odd = (me % 2) == 1
    offset_mixed = jnp.where(odd, 1, 3)
    offset_swap = jnp.where(odd, 3, 1)

    def length_at(offset):
        source = me - offset
        return jnp.where(source >= 0, all_lengths[jnp.maximum(source, 0)], 0)

    table = jnp.stack([lengths[0], length_at(offset_mixed), length_at(2), length_at(offset_swap), levels[0]]).astype(jnp.int32)
    return attend(table, queries, kv, from_mixed, from_two, from_swap, all_cache_keys, all_cache_values, gate_table)


def solution(mesh):
    return jax.shard_map(
        body,
        mesh=mesh,
        in_specs=(
            P(("videos", "group"), None),
            P(("videos", "group"), None),
            P(("videos", "group"), None),
            P(("videos", "group"), None),
            P(("videos", "group"), None),
            P(("videos", "group")),
            P(("videos", "group")),
            P(),
        ),
        out_specs=P(("videos", "group"), None),
        check_vma=False,
    )
```

time: 106 us -> 90.7 us (0.86)
  waiting for transfers between devices: 0.01 us -> 30.9 us
  blocking collectives: 59.6 us -> 28.9 us
  local copies, waits for them, and re-layouts: 18 us -> 3.95 us
  Pallas kernels: 0 us -> 12 us
  matrix products: 9.9 us -> 0 us
  other arithmetic: 4.76 us -> 2.99 us
  starting transfers between devices: 9.07 us -> 7.6 us
    ppermute x1, waiting for transfers between devices: 0.01 us -> 30.9 us  [body(): from_two = lax.ppermute(kv, 'group', pairs_two)]
    all_gather x1, blocking collectives: 59.6 us -> 28.9 us  [body(): gathered = lax.all_gather(packed, 'group', axis=0, tiled=False)]
    pallas_call x0 -> x1, Pallas kernels: none -> 12 us  [attend(): pl.pallas_call(functools.partial(attention_kernel, heads=HEADS_PER_STEP),...]
    dot_general x5 -> x0, matrix products: 9.9 us -> none  [the longest x2 5.12 us: attend_block(): jnp.einsum('thd,khd->htk', query_heads, key_heads, preferred_element_type...]
    slice x3 -> x0, local copies, waits for them, and re-layouts: 7.06 us -> none  [the longest x1 2.37 us: body(): from_mixed[1]]
    concatenate x4 -> x0, local copies, waits for them, and re-layouts: 4.76 us -> none  [body(): jnp.concatenate([fresh_keys, from_mixed[0], from_two[0], from_swap[0]], 0)]
    unnamed x14 -> x10, local copies, waits for them, and re-layouts: 3.23 us -> 0.89 us
    reduce_sum x2 -> x0, other arithmetic: 1.49 us -> none  [attend_block(): denominator = denominator * rescale + jnp.sum(probabilities, axis=2)]
  transfers between devices with their start and end apart: 3 -> 3, of which waited for: 0 -> 1; matrix products, arithmetic and copies ran while one was open for 11% -> 5% of each run, Pallas kernels for 0% -> 0%
where the time goes in v2:
time: 90.7 us; the launch traced here: 90.4 us
  waiting for transfers between devices  30.9 us (34%)
  blocking collectives  28.9 us (32%)
  Pallas kernels  12 us (13%)
  starting transfers between devices  7.6 us (8%)
  between operations  3.99 us (4%)
  local copies, waits for them, and re-layouts  3.95 us (4%)
  other arithmetic  2.99 us (3%)
    ppermute x1, waiting for transfers between devices, body(): from_two = lax.ppermute(kv, 'group', pairs_two)  30.9 us
    all_gather x1, blocking collectives, body(): gathered = lax.all_gather(packed, 'group', axis=0, tiled=False)  28.9 us
    pallas_call x1, Pallas kernels, attend(): pl.pallas_call(functools.partial(attention_kernel, heads=HEADS_PER_STEP),...  12 us
    ppermute x1, starting transfers between devices, body(): from_two = lax.ppermute(kv, 'group', pairs_two)  4.97 us
    ppermute x1, starting transfers between devices, body(): from_mixed = lax.ppermute(kv, 'group', pairs_mixed)  2.62 us
  transfers between devices with their start and end apart: 3, of which 1 were waited for; matrix products, arithmetic and copies ran while one was open for 5% of the time, Pallas kernels for 0%

profile of v2, /device:TPU:0, one launch (start us, length us, event | category | flops | bytes accessed | tf_op | source)
XLA Modules:
  0.0 90.4 jit_solution(4948357971155998043)
XLA Ops:
  0.0 0.0 copy-start.3
  0.0 0.0 copy-start.4
  0.0 1.5 %pad_maximum_fusion.k0.v0 = bf16[2,128,3072]{2,1,0:T(8,128)(2,1)S(1)} fusion(bf16[1,128,3072]{2,1,0:T(8,128)(2,1)} %bitcast.12, bf16[1,128,3072]{2,1,0:T(8,128)(2,1)} %bitcast.13), kind=kLoop, calls=%fused_computation | loop fusion | flops 786432 | bytes 3145728 | tf_op jit(solution)/shard_map/stack | solution.py:94
  1.5 0.0 copy-start
  1.6 5.0 %collective-permute-start.1 = (bf16[2,128,3072]{2,1,0:T(8,128)(2,1)S(1)}, bf16[2,128,3072]{2,1,0:T(8,128)(2,1)S(1)}, u32[]{:S(2)}, u32[]{:S(2)}) collective-permute-start(bf16[2,128,3072]{2,1,0:T(8,128)(2,1)S(1)} %pad_maximum_fusion.k0.v0), channel_id=1, source_target_pairs={{0,2},{1,3},{2,4},{3,5},{4,6},{5,7},{6,8},{7,9},{8,10},{9,11},{10,... | collective-permute-start | bytes 4718600 | tf_op jit(solution)/shard_map/ppermute | solution.py:97
  6.5 2.6 %collective-permute-start = (bf16[2,128,3072]{2,1,0:T(8,128)(2,1)S(1)}, bf16[2,128,3072]{2,1,0:T(8,128)(2,1)}, u32[]{:S(2)}, u32[]{:S(2)}) collective-permute-start(bf16[2,128,3072]{2,1,0:T(8,128)(2,1)S(1)} %pad_maximum_fusion.k0.v0), channel_id=1, source_target_pairs={{0,1},{2,3},{4,5},{6,7},{8,9},{10,11},{12,13},{14,15},{1,4},{3,6},... | collective-permute-start | bytes 4718600 | tf_op jit(solution)/shard_map/ppermute | solution.py:98
  9.2 30.9 %collective-permute-done.1.k2.v2 = bf16[2,128,3072]{2,1,0:T(8,128)(2,1)S(1)} collective-permute-done((bf16[2,128,3072]{2,1,0:T(8,128)(2,1)S(1)}, bf16[2,128,3072]{2,1,0:T(8,128)(2,1)S(1)}, u32[]{:S(2)}, u32[]{:S(2)}) %collective-permute-start.1) | collective-permute-done | bytes 1572896 | tf_op jit(solution)/shard_map/ppermute | solution.py:97
  40.1 0.0 copy-start.1
  40.1 0.0 collective-permute-start.2
  41.4 0.6 compare_reduce_fusion
  42.7 0.0 copy-done.3
  42.7 0.0 copy-done.4
  42.7 28.9 %all-gather.1 = bf16[16,5,3072]{2,1,0:T(8,128)(2,1)S(1)} all-gather(bf16[1,5,3072]{2,1,0:T(8,128)(2,1)S(1)} %fusion.2), channel_id=2, replica_groups=mesh['videos'=2,'group'=16] {'group'}, dimensions={0}, use_global_device_ids=true | all-gather | bytes 522240 | tf_op jit(solution)/shard_map/all_gather | solution.py:89
  71.6 0.0 copy-start.2
  71.6 0.9 copy-done.2
  72.5 0.3 fusion.3
  72.8 0.8 reshape.50.cv
  73.5 0.7 reshape.49.ck
  74.3 0.8 slice_convert_fusion
  75.1 0.6 constant_dynamic-slice_fusion
  77.6 0.7 stack.24.table_ref
  78.3 0.0 collective-permute-done.k1.v1
  78.3 0.0 collective-permute-done.2.k3.v3
  78.3 0.0 copy-done
  78.3 0.0 copy-done.1
  78.3 12.0 %shard_map.82 = bf16[128,3072]{1,0:T(8,128)(2,1)} custom-call(s32[5]{0:T(128)} %stack.24.table_ref, bf16[128,3072]{1,0:T(8,128)(2,1)} %q_ref.1, bf16[2,128,3072]{2,1,0:T(8,128)(2,1)} %copy-done, bf16[2,128,3072]{2,1,0:T(8,128)(2,1)} %copy-done, bf16[2,128,3072]{2,1,0:T(8,128)(2,1)} %collective-permute-done.k1.v1, ...), custom_call_target="tpu_custom_call" | custom-call | flops 855638016 | bytes 8454144 | tf_op jit(solution)/shard_map/pallas_call | solution.py:73
  (1 shorter events, 0.0 us)
Async XLA Ops:
  0.0 42.7 %copy-start.3 = (bf16[2,3072]{1,0:T(2,128)(2,1)S(1)}, bf16[2,3072]{1,0:T(2,128)(2,1)}, u32[]{:S(2)}) copy-start(bf16[2,3072]{1,0:T(2,128)(2,1)} %param.14) | copy-start | bytes 36868
  0.0 42.7 %copy-start.4 = (bf16[2,3072]{1,0:T(2,128)(2,1)S(1)}, bf16[2,3072]{1,0:T(2,128)(2,1)}, u32[]{:S(2)}) copy-start(bf16[2,3072]{1,0:T(2,128)(2,1)} %param.13) | copy-start | bytes 36868
  1.5 76.8 %copy-start = (bf16[2,128,3072]{2,1,0:T(8,128)(2,1)}, bf16[2,128,3072]{2,1,0:T(8,128)(2,1)S(1)}, u32[]{:S(2)}) copy-start(bf16[2,128,3072]{2,1,0:T(8,128)(2,1)S(1)} %pad_maximum_fusion.k0.v0) | copy-start | bytes 4718596
  1.6 38.5 %collective-permute-start.1 = (bf16[2,128,3072]{2,1,0:T(8,128)(2,1)S(1)}, bf16[2,128,3072]{2,1,0:T(8,128)(2,1)S(1)}, u32[]{:S(2)}, u32[]{:S(2)}) collective-permute-start(bf16[2,128,3072]{2,1,0:T(8,128)(2,1)S(1)} %pad_maximum_fusion.k0.v0), channel_id=1, source_target_pairs={{0,2},{1,3},{2,4},{3,5},{4,6},{5,7},{6,8},{7,9},{8,10},{9,11},{10,... | collective-permute-start | bytes 4718600 | tf_op jit(solution)/shard_map/ppermute | solution.py:97
  6.5 71.8 %collective-permute-start = (bf16[2,128,3072]{2,1,0:T(8,128)(2,1)S(1)}, bf16[2,128,3072]{2,1,0:T(8,128)(2,1)}, u32[]{:S(2)}, u32[]{:S(2)}) collective-permute-start(bf16[2,128,3072]{2,1,0:T(8,128)(2,1)S(1)} %pad_maximum_fusion.k0.v0), channel_id=1, source_target_pairs={{0,1},{2,3},{4,5},{6,7},{8,9},{10,11},{12,13},{14,15},{1,4},{3,6},... | collective-permute-start | bytes 4718600 | tf_op jit(solution)/shard_map/ppermute | solution.py:98
  40.1 38.2 %copy-start.1 = (bf16[2,128,3072]{2,1,0:T(8,128)(2,1)}, bf16[2,128,3072]{2,1,0:T(8,128)(2,1)S(1)}, u32[]{:S(2)}) copy-start(bf16[2,128,3072]{2,1,0:T(8,128)(2,1)S(1)} %collective-permute-done.1.k2.v2) | copy-start | bytes 4718596
  40.1 38.2 %collective-permute-start.2 = (bf16[2,128,3072]{2,1,0:T(8,128)(2,1)S(1)}, bf16[2,128,3072]{2,1,0:T(8,128)(2,1)}, u32[]{:S(2)}, u32[]{:S(2)}) collective-permute-start(bf16[2,128,3072]{2,1,0:T(8,128)(2,1)S(1)} %collective-permute-done.1.k2.v2), channel_id=1, source_target_pairs={{0,1},{1,0},{2,3},{3,2},{4,5},{5,4},{6,7},{7,6},{8,9},{9,8},{10,11... | collective-permute-start | bytes 4718600 | tf_op jit(solution)/shard_map/ppermute | solution.py:100
  71.6 0.9 copy-start.2

commit v3 on v2

--- a/solution.py
+++ b/solution.py
@@ -78,18 +78,33 @@
     )(table, queries, kv_own, kv_own, kv_a, kv_a, kv_b, kv_b, kv_c, kv_c, cache_keys, cache_values, gate_table)
 
 
+def gather_pieces(piece, size):
+    if size & (size - 1):
+        return lax.all_gather(piece, "group", axis=0, tiled=False)
+    me = lax.axis_index("group")
+    held = piece[None]
+    step = size // 2
+    while step >= 1:
+        other = lax.ppermute(held, "group", [(i, i ^ step) for i in range(size)])
+        held = jnp.concatenate([held, other], 0)
+        step //= 2
+    return held
+
+
 def body(queries, fresh_keys, fresh_values, cache_keys, cache_values, lengths, levels, gate_table):
     row_count, feat_width = queries.shape
     size = lax.axis_size("group")
     me = lax.axis_index("group")
 
     cache_rows = cache_keys.shape[0]
-    length_row = jnp.zeros((1, feat_width), jnp.bfloat16).at[0, 0].set(lengths[0].astype(jnp.bfloat16))
-    packed = jnp.concatenate([cache_keys, cache_values, length_row], 0)
-    gathered = lax.all_gather(packed, "group", axis=0, tiled=False)
+    tag_row = jnp.zeros((1, feat_width), jnp.bfloat16)
+    tag_row = tag_row.at[0, 0].set(lengths[0].astype(jnp.bfloat16)).at[0, 1].set(me.astype(jnp.bfloat16))
+    packed = jnp.concatenate([cache_keys, cache_values, tag_row], 0)
+    gathered = gather_pieces(packed, size)
     all_cache_keys = gathered[:, :cache_rows].reshape(-1, feat_width)
     all_cache_values = gathered[:, cache_rows:2 * cache_rows].reshape(-1, feat_width)
-    all_lengths = gathered[:, 2 * cache_rows, 0].astype(jnp.int32)
+    piece_lengths = gathered[:, 2 * cache_rows, 0].astype(jnp.int32)
+    piece_index = gathered[:, 2 * cache_rows, 1].astype(jnp.int32)
 
     kv = jnp.stack([fresh_keys, fresh_values], 0)
     pairs_two = [(i, i + 2) for i in range(size - 2)]
@@ -105,7 +120,7 @@
 
     def length_at(offset):
         source = me - offset
-        return jnp.where(source >= 0, all_lengths[jnp.maximum(source, 0)], 0)
+        return jnp.sum(jnp.where(piece_index == source, piece_lengths, 0))
 
     table = jnp.stack([lengths[0], length_at(offset_mixed), length_at(2), length_at(offset_swap), levels[0]]).astype(jnp.int32)
     return attend(table, queries, kv, from_mixed, from_two, from_swap, all_cache_keys, all_cache_values, gate_table)

time: 90.7 us -> 89.4 us (0.986)
  the two profiles are of different devices: /device:TPU:0 before, /device:TPU:15 now
where the time goes in v3:
time: 89.4 us; the launch traced here: 87.8 us
  waiting for transfers between devices  47.6 us (53%)
  Pallas kernels  12 us (13%)
  local copies, waits for them, and re-layouts  10.7 us (12%)
  starting transfers between devices  8.2 us (9%)
  other arithmetic  7.17 us (8%)
  between operations  2.08 us (2%)
    ppermute x4, waiting for transfers between devices, gather_pieces(): other = lax.ppermute(held, 'group', [(i, i ^ step) for i in range(size)])  47.6 us
    pallas_call x1, Pallas kernels, attend(): pl.pallas_call(functools.partial(attention_kernel, heads=HEADS_PER_STEP),...  12 us
    ppermute x1, starting transfers between devices, body(): from_mixed = lax.ppermute(kv, 'group', pairs_mixed)  4.05 us
    ppermute x1, starting transfers between devices, body(): from_two = lax.ppermute(kv, 'group', pairs_two)  3.18 us
    another operation x3, other arithmetic  3.06 us
    another operation x1, local copies, waits for them, and re-layouts, body(): jnp.stack([lengths[0], length_at(offset_mixed), length_at(2), length_at(o...  2.62 us
    unnamed x11, local copies, waits for them, and re-layouts  1.98 us
  transfers between devices with their start and end apart: 7, of which 4 were waited for; matrix products, arithmetic and copies ran while one was open for 19% of the time, Pallas kernels for 0%

profile of v3, /device:TPU:15, one launch (start us, length us, event | category | flops | bytes accessed | tf_op | source)
XLA Modules:
  0.0 87.8 jit_solution(14634099626765279823)
XLA Ops:
  0.0 0.0 copy-start.2
  0.0 0.0 copy-start.3
  0.0 1.5 %pad_maximum_fusion.k0.v0 = bf16[2,128,3072]{2,1,0:T(8,128)(2,1)S(1)} fusion(bf16[1,128,3072]{2,1,0:T(8,128)(2,1)} %bitcast.14, bf16[1,128,3072]{2,1,0:T(8,128)(2,1)} %bitcast.15), kind=kLoop, calls=%fused_computation | loop fusion | flops 786432 | bytes 3145728 | tf_op jit(solution)/shard_map/stack | solution.py:109
  1.5 0.0 copy-start
  1.6 3.2 %collective-permute-start.5 = (bf16[2,128,3072]{2,1,0:T(8,128)(2,1)S(1)}, bf16[2,128,3072]{2,1,0:T(8,128)(2,1)S(1)}, u32[]{:S(2)}, u32[]{:S(2)}) collective-permute-start(bf16[2,128,3072]{2,1,0:T(8,128)(2,1)S(1)} %pad_maximum_fusion.k0.v0), channel_id=1, source_target_pairs={{0,2},{1,3},{2,4},{3,5},{4,6},{5,7},{6,8},{7,9},{8,10},{9,11},{10,... | collective-permute-start | bytes 4718600 | tf_op jit(solution)/shard_map/ppermute | solution.py:112
  4.7 4.0 %collective-permute-start.4 = (bf16[2,128,3072]{2,1,0:T(8,128)(2,1)S(1)}, bf16[2,128,3072]{2,1,0:T(8,128)(2,1)}, u32[]{:S(2)}, u32[]{:S(2)}) collective-permute-start(bf16[2,128,3072]{2,1,0:T(8,128)(2,1)S(1)} %pad_maximum_fusion.k0.v0), channel_id=1, source_target_pairs={{0,1},{2,3},{4,5},{6,7},{8,9},{10,11},{12,13},{14,15},{1,4},{3,6},... | collective-permute-start | bytes 4718600 | tf_op jit(solution)/shard_map/ppermute | solution.py:113
  8.8 0.6 compare_reduce_fusion.1
  9.4 0.6 compare_reduce_fusion
  10.7 0.7 slice.47
  12.0 1.8 %fusion.4 = bf16[1,1]{1,0:T(2,128)(2,1)} fusion(pred[1,1]{1,0:T(4,128)(4,1)} %bitcast.2, bf16[1,1]{1,0:T(2,128)(2,1)} %bitcast.3, s32[]{:T(128)} %bitcast.4, bf16[1,1]{1,0:T(2,128)(2,1)} %bitcast.1), kind=kLoop, calls=%fused_computation.23 | loop fusion | flops 1 | bytes 11 | tf_op jit(solution)/shard_map/select.3
  13.9 1.4 %scatter.9 = bf16[1,3072]{1,0:T(2,128)(2,1)S(1)} dynamic-update-slice(bf16[1,3072]{1,0:T(2,128)(2,1)S(1)} %scatter.6, bf16[1,1]{1,0:T(2,128)(2,1)} %fusion.4, s32[]{:T(128)} %constant.69.clone.1, s32[]{:T(128)} %bitcast.4) | dynamic-update-slice | bytes 8 | tf_op jit(solution)/shard_map/scatter | solution.py:101
  15.3 0.0 copy-done.2
  15.3 0.0 copy-done.3
  15.4 0.1 collective-permute-start
  15.5 0.7 constant_dynamic-update-slice_fusion.4
  16.8 40.6 %collective-permute-done = bf16[1,5,3072]{2,1,0:T(8,128)(2,1)S(1)} collective-permute-done((bf16[1,5,3072]{2,1,0:T(8,128)(2,1)S(1)}, bf16[1,5,3072]{2,1,0:T(8,128)(2,1)S(1)}, u32[]{:S(2)}, u32[]{:S(2)}) %collective-permute-start) | collective-permute-done | bytes 30752 | tf_op jit(solution)/shard_map/ppermute | solution.py:88
  57.4 0.8 collective-permute-start.1
  58.2 0.6 constant_dynamic-update-slice_fusion.3
  58.8 2.1 %collective-permute-done.1 = bf16[2,5,3072]{2,1,0:T(8,128)(2,1)S(1)} collective-permute-done((bf16[2,5,3072]{2,1,0:T(8,128)(2,1)S(1)}, bf16[2,5,3072]{2,1,0:T(8,128)(2,1)S(1)}, u32[]{:S(2)}, u32[]{:S(2)}) %collective-permute-start.1) | collective-permute-done | bytes 61472 | tf_op jit(solution)/shard_map/ppermute | solution.py:88
  61.0 0.1 collective-permute-start.2
  61.1 0.7 constant_dynamic-update-slice_fusion.2
  61.7 0.0 collective-permute-done.5.k2.v2
  61.7 0.0 copy-start.1
  61.7 0.0 collective-permute-start.6
  61.7 3.8 %collective-permute-done.2 = bf16[4,5,3072]{2,1,0:T(8,128)(2,1)S(1)} collective-permute-done((bf16[4,5,3072]{2,1,0:T(8,128)(2,1)S(1)}, bf16[4,5,3072]{2,1,0:T(8,128)(2,1)S(1)}, u32[]{:S(2)}, u32[]{:S(2)}) %collective-permute-start.2) | collective-permute-done | bytes 122912 | tf_op jit(solution)/shard_map/ppermute | solution.py:88
  65.6 0.1 pad_maximum_fusion.1
  65.7 0.1 collective-permute-start.3
  65.7 0.7 constant_dynamic-update-slice_fusion.1
  66.4 1.0 %collective-permute-done.3 = bf16[8,5,3072]{2,1,0:T(8,128)(2,1)S(1)} collective-permute-done((bf16[8,5,3072]{2,1,0:T(8,128)(2,1)S(1)}, bf16[8,5,3072]{2,1,0:T(8,128)(2,1)S(1)}, u32[]{:S(2)}, u32[]{:S(2)}) %collective-permute-start.3) | collective-permute-done | bytes 245792 | tf_op jit(solution)/shard_map/ppermute | solution.py:88
  67.4 0.8 constant_dynamic-update-slice_fusion
  68.2 1.7 %fusion.3 = (bf16[16,2,3072]{2,1,0:T(2,128)(2,1)S(1)}, bf16[16,2,3072]{2,1,0:T(2,128)(2,1)S(1)}) fusion(bf16[16,5,3072]{2,1,0:T(8,128)(2,1)} %constant_dynamic-update-slice_fusion), kind=kLoop, calls=%fused_computation.22 | loop fusion | bytes 786432 | tf_op jit(solution)/shard_map/slice | solution.py:105
  70.0 0.0 copy-done
  70.0 0.7 reshape.90.cv
  70.7 0.0 copy-done.1
  70.7 0.7 reshape.89.ck
  71.5 1.7 %fusion.2 = (s32[]{:T(128)}, s32[]{:T(128)}, s32[]{:T(128)}) fusion(s32[]{:T(128)S(6)} %sub.11, bf16[16,5,3072]{2,1,0:T(8,128)(2,1)} %constant_dynamic-update-slice_fusion, s32[]{:T(128)S(6)} %sub.10, s32[]{:T(128)S(6)} %sub.9), kind=kLoop, calls=%fused_computation.17 | loop fusion | flops 173 | bytes 88 | tf_op jit(solution)/shard_map/reduce_sum | solution.py:123
  73.2 2.6 %stack.24.table_ref = s32[5]{0:T(128)} concatenate(s32[1]{0:T(128)S(6)} %copy.14, s32[1]{0:T(128)} %bitcast.6, s32[1]{0:T(128)} %bitcast.7, s32[1]{0:T(128)} %bitcast.8, s32[1]{0:T(128)S(6)} %copy.15), dimensions={0} | concatenate | bytes 40 | tf_op jit(solution)/shard_map/stack | solution.py:125
  75.8 0.0 collective-permute-done.4.k1.v1
  75.8 0.0 collective-permute-done.6.k3.v3
  75.8 12.0 %shard_map.82 = bf16[128,3072]{1,0:T(8,128)(2,1)} custom-call(s32[5]{0:T(128)} %stack.24.table_ref, bf16[128,3072]{1,0:T(8,128)(2,1)} %q_ref.1, bf16[2,128,3072]{2,1,0:T(8,128)(2,1)} %copy-done, bf16[2,128,3072]{2,1,0:T(8,128)(2,1)} %copy-done, bf16[2,128,3072]{2,1,0:T(8,128)(2,1)} %collective-permute-done.4.k1.v1, ...), custom_call_target="tpu_custom_call" | custom-call | flops 855638016 | bytes 8454144 | tf_op jit(solution)/shard_map/pallas_call | solution.py:73
  (5 shorter events, 0.1 us)
Async XLA Ops:
  0.0 15.3 %copy-start.2 = (bf16[2,3072]{1,0:T(2,128)(2,1)S(1)}, bf16[2,3072]{1,0:T(2,128)(2,1)}, u32[]{:S(2)}) copy-start(bf16[2,3072]{1,0:T(2,128)(2,1)} %param.16) | copy-start | bytes 36868
  0.0 15.3 %copy-start.3 = (bf16[2,3072]{1,0:T(2,128)(2,1)S(1)}, bf16[2,3072]{1,0:T(2,128)(2,1)}, u32[]{:S(2)}) copy-start(bf16[2,3072]{1,0:T(2,128)(2,1)} %param.15) | copy-start | bytes 36868
  1.5 68.4 %copy-start = (bf16[2,128,3072]{2,1,0:T(8,128)(2,1)}, bf16[2,128,3072]{2,1,0:T(8,128)(2,1)S(1)}, u32[]{:S(2)}) copy-start(bf16[2,128,3072]{2,1,0:T(8,128)(2,1)S(1)} %pad_maximum_fusion.k0.v0) | copy-start | bytes 4718596
  1.6 60.1 %collective-permute-start.5 = (bf16[2,128,3072]{2,1,0:T(8,128)(2,1)S(1)}, bf16[2,128,3072]{2,1,0:T(8,128)(2,1)S(1)}, u32[]{:S(2)}, u32[]{:S(2)}) collective-permute-start(bf16[2,128,3072]{2,1,0:T(8,128)(2,1)S(1)} %pad_maximum_fusion.k0.v0), channel_id=1, source_target_pairs={{0,2},{1,3},{2,4},{3,5},{4,6},{5,7},{6,8},{7,9},{8,10},{9,11},{10,... | collective-permute-start | bytes 4718600 | tf_op jit(solution)/shard_map/ppermute | solution.py:112
  4.7 71.0 %collective-permute-start.4 = (bf16[2,128,3072]{2,1,0:T(8,128)(2,1)S(1)}, bf16[2,128,3072]{2,1,0:T(8,128)(2,1)}, u32[]{:S(2)}, u32[]{:S(2)}) collective-permute-start(bf16[2,128,3072]{2,1,0:T(8,128)(2,1)S(1)} %pad_maximum_fusion.k0.v0), channel_id=1, source_target_pairs={{0,1},{2,3},{4,5},{6,7},{8,9},{10,11},{12,13},{14,15},{1,4},{3,6},... | collective-permute-start | bytes 4718600 | tf_op jit(solution)/shard_map/ppermute | solution.py:113
  15.4 42.0 %collective-permute-start = (bf16[1,5,3072]{2,1,0:T(8,128)(2,1)S(1)}, bf16[1,5,3072]{2,1,0:T(8,128)(2,1)S(1)}, u32[]{:S(2)}, u32[]{:S(2)}) collective-permute-start(bf16[1,5,3072]{2,1,0:T(8,128)(2,1)S(1)} %maximum_bitcast_fusion), channel_id=1, source_target_pairs={{0,8},{1,9},{2,10},{3,11},{4,12},{5,13},{6,14},{7,15},{8,0},{9,1},... | collective-permute-start | bytes 92168 | tf_op jit(solution)/shard_map/ppermute | solution.py:88
  57.4 3.5 %collective-permute-start.1 = (bf16[2,5,3072]{2,1,0:T(8,128)(2,1)S(1)}, bf16[2,5,3072]{2,1,0:T(8,128)(2,1)S(1)}, u32[]{:S(2)}, u32[]{:S(2)}) collective-permute-start(bf16[2,5,3072]{2,1,0:T(8,128)(2,1)S(1)} %pad_maximum_fusion.3), channel_id=1, source_target_pairs={{0,4},{1,5},{2,6},{3,7},{4,0},{5,1},{6,2},{7,3},{8,12},{9,13},{10,... | collective-permute-start | bytes 184328 | tf_op jit(solution)/shard_map/ppermute | solution.py:88
  61.0 4.6 %collective-permute-start.2 = (bf16[4,5,3072]{2,1,0:T(8,128)(2,1)S(1)}, bf16[4,5,3072]{2,1,0:T(8,128)(2,1)S(1)}, u32[]{:S(2)}, u32[]{:S(2)}) collective-permute-start(bf16[4,5,3072]{2,1,0:T(8,128)(2,1)S(1)} %pad_maximum_fusion.2), channel_id=1, source_target_pairs={{0,2},{1,3},{2,0},{3,1},{4,6},{5,7},{6,4},{7,5},{8,10},{9,11},{10,... | collective-permute-start | bytes 368648 | tf_op jit(solution)/shard_map/ppermute | solution.py:88
  61.7 9.0 %copy-start.1 = (bf16[2,128,3072]{2,1,0:T(8,128)(2,1)}, bf16[2,128,3072]{2,1,0:T(8,128)(2,1)S(1)}, u32[]{:S(2)}) copy-start(bf16[2,128,3072]{2,1,0:T(8,128)(2,1)S(1)} %collective-permute-done.5.k2.v2) | copy-start | bytes 4718596
  61.7 14.1 %collective-permute-start.6 = (bf16[2,128,3072]{2,1,0:T(8,128)(2,1)S(1)}, bf16[2,128,3072]{2,1,0:T(8,128)(2,1)}, u32[]{:S(2)}, u32[]{:S(2)}) collective-permute-start(bf16[2,128,3072]{2,1,0:T(8,128)(2,1)S(1)} %collective-permute-done.5.k2.v2), channel_id=1, source_target_pairs={{0,1},{1,0},{2,3},{3,2},{4,5},{5,4},{6,7},{7,6},{8,9},{9,8},{10,11... | collective-permute-start | bytes 4718600 | tf_op jit(solution)/shard_map/ppermute | solution.py:115
  65.7 1.8 %collective-permute-start.3 = (bf16[8,5,3072]{2,1,0:T(8,128)(2,1)S(1)}, bf16[8,5,3072]{2,1,0:T(8,128)(2,1)S(1)}, u32[]{:S(2)}, u32[]{:S(2)}) collective-permute-start(bf16[8,5,3072]{2,1,0:T(8,128)(2,1)S(1)} %pad_maximum_fusion.1), channel_id=1, source_target_pairs={{0,1},{1,0},{2,3},{3,2},{4,5},{5,4},{6,7},{7,6},{8,9},{9,8},{10,11... | collective-permute-start | bytes 737288 | tf_op jit(solution)/shard_map/ppermute | solution.py:88

commit v4 on v3

--- a/solution.py
+++ b/solution.py
@@ -28,7 +28,7 @@
         q = q_ref[:, cols]
         scores = []
         for j, (k_ref, _) in enumerate(blocks):
-            s = lax.dot_general(q, k_ref[:, cols], dims, preferred_element_type=jnp.float32) * scale
+            s = jnp.dot(q, k_ref[:, cols], preferred_element_type=jnp.float32) * scale
             scores.append(jnp.where(slot < table_ref[j], s, -jnp.inf))
         scores.append(lax.dot_general(q, ck[:, cols], dims, preferred_element_type=jnp.float32) * scale)
         row_max = scores[0].max(axis=1, keepdims=True)
@@ -106,7 +106,9 @@
     piece_lengths = gathered[:, 2 * cache_rows, 0].astype(jnp.int32)
     piece_index = gathered[:, 2 * cache_rows, 1].astype(jnp.int32)
 
-    kv = jnp.stack([fresh_keys, fresh_values], 0)
+    head_count = feat_width // HEAD_DIM
+    keys_by_head = fresh_keys.reshape(row_count, head_count, HEAD_DIM).transpose(2, 1, 0).reshape(HEAD_DIM, head_count * row_count)
+    kv = jnp.stack([keys_by_head, fresh_values], 0)
     pairs_two = [(i, i + 2) for i in range(size - 2)]
     pairs_mixed = [(i, i + 1) for i in range(0, size - 1, 2)] + [(i, i + 3) for i in range(1, size - 3, 2)]
     from_two = lax.ppermute(kv, "group", pairs_two)
@@ -115,14 +117,10 @@
     from_swap = lax.ppermute(from_two, "group", pairs_swap)
 
     odd = (me % 2) == 1
-    offset_mixed = jnp.where(odd, 1, 3)
-    offset_swap = jnp.where(odd, 3, 1)
-
-    def length_at(offset):
-        source = me - offset
-        return jnp.sum(jnp.where(piece_index == source, piece_lengths, 0))
-
-    table = jnp.stack([lengths[0], length_at(offset_mixed), length_at(2), length_at(offset_swap), levels[0]]).astype(jnp.int32)
+    offsets = jnp.where(odd, jnp.array([1, 2, 3], jnp.int32), jnp.array([3, 2, 1], jnp.int32))
+    sources = me - offsets
+    previous = jnp.sum(jnp.where(piece_index[None, :] == sources[:, None], piece_lengths[None, :], 0), axis=1)
+    table = jnp.concatenate([lengths[:1], previous, levels[:1]]).astype(jnp.int32)
     return attend(table, queries, kv, from_mixed, from_two, from_swap, all_cache_keys, all_cache_values, gate_table)
 
 

time: 89.4 us -> 86.1 us (0.963)
  the two profiles are of different devices: /device:TPU:15 before, /device:TPU:0 now
where the time goes in v4:
time: 86.1 us; the launch traced here: 85.5 us
  starting transfers between devices  46.3 us (54%)
  waiting for transfers between devices  10.8 us (13%)
  local copies, waits for them, and re-layouts  10.4 us (12%)
  Pallas kernels  9.35 us (11%)
  other arithmetic  6.6 us (8%)
  between operations  2.1 us (2%)
    ppermute x4, starting transfers between devices, gather_pieces(): other = lax.ppermute(held, 'group', [(i, i ^ step) for i in range(size)])  38.6 us
    ppermute x4, waiting for transfers between devices, gather_pieces(): other = lax.ppermute(held, 'group', [(i, i ^ step) for i in range(size)])  10.8 us
    pallas_call x1, Pallas kernels, attend(): pl.pallas_call(functools.partial(attention_kernel, heads=HEADS_PER_STEP),...  9.35 us
    ppermute x1, starting transfers between devices, body(): from_two = lax.ppermute(kv, 'group', pairs_two)  4.97 us
    unnamed x18, local copies, waits for them, and re-layouts  3.47 us
    another operation x3, other arithmetic  3.18 us
    ppermute x1, starting transfers between devices, body(): from_mixed = lax.ppermute(kv, 'group', pairs_mixed)  2.62 us
    slice x1, local copies, waits for them, and re-layouts, body(): gathered[:, cache_rows:2 * cache_rows].reshape(-1, feat_width)  1.74 us
  transfers between devices with their start and end apart: 7, of which 4 were waited for; matrix products, arithmetic and copies ran while one was open for 17% of the time, Pallas kernels for 0%

profile of v4, /device:TPU:0, one launch (start us, length us, event | category | flops | bytes accessed | tf_op | source)
XLA Modules:
  0.0 85.5 jit_solution(18026988257052972405)
XLA Ops:
  0.0 1.3 %copy.14 = bf16[16,8,24,128]{3,2,1,0:T(8,128)(2,1)S(1)} copy(bf16[16,8,24,128]{3,1,2,0:T(8,128)(2,1)} %bitcast.15) | data formatting | bytes 1572864
  1.3 0.0 copy-start.2
  1.3 0.7 copy.13
  2.0 0.3 stack_reshape.3
  2.3 0.1 copy-done.2
  2.4 0.0 copy-start.3
  2.4 0.0 copy-start.4
  2.4 0.0 copy-start.5
  2.4 0.0 copy-start.6
  2.4 0.1 pad_maximum_fusion.k0.v0
  2.6 0.0 copy-start
  2.6 5.0 %collective-permute-start.5 = (bf16[2,128,3072]{2,1,0:T(8,128)(2,1)S(1)}, bf16[2,128,3072]{2,1,0:T(8,128)(2,1)S(1)}, u32[]{:S(2)}, u32[]{:S(2)}) collective-permute-start(bf16[2,128,3072]{2,1,0:T(8,128)(2,1)S(1)} %pad_maximum_fusion.k0.v0), channel_id=1, source_target_pairs={{0,2},{1,3},{2,4},{3,5},{4,6},{5,7},{6,8},{7,9},{8,10},{9,11},{10,... | collective-permute-start | bytes 4718600 | tf_op jit(solution)/shard_map/ppermute | solution.py:114
  7.6 2.6 %collective-permute-start.4 = (bf16[2,128,3072]{2,1,0:T(8,128)(2,1)S(1)}, bf16[2,128,3072]{2,1,0:T(8,128)(2,1)}, u32[]{:S(2)}, u32[]{:S(2)}) collective-permute-start(bf16[2,128,3072]{2,1,0:T(8,128)(2,1)S(1)} %pad_maximum_fusion.k0.v0), channel_id=1, source_target_pairs={{0,1},{2,3},{4,5},{6,7},{8,9},{10,11},{12,13},{14,15},{1,4},{3,6},... | collective-permute-start | bytes 4718600 | tf_op jit(solution)/shard_map/ppermute | solution.py:115
  10.2 0.6 compare_reduce_fusion.1
  10.8 0.7 compare_reduce_fusion
  12.2 0.6 slice.47
  13.5 1.8 %fusion.4 = bf16[1,1]{1,0:T(2,128)(2,1)} fusion(pred[1,1]{1,0:T(4,128)(4,1)} %bitcast.2, bf16[1,1]{1,0:T(2,128)(2,1)} %bitcast.3, s32[]{:T(128)} %bitcast.4, bf16[1,1]{1,0:T(2,128)(2,1)} %bitcast.1), kind=kLoop, calls=%fused_computation.23 | loop fusion | flops 1 | bytes 11 | tf_op jit(solution)/shard_map/select.3
  15.3 1.3 %scatter.9 = bf16[1,3072]{1,0:T(2,128)(2,1)S(1)} dynamic-update-slice(bf16[1,3072]{1,0:T(2,128)(2,1)S(1)} %scatter.6, bf16[1,1]{1,0:T(2,128)(2,1)} %fusion.4, s32[]{:T(128)} %constant.71.clone.1, s32[]{:T(128)} %bitcast.4) | dynamic-update-slice | bytes 8 | tf_op jit(solution)/shard_map/scatter | solution.py:101
  16.6 0.0 copy-done.3
  16.6 0.0 copy-done.4
  16.6 1.9 %collective-permute-start = (bf16[1,5,3072]{2,1,0:T(8,128)(2,1)S(1)}, bf16[1,5,3072]{2,1,0:T(8,128)(2,1)S(1)}, u32[]{:S(2)}, u32[]{:S(2)}) collective-permute-start(bf16[1,5,3072]{2,1,0:T(8,128)(2,1)S(1)} %maximum_bitcast_fusion), channel_id=1, source_target_pairs={{0,8},{1,9},{2,10},{3,11},{4,12},{5,13},{6,14},{7,15},{8,0},{9,1},... | collective-permute-start | bytes 92168 | tf_op jit(solution)/shard_map/ppermute | solution.py:88
  18.5 0.7 constant_dynamic-update-slice_fusion.4
  19.2 0.0 copy-done.5
  19.2 0.0 copy-done.6
  19.8 3.4 %collective-permute-done = bf16[1,5,3072]{2,1,0:T(8,128)(2,1)S(1)} collective-permute-done((bf16[1,5,3072]{2,1,0:T(8,128)(2,1)S(1)}, bf16[1,5,3072]{2,1,0:T(8,128)(2,1)S(1)}, u32[]{:S(2)}, u32[]{:S(2)}) %collective-permute-start) | collective-permute-done | bytes 30752 | tf_op jit(solution)/shard_map/ppermute | solution.py:88
  23.2 0.1 collective-permute-start.1
  23.3 0.6 constant_dynamic-update-slice_fusion.3
  23.9 4.0 %collective-permute-done.1 = bf16[2,5,3072]{2,1,0:T(8,128)(2,1)S(1)} collective-permute-done((bf16[2,5,3072]{2,1,0:T(8,128)(2,1)S(1)}, bf16[2,5,3072]{2,1,0:T(8,128)(2,1)S(1)}, u32[]{:S(2)}, u32[]{:S(2)}) %collective-permute-start.1) | collective-permute-done | bytes 61472 | tf_op jit(solution)/shard_map/ppermute | solution.py:88
  28.0 22.2 %collective-permute-start.2 = (bf16[4,5,3072]{2,1,0:T(8,128)(2,1)S(1)}, bf16[4,5,3072]{2,1,0:T(8,128)(2,1)S(1)}, u32[]{:S(2)}, u32[]{:S(2)}) collective-permute-start(bf16[4,5,3072]{2,1,0:T(8,128)(2,1)S(1)} %pad_maximum_fusion.2), channel_id=1, source_target_pairs={{0,2},{1,3},{2,0},{3,1},{4,6},{5,7},{6,4},{7,5},{8,10},{9,11},{10,... | collective-permute-start | bytes 368648 | tf_op jit(solution)/shard_map/ppermute | solution.py:88
  50.2 0.6 constant_dynamic-update-slice_fusion.2
  50.8 3.0 %collective-permute-done.2 = bf16[4,5,3072]{2,1,0:T(8,128)(2,1)S(1)} collective-permute-done((bf16[4,5,3072]{2,1,0:T(8,128)(2,1)S(1)}, bf16[4,5,3072]{2,1,0:T(8,128)(2,1)S(1)}, u32[]{:S(2)}, u32[]{:S(2)}) %collective-permute-start.2) | collective-permute-done | bytes 122912 | tf_op jit(solution)/shard_map/ppermute | solution.py:88
  53.8 0.1 pad_maximum_fusion.1
  53.9 14.4 %collective-permute-start.3 = (bf16[8,5,3072]{2,1,0:T(8,128)(2,1)S(1)}, bf16[8,5,3072]{2,1,0:T(8,128)(2,1)S(1)}, u32[]{:S(2)}, u32[]{:S(2)}) collective-permute-start(bf16[8,5,3072]{2,1,0:T(8,128)(2,1)S(1)} %pad_maximum_fusion.1), channel_id=1, source_target_pairs={{0,1},{1,0},{2,3},{3,2},{4,5},{5,4},{6,7},{7,6},{8,9},{9,8},{10,11... | collective-permute-start | bytes 737288 | tf_op jit(solution)/shard_map/ppermute | solution.py:88
  68.3 0.0 collective-permute-done.5.k2.v2
  68.4 0.0 copy-start.1
  68.4 0.1 collective-permute-start.6
  68.4 0.8 constant_dynamic-update-slice_fusion.1
  69.2 0.5 collective-permute-done.3
  69.7 0.8 constant_dynamic-update-slice_fusion
  70.5 1.7 %fusion.3 = (bf16[16,2,3072]{2,1,0:T(2,128)(2,1)S(1)}, bf16[16,2,3072]{2,1,0:T(2,128)(2,1)S(1)}) fusion(bf16[16,5,3072]{2,1,0:T(8,128)(2,1)} %constant_dynamic-update-slice_fusion), kind=kLoop, calls=%fused_computation.22 | loop fusion | bytes 786432 | tf_op jit(solution)/shard_map/slice | solution.py:105
  72.2 0.0 copy-done
  72.2 0.7 reshape.95.cv
  73.0 0.8 reshape.94.ck
  73.7 1.6 %fusion.1 = (s32[16]{0:T(128)S(1)}, s32[16]{0:T(128)S(1)}) fusion(bf16[16,5,3072]{2,1,0:T(8,128)(2,1)} %constant_dynamic-update-slice_fusion), kind=kLoop, calls=%fused_computation.13 | loop fusion | flops 32 | bytes 192 | tf_op jit(solution)/shard_map/convert_element_type | solution.py:107
  75.3 0.2 select_reduce_fusion
  75.5 0.6 pad_add_fusion.table_ref
  76.1 0.0 collective-permute-done.4.k1.v1
  76.1 0.0 collective-permute-done.6.k3.v3
  76.1 0.0 copy-done.1
  76.1 9.3 %shard_map.100 = bf16[128,3072]{1,0:T(8,128)(2,1)} custom-call(s32[5]{0:T(128)} %pad_add_fusion.table_ref, bf16[128,3072]{1,0:T(8,128)(2,1)} %q_ref.1, bf16[2,128,3072]{2,1,0:T(8,128)(2,1)} %copy-done, bf16[2,128,3072]{2,1,0:T(8,128)(2,1)} %copy-done, bf16[2,128,3072]{2,1,0:T(8,128)(2,1)} %collective-permute-done.4.k1.v1, ...), custom_call_target="tpu_custom_call" | custom-call | flops 855638016 | bytes 8454144 | tf_op jit(solution)/shard_map/pallas_call | solution.py:73
  (6 shorter events, 0.1 us)
Async XLA Ops:
  1.3 1.1 %copy-start.2 = (bf16[128,3072]{1,0:T(8,128)(2,1)S(1)}, bf16[128,3072]{1,0:T(8,128)(2,1)}, u32[]{:S(2)}) copy-start(bf16[128,3072]{1,0:T(8,128)(2,1)} %param.16) | copy-start | bytes 2359300
  2.4 14.2 %copy-start.3 = (bf16[2,3072]{1,0:T(2,128)(2,1)S(1)}, bf16[2,3072]{1,0:T(2,128)(2,1)}, u32[]{:S(2)}) copy-start(bf16[2,3072]{1,0:T(2,128)(2,1)} %param.18) | copy-start | bytes 36868
  2.4 14.2 %copy-start.4 = (bf16[2,3072]{1,0:T(2,128)(2,1)S(1)}, bf16[2,3072]{1,0:T(2,128)(2,1)}, u32[]{:S(2)}) copy-start(bf16[2,3072]{1,0:T(2,128)(2,1)} %param.17) | copy-start | bytes 36868
  2.4 16.8 %copy-start.5 = (s32[3]{0:T(128)S(1)}, s32[3]{0:T(128)}, u32[]{:S(2)}) copy-start(s32[3]{0:T(128)} %constant.78.clone) | copy-start | bytes 40
  2.4 16.8 %copy-start.6 = (s32[3]{0:T(128)S(1)}, s32[3]{0:T(128)}, u32[]{:S(2)}) copy-start(s32[3]{0:T(128)} %constant.77.clone) | copy-start | bytes 40
  2.6 69.6 %copy-start = (bf16[2,128,3072]{2,1,0:T(8,128)(2,1)}, bf16[2,128,3072]{2,1,0:T(8,128)(2,1)S(1)}, u32[]{:S(2)}) copy-start(bf16[2,128,3072]{2,1,0:T(8,128)(2,1)S(1)} %pad_maximum_fusion.k0.v0) | copy-start | bytes 4718596
  2.6 65.8 %collective-permute-start.5 = (bf16[2,128,3072]{2,1,0:T(8,128)(2,1)S(1)}, bf16[2,128,3072]{2,1,0:T(8,128)(2,1)S(1)}, u32[]{:S(2)}, u32[]{:S(2)}) collective-permute-start(bf16[2,128,3072]{2,1,0:T(8,128)(2,1)S(1)} %pad_maximum_fusion.k0.v0), channel_id=1, source_target_pairs={{0,2},{1,3},{2,4},{3,5},{4,6},{5,7},{6,8},{7,9},{8,10},{9,11},{10,... | collective-permute-start | bytes 4718600 | tf_op jit(solution)/shard_map/ppermute | solution.py:114
  7.6 68.6 %collective-permute-start.4 = (bf16[2,128,3072]{2,1,0:T(8,128)(2,1)S(1)}, bf16[2,128,3072]{2,1,0:T(8,128)(2,1)}, u32[]{:S(2)}, u32[]{:S(2)}) collective-permute-start(bf16[2,128,3072]{2,1,0:T(8,128)(2,1)S(1)} %pad_maximum_fusion.k0.v0), channel_id=1, source_target_pairs={{0,1},{2,3},{4,5},{6,7},{8,9},{10,11},{12,13},{14,15},{1,4},{3,6},... | collective-permute-start | bytes 4718600 | tf_op jit(solution)/shard_map/ppermute | solution.py:115
  16.6 6.6 %collective-permute-start = (bf16[1,5,3072]{2,1,0:T(8,128)(2,1)S(1)}, bf16[1,5,3072]{2,1,0:T(8,128)(2,1)S(1)}, u32[]{:S(2)}, u32[]{:S(2)}) collective-permute-start(bf16[1,5,3072]{2,1,0:T(8,128)(2,1)S(1)} %maximum_bitcast_fusion), channel_id=1, source_target_pairs={{0,8},{1,9},{2,10},{3,11},{4,12},{5,13},{6,14},{7,15},{8,0},{9,1},... | collective-permute-start | bytes 92168 | tf_op jit(solution)/shard_map/ppermute | solution.py:88
  23.2 4.7 %collective-permute-start.1 = (bf16[2,5,3072]{2,1,0:T(8,128)(2,1)S(1)}, bf16[2,5,3072]{2,1,0:T(8,128)(2,1)S(1)}, u32[]{:S(2)}, u32[]{:S(2)}) collective-permute-start(bf16[2,5,3072]{2,1,0:T(8,128)(2,1)S(1)} %pad_maximum_fusion.3), channel_id=1, source_target_pairs={{0,4},{1,5},{2,6},{3,7},{4,0},{5,1},{6,2},{7,3},{8,12},{9,13},{10,... | collective-permute-start | bytes 184328 | tf_op jit(solution)/shard_map/ppermute | solution.py:88
  28.0 25.9 %collective-permute-start.2 = (bf16[4,5,3072]{2,1,0:T(8,128)(2,1)S(1)}, bf16[4,5,3072]{2,1,0:T(8,128)(2,1)S(1)}, u32[]{:S(2)}, u32[]{:S(2)}) collective-permute-start(bf16[4,5,3072]{2,1,0:T(8,128)(2,1)S(1)} %pad_maximum_fusion.2), channel_id=1, source_target_pairs={{0,2},{1,3},{2,0},{3,1},{4,6},{5,7},{6,4},{7,5},{8,10},{9,11},{10,... | collective-permute-start | bytes 368648 | tf_op jit(solution)/shard_map/ppermute | solution.py:88
  53.9 15.8 %collective-permute-start.3 = (bf16[8,5,3072]{2,1,0:T(8,128)(2,1)S(1)}, bf16[8,5,3072]{2,1,0:T(8,128)(2,1)S(1)}, u32[]{:S(2)}, u32[]{:S(2)}) collective-permute-start(bf16[8,5,3072]{2,1,0:T(8,128)(2,1)S(1)} %pad_maximum_fusion.1), channel_id=1, source_target_pairs={{0,1},{1,0},{2,3},{3,2},{4,5},{5,4},{6,7},{7,6},{8,9},{9,8},{10,11... | collective-permute-start | bytes 737288 | tf_op jit(solution)/shard_map/ppermute | solution.py:88
  68.4 7.8 %copy-start.1 = (bf16[2,128,3072]{2,1,0:T(8,128)(2,1)}, bf16[2,128,3072]{2,1,0:T(8,128)(2,1)S(1)}, u32[]{:S(2)}) copy-start(bf16[2,128,3072]{2,1,0:T(8,128)(2,1)S(1)} %collective-permute-done.5.k2.v2) | copy-start | bytes 4718596
  68.4 7.8 %collective-permute-start.6 = (bf16[2,128,3072]{2,1,0:T(8,128)(2,1)S(1)}, bf16[2,128,3072]{2,1,0:T(8,128)(2,1)}, u32[]{:S(2)}, u32[]{:S(2)}) collective-permute-start(bf16[2,128,3072]{2,1,0:T(8,128)(2,1)S(1)} %collective-permute-done.5.k2.v2), channel_id=1, source_target_pairs={{0,1},{1,0},{2,3},{3,2},{4,5},{5,4},{6,7},{7,6},{8,9},{9,8},{10,11... | collective-permute-start | bytes 4718600 | tf_op jit(solution)/shard_map/ppermute | solution.py:117

commit v5 on v4

--- a/solution.py
+++ b/solution.py
@@ -46,22 +46,23 @@
         o_ref[:, cols] = out.astype(o_ref.dtype)
 
 
-def attend(table, queries, kv_own, kv_a, kv_b, kv_c, cache_keys, cache_values, gate_table):
+def attend(table, queries, kv_own, kv_a, kv_b, kv_c, cache, gate_table):
     rows, feat = queries.shape
     width = HEADS_PER_STEP * HEAD_DIM
     steps = feat // width
-    cache_rows = cache_keys.shape[0]
+    cache_rows = cache.shape[0]
     levels = gate_table.shape[0]
     row_block = pl.BlockSpec((rows, width), lambda h, t: (0, h))
     k_block = pl.BlockSpec((None, rows, width), lambda h, t: (0, 0, h))
     v_block = pl.BlockSpec((None, rows, width), lambda h, t: (1, 0, h))
-    cache_block = pl.BlockSpec((cache_rows, width), lambda h, t: (0, h))
+    cache_k_block = pl.BlockSpec((cache_rows, width), lambda h, t: (0, h))
+    cache_v_block = pl.BlockSpec((cache_rows, width), lambda h, t: (0, steps + h))
     gate_block = pl.BlockSpec((levels, width), lambda h, t: (0, h))
     grid_spec = pltpu.PrefetchScalarGridSpec(
         num_scalar_prefetch=1,
         grid=(steps,),
         in_specs=[row_block, k_block, v_block, k_block, v_block, k_block, v_block, k_block, v_block,
-                  cache_block, cache_block, gate_block],
+                  cache_k_block, cache_v_block, gate_block],
         out_specs=row_block,
     )
     keys = 4 * rows + cache_rows
@@ -75,14 +76,13 @@
         out_shape=jax.ShapeDtypeStruct((rows, feat), jnp.bfloat16),
         grid_spec=grid_spec,
         cost_estimate=cost,
-    )(table, queries, kv_own, kv_own, kv_a, kv_a, kv_b, kv_b, kv_c, kv_c, cache_keys, cache_values, gate_table)
+    )(table, queries, kv_own, kv_own, kv_a, kv_a, kv_b, kv_b, kv_c, kv_c, cache, cache, gate_table)
 
 
 def gather_pieces(piece, size):
     if size & (size - 1):
-        return lax.all_gather(piece, "group", axis=0, tiled=False)
-    me = lax.axis_index("group")
-    held = piece[None]
+        return lax.all_gather(piece, "group", axis=0, tiled=True)
+    held = piece
     step = size // 2
     while step >= 1:
         other = lax.ppermute(held, "group", [(i, i ^ step) for i in range(size)])
@@ -97,14 +97,12 @@
     me = lax.axis_index("group")
 
     cache_rows = cache_keys.shape[0]
-    tag_row = jnp.zeros((1, feat_width), jnp.bfloat16)
-    tag_row = tag_row.at[0, 0].set(lengths[0].astype(jnp.bfloat16)).at[0, 1].set(me.astype(jnp.bfloat16))
-    packed = jnp.concatenate([cache_keys, cache_values, tag_row], 0)
+    tag = jnp.zeros((cache_rows, HEAD_DIM), jnp.bfloat16)
+    tag = tag.at[0, 0].set(lengths[0].astype(jnp.bfloat16)).at[0, 1].set(me.astype(jnp.bfloat16))
+    packed = jnp.concatenate([cache_keys, cache_values, tag], 1)
     gathered = gather_pieces(packed, size)
-    all_cache_keys = gathered[:, :cache_rows].reshape(-1, feat_width)
-    all_cache_values = gathered[:, cache_rows:2 * cache_rows].reshape(-1, feat_width)
-    piece_lengths = gathered[:, 2 * cache_rows, 0].astype(jnp.int32)
-    piece_index = gathered[:, 2 * cache_rows, 1].astype(jnp.int32)
+    piece_lengths = gathered[:, 2 * feat_width].astype(jnp.int32)
+    piece_index = gathered[:, 2 * feat_width + 1].astype(jnp.int32)
 
     head_count = feat_width // HEAD_DIM
     keys_by_head = fresh_keys.reshape(row_count, head_count, HEAD_DIM).transpose(2, 1, 0).reshape(HEAD_DIM, head_count * row_count)
@@ -121,7 +119,7 @@
     sources = me - offsets
     previous = jnp.sum(jnp.where(piece_index[None, :] == sources[:, None], piece_lengths[None, :], 0), axis=1)
     table = jnp.concatenate([lengths[:1], previous, levels[:1]]).astype(jnp.int32)
-    return attend(table, queries, kv, from_mixed, from_two, from_swap, all_cache_keys, all_cache_values, gate_table)
+    return attend(table, queries, kv, from_mixed, from_two, from_swap, gathered, gate_table)
 
 
 def solution(mesh):

time: 86.1 us -> 76 us (0.88)
  the two profiles are of different devices: /device:TPU:0 before, /device:TPU:15 now
where the time goes in v5:
time: 76 us; the launch traced here: 74.6 us
  waiting for transfers between devices  39.3 us (52%)
  starting transfers between devices  12.7 us (17%)
  Pallas kernels  9.33 us (12%)
  local copies, waits for them, and re-layouts  7.2 us (9%)
  other arithmetic  4.61 us (6%)
  between operations  1.5 us (2%)
    ppermute x4, waiting for transfers between devices, gather_pieces(): other = lax.ppermute(held, 'group', [(i, i ^ step) for i in range(size)])  34.6 us
    pallas_call x1, Pallas kernels, attend(): pl.pallas_call(functools.partial(attention_kernel, heads=HEADS_PER_STEP),...  9.33 us
    ppermute x1, starting transfers between devices, body(): from_mixed = lax.ppermute(kv, 'group', pairs_mixed)  7.45 us
    ppermute x1, waiting for transfers between devices, body(): from_mixed = lax.ppermute(kv, 'group', pairs_mixed)  4.68 us
    ppermute x1, starting transfers between devices, body(): from_two = lax.ppermute(kv, 'group', pairs_two)  3.18 us
    concatenate x3, other arithmetic, gather_pieces(): held = jnp.concatenate([held, other], 0)  2.81 us
    concatenate x1, local copies, waits for them, and re-layouts, gather_pieces(): held = jnp.concatenate([held, other], 0)  2.79 us
    ppermute x4, starting transfers between devices, gather_pieces(): other = lax.ppermute(held, 'group', [(i, i ^ step) for i in range(size)])  1.95 us
  transfers between devices with their start and end apart: 7, of which 4 were waited for; matrix products, arithmetic and copies ran while one was open for 12% of the time, Pallas kernels for 0%

profile of v5, /device:TPU:15, one launch (start us, length us, event | category | flops | bytes accessed | tf_op | source)
XLA Modules:
  0.0 74.6 jit_solution(15459221475682637291)
XLA Ops:
  0.0 1.3 %copy.14 = bf16[16,8,24,128]{3,2,1,0:T(8,128)(2,1)S(1)} copy(bf16[16,8,24,128]{3,1,2,0:T(8,128)(2,1)} %bitcast.10) | data formatting | bytes 1572864
  1.3 0.0 copy-start.3
  1.3 0.7 copy.13
  2.0 0.3 stack_reshape.3
  2.3 0.1 copy-done.3
  2.4 0.0 copy-start.4
  2.4 0.0 copy-start.5
  2.4 0.0 copy-start.6
  2.4 0.0 copy-start.7
  2.4 0.1 pad_maximum_fusion.k0.v0
  2.6 0.0 copy-start
  2.6 3.2 %collective-permute-start.5 = (bf16[2,128,3072]{2,1,0:T(8,128)(2,1)S(1)}, bf16[2,128,3072]{2,1,0:T(8,128)(2,1)S(1)}, u32[]{:S(2)}, u32[]{:S(2)}) collective-permute-start(bf16[2,128,3072]{2,1,0:T(8,128)(2,1)S(1)} %pad_maximum_fusion.k0.v0), channel_id=1, source_target_pairs={{0,2},{1,3},{2,4},{3,5},{4,6},{5,7},{6,8},{7,9},{8,10},{9,11},{10,... | collective-permute-start | bytes 4718600 | tf_op jit(solution)/shard_map/ppermute | solution.py:112
  6.5 0.6 fusion.1
  7.1 1.3 %scatter.9 = bf16[2,128]{1,0:T(2,128)(2,1)S(1)} dynamic-update-slice(bf16[2,128]{1,0:T(2,128)(2,1)S(1)} %scatter.6, bf16[1,1]{1,0:T(2,128)(2,1)} %bitcast.1, s32[]{:T(128)} %bitcast.2, s32[]{:T(128)} %bitcast.3) | dynamic-update-slice | bytes 8 | tf_op jit(solution)/shard_map/scatter | solution.py:101
  8.5 0.0 copy-done.4
  8.5 0.0 copy-done.5
  8.5 0.6 pad_maximum_fusion.4
  9.1 0.4 collective-permute-start
  9.5 30.0 %collective-permute-done = bf16[2,6272]{1,0:T(2,128)(2,1)} collective-permute-done((bf16[2,6272]{1,0:T(2,128)(2,1)}, bf16[2,6272]{1,0:T(2,128)(2,1)}, u32[]{:S(2)}, u32[]{:S(2)}) %collective-permute-start) | collective-permute-done | bytes 25120 | tf_op jit(solution)/shard_map/ppermute | solution.py:88
  39.5 0.8 %pad_maximum_fusion.3 = bf16[4,6272]{1,0:T(4,128)(2,1)S(1)} fusion(bf16[2,6272]{1,0:T(2,128)(2,1)} %collective-permute-done, bf16[2,128]{1,0:T(2,128)(2,1)S(1)} %scatter.9, bf16[2,3072]{1,0:T(2,128)(2,1)S(1)} %copy-done.4, bf16[2,3072]{1,0:T(2,128)(2,1)S(1)} %copy-done.5), kind=kLoop, calls=%fused_computation.3 | loop fusion | flops 200704 | bytes 100352 | tf_op jit(solution)/shard_map/concatenate | solution.py:89
  40.3 0.1 collective-permute-start.1
  40.4 7.4 %collective-permute-start.4 = (bf16[2,128,3072]{2,1,0:T(8,128)(2,1)S(1)}, bf16[2,128,3072]{2,1,0:T(8,128)(2,1)}, u32[]{:S(2)}, u32[]{:S(2)}) collective-permute-start(bf16[2,128,3072]{2,1,0:T(8,128)(2,1)S(1)} %pad_maximum_fusion.k0.v0), channel_id=1, source_target_pairs={{0,1},{2,3},{4,5},{6,7},{8,9},{10,11},{12,13},{14,15},{1,4},{3,6},... | collective-permute-start | bytes 4718600 | tf_op jit(solution)/shard_map/ppermute | solution.py:113
  47.9 0.0 collective-permute-done.5.k2.v2
  47.9 0.0 copy-start.1
  47.9 0.1 collective-permute-start.6
  48.0 0.0 collective-permute-done.1
  48.0 1.0 %pad_maximum_fusion.2 = bf16[8,6272]{1,0:T(8,128)(2,1)S(1)} fusion(bf16[4,6272]{1,0:T(4,128)(2,1)} %collective-permute-done.1, bf16[2,6272]{1,0:T(2,128)(2,1)} %collective-permute-done, bf16[2,128]{1,0:T(2,128)(2,1)S(1)} %scatter.9, bf16[2,3072]{1,0:T(2,128)(2,1)S(1)} %copy-done.4, bf16[2,3072]{1,0:T(2,128)(2,1)S(1)} %copy-done.5), kind=kLoop, calls=%fused_computation.2 | loop fusion | flops 501760 | bytes 200704 | tf_op jit(solution)/shard_map/concatenate | solution.py:89
  48.9 0.1 collective-permute-start.2
  49.7 3.4 %collective-permute-done.2 = bf16[8,6272]{1,0:T(8,128)(2,1)} collective-permute-done((bf16[8,6272]{1,0:T(8,128)(2,1)S(1)}, bf16[8,6272]{1,0:T(8,128)(2,1)}, u32[]{:S(2)}, u32[]{:S(2)}) %collective-permute-start.2) | collective-permute-done | bytes 100384 | tf_op jit(solution)/shard_map/ppermute | solution.py:88
  53.1 1.1 %pad_maximum_fusion.1 = bf16[16,6272]{1,0:T(8,128)(2,1)S(1)} fusion(bf16[8,6272]{1,0:T(8,128)(2,1)} %collective-permute-done.2, bf16[4,6272]{1,0:T(4,128)(2,1)} %collective-permute-done.1, bf16[2,6272]{1,0:T(2,128)(2,1)} %collective-permute-done, bf16[2,128]{1,0:T(2,128)(2,1)S(1)} %scatter.9, bf16[2,3072]{1,0:T(2,128)(2,1)S(1)} %copy-done.4, ...), kind=kLoop, calls=%fused_computation.1 | loop fusion | flops 1204224 | bytes 401408 | tf_op jit(solution)/shard_map/concatenate | solution.py:89
  54.1 1.3 %collective-permute-start.3 = (bf16[16,6272]{1,0:T(8,128)(2,1)S(1)}, bf16[16,6272]{1,0:T(8,128)(2,1)}, u32[]{:S(2)}, u32[]{:S(2)}) collective-permute-start(bf16[16,6272]{1,0:T(8,128)(2,1)S(1)} %pad_maximum_fusion.1), channel_id=1, source_target_pairs={{0,1},{1,0},{2,3},{3,2},{4,5},{5,4},{6,7},{7,6},{8,9},{9,8},{10,11... | collective-permute-start | bytes 602120 | tf_op jit(solution)/shard_map/ppermute | solution.py:88
  55.5 0.0 copy-done.6
  55.5 0.0 copy-done.7
  55.5 1.2 %collective-permute-done.3 = bf16[16,6272]{1,0:T(8,128)(2,1)} collective-permute-done((bf16[16,6272]{1,0:T(8,128)(2,1)S(1)}, bf16[16,6272]{1,0:T(8,128)(2,1)}, u32[]{:S(2)}, u32[]{:S(2)}) %collective-permute-start.3) | collective-permute-done | bytes 200736 | tf_op jit(solution)/shard_map/ppermute | solution.py:88
  56.7 2.8 %concatenate.29.ck.cv = bf16[32,6272]{1,0:T(8,128)(2,1)S(1)} concatenate(bf16[2,6272]{1,0:T(2,128)(2,1)} %pad_maximum_fusion.4, bf16[2,6272]{1,0:T(2,128)(2,1)} %collective-permute-done, bf16[4,6272]{1,0:T(4,128)(2,1)} %collective-permute-done.1, bf16[8,6272]{1,0:T(8,128)(2,1)} %collective-permute-done.2, bf16[16,6272]{1,0:T(8,128)(2,1)} %collective-permute-done.3), dimensions={0} | concatenate | bytes 802816 | tf_op jit(solution)/shard_map/concatenate | solution.py:89
  59.5 0.0 copy-start.2
  59.5 0.2 convert_reduce_fusion.1
  59.7 0.2 select_reduce_fusion
  59.9 0.7 pad_add_fusion.table_ref
  60.5 4.7 %collective-permute-done.4.k1.v1 = bf16[2,128,3072]{2,1,0:T(8,128)(2,1)} collective-permute-done((bf16[2,128,3072]{2,1,0:T(8,128)(2,1)S(1)}, bf16[2,128,3072]{2,1,0:T(8,128)(2,1)}, u32[]{:S(2)}, u32[]{:S(2)}) %collective-permute-start.4) | collective-permute-done | bytes 1572896 | tf_op jit(solution)/shard_map/ppermute | solution.py:113
  65.2 0.0 collective-permute-done.6.k3.v3
  65.2 0.0 copy-done
  65.2 0.0 copy-done.1
  65.2 0.0 copy-done.2
  65.2 9.3 %shard_map.100 = bf16[128,3072]{1,0:T(8,128)(2,1)} custom-call(s32[5]{0:T(128)} %pad_add_fusion.table_ref, bf16[128,3072]{1,0:T(8,128)(2,1)} %q_ref.1, bf16[2,128,3072]{2,1,0:T(8,128)(2,1)} %copy-done, bf16[2,128,3072]{2,1,0:T(8,128)(2,1)} %copy-done, bf16[2,128,3072]{2,1,0:T(8,128)(2,1)} %collective-permute-done.4.k1.v1, ...), custom_call_target="tpu_custom_call" | custom-call | flops 855638016 | bytes 8454144 | tf_op jit(solution)/shard_map/pallas_call | solution.py:74
  (3 shorter events, 0.0 us)
Async XLA Ops:
  1.3 1.1 %copy-start.3 = (bf16[128,3072]{1,0:T(8,128)(2,1)S(1)}, bf16[128,3072]{1,0:T(8,128)(2,1)}, u32[]{:S(2)}) copy-start(bf16[128,3072]{1,0:T(8,128)(2,1)} %param.16) | copy-start | bytes 2359300
  2.4 6.0 %copy-start.4 = (bf16[2,3072]{1,0:T(2,128)(2,1)S(1)}, bf16[2,3072]{1,0:T(2,128)(2,1)}, u32[]{:S(2)}) copy-start(bf16[2,3072]{1,0:T(2,128)(2,1)} %param.18) | copy-start | bytes 36868
  2.4 6.0 %copy-start.5 = (bf16[2,3072]{1,0:T(2,128)(2,1)S(1)}, bf16[2,3072]{1,0:T(2,128)(2,1)}, u32[]{:S(2)}) copy-start(bf16[2,3072]{1,0:T(2,128)(2,1)} %param.17) | copy-start | bytes 36868
  2.4 53.1 %copy-start.6 = (s32[3]{0:T(128)S(1)}, s32[3]{0:T(128)}, u32[]{:S(2)}) copy-start(s32[3]{0:T(128)} %constant.76.clone) | copy-start | bytes 40
  2.4 53.1 %copy-start.7 = (s32[3]{0:T(128)S(1)}, s32[3]{0:T(128)}, u32[]{:S(2)}) copy-start(s32[3]{0:T(128)} %constant.75.clone) | copy-start | bytes 40
  2.6 62.6 %copy-start = (bf16[2,128,3072]{2,1,0:T(8,128)(2,1)}, bf16[2,128,3072]{2,1,0:T(8,128)(2,1)S(1)}, u32[]{:S(2)}) copy-start(bf16[2,128,3072]{2,1,0:T(8,128)(2,1)S(1)} %pad_maximum_fusion.k0.v0) | copy-start | bytes 4718596
  2.6 45.3 %collective-permute-start.5 = (bf16[2,128,3072]{2,1,0:T(8,128)(2,1)S(1)}, bf16[2,128,3072]{2,1,0:T(8,128)(2,1)S(1)}, u32[]{:S(2)}, u32[]{:S(2)}) collective-permute-start(bf16[2,128,3072]{2,1,0:T(8,128)(2,1)S(1)} %pad_maximum_fusion.k0.v0), channel_id=1, source_target_pairs={{0,2},{1,3},{2,4},{3,5},{4,6},{5,7},{6,8},{7,9},{8,10},{9,11},{10,... | collective-permute-start | bytes 4718600 | tf_op jit(solution)/shard_map/ppermute | solution.py:112
  9.1 30.4 %collective-permute-start = (bf16[2,6272]{1,0:T(2,128)(2,1)}, bf16[2,6272]{1,0:T(2,128)(2,1)}, u32[]{:S(2)}, u32[]{:S(2)}) collective-permute-start(bf16[2,6272]{1,0:T(2,128)(2,1)} %pad_maximum_fusion.4), channel_id=1, source_target_pairs={{0,8},{1,9},{2,10},{3,11},{4,12},{5,13},{6,14},{7,15},{8,0},{9,1},... | collective-permute-start | bytes 75272 | tf_op jit(solution)/shard_map/ppermute | solution.py:88
  40.3 7.7 %collective-permute-start.1 = (bf16[4,6272]{1,0:T(4,128)(2,1)S(1)}, bf16[4,6272]{1,0:T(4,128)(2,1)}, u32[]{:S(2)}, u32[]{:S(2)}) collective-permute-start(bf16[4,6272]{1,0:T(4,128)(2,1)S(1)} %pad_maximum_fusion.3), channel_id=1, source_target_pairs={{0,4},{1,5},{2,6},{3,7},{4,0},{5,1},{6,2},{7,3},{8,12},{9,13},{10,... | collective-permute-start | bytes 150536 | tf_op jit(solution)/shard_map/ppermute | solution.py:88
  40.4 24.8 %collective-permute-start.4 = (bf16[2,128,3072]{2,1,0:T(8,128)(2,1)S(1)}, bf16[2,128,3072]{2,1,0:T(8,128)(2,1)}, u32[]{:S(2)}, u32[]{:S(2)}) collective-permute-start(bf16[2,128,3072]{2,1,0:T(8,128)(2,1)S(1)} %pad_maximum_fusion.k0.v0), channel_id=1, source_target_pairs={{0,1},{2,3},{4,5},{6,7},{8,9},{10,11},{12,13},{14,15},{1,4},{3,6},... | collective-permute-start | bytes 4718600 | tf_op jit(solution)/shard_map/ppermute | solution.py:113
  47.9 17.3 %copy-start.1 = (bf16[2,128,3072]{2,1,0:T(8,128)(2,1)}, bf16[2,128,3072]{2,1,0:T(8,128)(2,1)S(1)}, u32[]{:S(2)}) copy-start(bf16[2,128,3072]{2,1,0:T(8,128)(2,1)S(1)} %collective-permute-done.5.k2.v2) | copy-start | bytes 4718596
  47.9 17.3 %collective-permute-start.6 = (bf16[2,128,3072]{2,1,0:T(8,128)(2,1)S(1)}, bf16[2,128,3072]{2,1,0:T(8,128)(2,1)}, u32[]{:S(2)}, u32[]{:S(2)}) collective-permute-start(bf16[2,128,3072]{2,1,0:T(8,128)(2,1)S(1)} %collective-permute-done.5.k2.v2), channel_id=1, source_target_pairs={{0,1},{1,0},{2,3},{3,2},{4,5},{5,4},{6,7},{7,6},{8,9},{9,8},{10,11... | collective-permute-start | bytes 4718600 | tf_op jit(solution)/shard_map/ppermute | solution.py:115
  48.9 4.1 %collective-permute-start.2 = (bf16[8,6272]{1,0:T(8,128)(2,1)S(1)}, bf16[8,6272]{1,0:T(8,128)(2,1)}, u32[]{:S(2)}, u32[]{:S(2)}) collective-permute-start(bf16[8,6272]{1,0:T(8,128)(2,1)S(1)} %pad_maximum_fusion.2), channel_id=1, source_target_pairs={{0,2},{1,3},{2,0},{3,1},{4,6},{5,7},{6,4},{7,5},{8,10},{9,11},{10,... | collective-permute-start | bytes 301064 | tf_op jit(solution)/shard_map/ppermute | solution.py:88
  54.1 2.6 %collective-permute-start.3 = (bf16[16,6272]{1,0:T(8,128)(2,1)S(1)}, bf16[16,6272]{1,0:T(8,128)(2,1)}, u32[]{:S(2)}, u32[]{:S(2)}) collective-permute-start(bf16[16,6272]{1,0:T(8,128)(2,1)S(1)} %pad_maximum_fusion.1), channel_id=1, source_target_pairs={{0,1},{1,0},{2,3},{3,2},{4,5},{5,4},{6,7},{7,6},{8,9},{9,8},{10,11... | collective-permute-start | bytes 602120 | tf_op jit(solution)/shard_map/ppermute | solution.py:88
  59.5 5.7 %copy-start.2 = (bf16[32,6272]{1,0:T(8,128)(2,1)}, bf16[32,6272]{1,0:T(8,128)(2,1)S(1)}, u32[]{:S(2)}) copy-start(bf16[32,6272]{1,0:T(8,128)(2,1)S(1)} %concatenate.29.ck.cv) | copy-start | bytes 1204228

commit v6 on v5

--- a/solution.py
+++ b/solution.py
@@ -13,7 +13,7 @@
 HEADS_PER_STEP = 4
 
 
-def attention_kernel(table_ref, q_ref, k0, v0, k1, v1, k2, v2, k3, v3, ck, cv, gate_ref, o_ref, *, heads):
+def attention_kernel(table_ref, q_ref, k0, v0, k1, v1, k2, v2, k3, v3, ck0, cv0, ck1, cv1, gate_ref, o_ref, *, heads):
     scale = 1.0 / math.sqrt(HEAD_DIM)
     rows = q_ref.shape[0]
     slot = lax.broadcasted_iota(jnp.int32, (1, rows), 1)
@@ -30,27 +30,28 @@
         for j, (k_ref, _) in enumerate(blocks):
             s = jnp.dot(q, k_ref[:, cols], preferred_element_type=jnp.float32) * scale
             scores.append(jnp.where(slot < table_ref[j], s, -jnp.inf))
-        scores.append(lax.dot_general(q, ck[:, cols], dims, preferred_element_type=jnp.float32) * scale)
+        cache_keys = jnp.concatenate([ck0[:, cols], ck1[:, cols]], 0)
+        scores.append(lax.dot_general(q, cache_keys, dims, preferred_element_type=jnp.float32) * scale)
         row_max = scores[0].max(axis=1, keepdims=True)
         for s in scores[1:]:
             row_max = jnp.maximum(row_max, s.max(axis=1, keepdims=True))
-        values = [v_ref for _, v_ref in blocks] + [cv]
+        values = [v_ref[:, cols] for _, v_ref in blocks] + [jnp.concatenate([cv0[:, cols], cv1[:, cols]], 0)]
         denominator = jnp.zeros((rows, 1), jnp.float32)
         attended = jnp.zeros((rows, HEAD_DIM), jnp.float32)
         for s, v_ref in zip(scores, values):
             p = jnp.exp(s - row_max)
             denominator = denominator + p.sum(axis=1, keepdims=True)
-            attended = attended + jnp.dot(p.astype(jnp.bfloat16), v_ref[:, cols], preferred_element_type=jnp.float32)
+            attended = attended + jnp.dot(p.astype(jnp.bfloat16), v_ref, preferred_element_type=jnp.float32)
         attended = attended / denominator
         out = jnp.where(live_row, attended * gate[:, cols], 0.0)
         o_ref[:, cols] = out.astype(o_ref.dtype)
 
 
-def attend(table, queries, kv_own, kv_a, kv_b, kv_c, cache, gate_table):
+def attend(table, queries, kv_own, kv_a, kv_b, kv_c, cache_low, cache_high, gate_table):
     rows, feat = queries.shape
     width = HEADS_PER_STEP * HEAD_DIM
     steps = feat // width
-    cache_rows = cache.shape[0]
+    cache_rows = cache_low.shape[0]
     levels = gate_table.shape[0]
     row_block = pl.BlockSpec((rows, width), lambda h, t: (0, h))
     k_block = pl.BlockSpec((None, rows, width), lambda h, t: (0, 0, h))
@@ -62,33 +63,35 @@
         num_scalar_prefetch=1,
         grid=(steps,),
         in_specs=[row_block, k_block, v_block, k_block, v_block, k_block, v_block, k_block, v_block,
-                  cache_k_block, cache_v_block, gate_block],
+                  cache_k_block, cache_v_block, cache_k_block, cache_v_block, gate_block],
         out_specs=row_block,
     )
-    keys = 4 * rows + cache_rows
+    keys = 4 * rows + 2 * cache_rows
     cost = pl.CostEstimate(
         flops=4 * rows * keys * feat,
         transcendentals=rows * keys * (feat // HEAD_DIM),
-        bytes_accessed=2 * (2 * rows * feat + 8 * rows * feat + 2 * cache_rows * feat) + 4 * levels * feat,
+        bytes_accessed=2 * (2 * rows * feat + 8 * rows * feat + 4 * cache_rows * feat) + 4 * levels * feat,
     )
     return pl.pallas_call(
         functools.partial(attention_kernel, heads=HEADS_PER_STEP),
         out_shape=jax.ShapeDtypeStruct((rows, feat), jnp.bfloat16),
         grid_spec=grid_spec,
         cost_estimate=cost,
-    )(table, queries, kv_own, kv_own, kv_a, kv_a, kv_b, kv_b, kv_c, kv_c, cache, cache, gate_table)
+    )(table, queries, kv_own, kv_own, kv_a, kv_a, kv_b, kv_b, kv_c, kv_c, cache_low, cache_low, cache_high, cache_high, gate_table)
 
 
 def gather_pieces(piece, size):
-    if size & (size - 1):
-        return lax.all_gather(piece, "group", axis=0, tiled=True)
+    if size & (size - 1) or size < 2:
+        whole = lax.all_gather(piece, "group", axis=0, tiled=True)
+        half = whole.shape[0] // 2
+        return whole[:half], whole[half:]
     held = piece
     step = size // 2
-    while step >= 1:
+    while step > 1:
         other = lax.ppermute(held, "group", [(i, i ^ step) for i in range(size)])
         held = jnp.concatenate([held, other], 0)
         step //= 2
-    return held
+    return held, lax.ppermute(held, "group", [(i, i ^ 1) for i in range(size)])
 
 
 def body(queries, fresh_keys, fresh_values, cache_keys, cache_values, lengths, levels, gate_table):
@@ -100,9 +103,7 @@
     tag = jnp.zeros((cache_rows, HEAD_DIM), jnp.bfloat16)
     tag = tag.at[0, 0].set(lengths[0].astype(jnp.bfloat16)).at[0, 1].set(me.astype(jnp.bfloat16))
     packed = jnp.concatenate([cache_keys, cache_values, tag], 1)
-    gathered = gather_pieces(packed, size)
-    piece_lengths = gathered[:, 2 * feat_width].astype(jnp.int32)
-    piece_index = gathered[:, 2 * feat_width + 1].astype(jnp.int32)
+    gathered = None
 
     head_count = feat_width // HEAD_DIM
     keys_by_head = fresh_keys.reshape(row_count, head_count, HEAD_DIM).transpose(2, 1, 0).reshape(HEAD_DIM, head_count * row_count)
@@ -111,15 +112,21 @@
     pairs_mixed = [(i, i + 1) for i in range(0, size - 1, 2)] + [(i, i + 3) for i in range(1, size - 3, 2)]
     from_two = lax.ppermute(kv, "group", pairs_two)
     from_mixed = lax.ppermute(kv, "group", pairs_mixed)
+
+    packed, from_mixed, from_two = lax.optimization_barrier((packed, from_mixed, from_two))
     pairs_swap = [(i, i ^ 1) for i in range(size)]
     from_swap = lax.ppermute(from_two, "group", pairs_swap)
+    cache_low, cache_high = gather_pieces(packed, size)
+    tags = jnp.concatenate([cache_low[:, 2 * feat_width:2 * feat_width + 2], cache_high[:, 2 * feat_width:2 * feat_width + 2]], 0)
+    piece_lengths = tags[:, 0].astype(jnp.int32)
+    piece_index = tags[:, 1].astype(jnp.int32)
 
     odd = (me % 2) == 1
     offsets = jnp.where(odd, jnp.array([1, 2, 3], jnp.int32), jnp.array([3, 2, 1], jnp.int32))
     sources = me - offsets
     previous = jnp.sum(jnp.where(piece_index[None, :] == sources[:, None], piece_lengths[None, :], 0), axis=1)
     table = jnp.concatenate([lengths[:1], previous, levels[:1]]).astype(jnp.int32)
-    return attend(table, queries, kv, from_mixed, from_two, from_swap, gathered, gate_table)
+    return attend(table, queries, kv, from_mixed, from_two, from_swap, cache_low, cache_high, gate_table)
 
 
 def solution(mesh):

time: 76 us -> 86.7 us (1.14)
  waiting for transfers between devices: 39.3 us -> 50.7 us
  starting transfers between devices: 12.7 us -> 15.4 us
  local copies, waits for them, and re-layouts: 7.2 us -> 5.57 us
  other arithmetic: 4.61 us -> 3.55 us
    ppermute x4 -> x3, waiting for transfers between devices: 34.6 us -> 6.36 us  [gather_pieces(): other = lax.ppermute(held, 'group', [(i, i ^ step) for i in range(size)])]
    ppermute x1, waiting for transfers between devices: 0.01 us -> 27.4 us  [body(): from_two = lax.ppermute(kv, 'group', pairs_two)]
    ppermute x1, waiting for transfers between devices: 4.68 us -> 16.9 us  [body(): from_mixed = lax.ppermute(kv, 'group', pairs_mixed)]
    ppermute x0 -> x1, starting transfers between devices: none -> 4.07 us  [gather_pieces(): lax.ppermute(held, 'group', [(i, i ^ 1) for i in range(size)])]
    ppermute x1, starting transfers between devices: 0.07 us -> 3.77 us  [body(): from_swap = lax.ppermute(from_two, 'group', pairs_swap)]
    ppermute x1, starting transfers between devices: 7.45 us -> 4.05 us  [body(): from_mixed = lax.ppermute(kv, 'group', pairs_mixed)]
    concatenate x1 -> x0, local copies, waits for them, and re-layouts: 2.79 us -> none  [gather_pieces(): held = jnp.concatenate([held, other], 0)]
    ppermute x4 -> x3, starting transfers between devices: 1.95 us -> 0.31 us  [gather_pieces(): other = lax.ppermute(held, 'group', [(i, i ^ step) for i in range(size)])]
  transfers between devices with their start and end apart: 7 -> 7, of which waited for: 4 -> 4; matrix products, arithmetic and copies ran while one was open for 12% -> 7% of each run, Pallas kernels for 0% -> 0%
where the time goes in v6:
time: 86.7 us; the launch traced here: 86 us
  waiting for transfers between devices  50.7 us (58%)
  starting transfers between devices  15.4 us (18%)
  Pallas kernels  9.36 us (11%)
  local copies, waits for them, and re-layouts  5.57 us (6%)
  other arithmetic  3.55 us (4%)
  between operations  1.48 us (2%)
    ppermute x1, waiting for transfers between devices, body(): from_two = lax.ppermute(kv, 'group', pairs_two)  27.4 us
    ppermute x1, waiting for transfers between devices, body(): from_mixed = lax.ppermute(kv, 'group', pairs_mixed)  16.9 us
    pallas_call x1, Pallas kernels, attend(): pl.pallas_call(functools.partial(attention_kernel, heads=HEADS_PER_STEP),...  9.36 us
    ppermute x3, waiting for transfers between devices, gather_pieces(): other = lax.ppermute(held, 'group', [(i, i ^ step) for i in range(size)])  6.36 us
    ppermute x1, starting transfers between devices, gather_pieces(): lax.ppermute(held, 'group', [(i, i ^ 1) for i in range(size)])  4.07 us
    ppermute x1, starting transfers between devices, body(): from_mixed = lax.ppermute(kv, 'group', pairs_mixed)  4.05 us
    ppermute x1, starting transfers between devices, body(): from_swap = lax.ppermute(from_two, 'group', pairs_swap)  3.77 us
    ppermute x1, starting transfers between devices, body(): from_two = lax.ppermute(kv, 'group', pairs_two)  3.18 us
  transfers between devices with their start and end apart: 7, of which 4 were waited for; matrix products, arithmetic and copies ran while one was open for 7% of the time, Pallas kernels for 0%

profile of v6, /device:TPU:15, one launch (start us, length us, event | category | flops | bytes accessed | tf_op | source)
XLA Modules:
  0.0 86.0 jit_solution(13944936354858241347)
XLA Ops:
  0.0 1.3 %copy.19 = bf16[16,8,24,128]{3,2,1,0:T(8,128)(2,1)S(1)} copy(bf16[16,8,24,128]{3,1,2,0:T(8,128)(2,1)} %bitcast.16) | data formatting | bytes 1572864
  1.3 0.0 copy-start.4
  1.3 0.7 copy.16
  2.0 0.3 stack_reshape.3
  2.3 0.1 copy-done.4
  2.4 0.0 copy-start.5
  2.4 0.0 copy-start.6
  2.4 0.0 copy-start.7
  2.4 0.1 pad_maximum_fusion.k0.v0
  2.6 0.0 copy-start
  2.6 3.2 %collective-permute-start.1 = (bf16[2,128,3072]{2,1,0:T(8,128)(2,1)S(1)}, bf16[2,128,3072]{2,1,0:T(8,128)(2,1)S(1)}, u32[]{:S(2)}, u32[]{:S(2)}) collective-permute-start(bf16[2,128,3072]{2,1,0:T(8,128)(2,1)S(1)} %pad_maximum_fusion.k0.v0), channel_id=1, source_target_pairs={{0,2},{1,3},{2,4},{3,5},{4,6},{5,7},{6,8},{7,9},{8,10},{9,11},{10,... | collective-permute-start | bytes 4718600 | tf_op jit(solution)/shard_map/ppermute | solution.py:113
  5.8 4.0 %collective-permute-start = (bf16[2,128,3072]{2,1,0:T(8,128)(2,1)S(1)}, bf16[2,128,3072]{2,1,0:T(8,128)(2,1)}, u32[]{:S(2)}, u32[]{:S(2)}) collective-permute-start(bf16[2,128,3072]{2,1,0:T(8,128)(2,1)S(1)} %pad_maximum_fusion.k0.v0), channel_id=1, source_target_pairs={{0,1},{2,3},{4,5},{6,7},{8,9},{10,11},{12,13},{14,15},{1,4},{3,6},... | collective-permute-start | bytes 4718600 | tf_op jit(solution)/shard_map/ppermute | solution.py:114
  10.5 0.6 fusion.1
  11.1 1.3 %scatter.9 = bf16[2,128]{1,0:T(2,128)(2,1)S(1)} dynamic-update-slice(bf16[2,128]{1,0:T(2,128)(2,1)S(1)} %scatter.6, bf16[1,1]{1,0:T(2,128)(2,1)} %bitcast.1, s32[]{:T(128)} %bitcast.2, s32[]{:T(128)} %bitcast.3) | dynamic-update-slice | bytes 8 | tf_op jit(solution)/shard_map/scatter | solution.py:104
  12.4 0.0 copy-done.5
  12.4 0.0 copy-done.6
  12.5 27.4 %collective-permute-done.1.k2.v2 = bf16[2,128,3072]{2,1,0:T(8,128)(2,1)S(1)} collective-permute-done((bf16[2,128,3072]{2,1,0:T(8,128)(2,1)S(1)}, bf16[2,128,3072]{2,1,0:T(8,128)(2,1)S(1)}, u32[]{:S(2)}, u32[]{:S(2)}) %collective-permute-start.1) | collective-permute-done | bytes 1572896 | tf_op jit(solution)/shard_map/ppermute | solution.py:113
  39.9 0.0 copy-start.1
  39.9 16.9 %collective-permute-done.k1.v1 = bf16[2,128,3072]{2,1,0:T(8,128)(2,1)} collective-permute-done((bf16[2,128,3072]{2,1,0:T(8,128)(2,1)S(1)}, bf16[2,128,3072]{2,1,0:T(8,128)(2,1)}, u32[]{:S(2)}, u32[]{:S(2)}) %collective-permute-start) | collective-permute-done | bytes 1572896 | tf_op jit(solution)/shard_map/ppermute | solution.py:114
  56.8 0.0 collective-permute-start.2
  56.8 3.6 %collective-permute-done.2 = bf16[2,6272]{1,0:T(2,128)(2,1)S(1)} collective-permute-done((bf16[2,6272]{1,0:T(2,128)(2,1)S(1)}, bf16[2,6272]{1,0:T(2,128)(2,1)S(1)}, u32[]{:S(2)}, u32[]{:S(2)}) %collective-permute-start.2) | collective-permute-done | bytes 25120 | tf_op jit(solution)/shard_map/ppermute | solution.py:91
  60.4 0.1 pad_maximum_fusion.3
  60.5 0.2 collective-permute-start.3
  60.7 2.8 %collective-permute-done.3 = bf16[4,6272]{1,0:T(4,128)(2,1)S(1)} collective-permute-done((bf16[4,6272]{1,0:T(4,128)(2,1)S(1)}, bf16[4,6272]{1,0:T(4,128)(2,1)S(1)}, u32[]{:S(2)}, u32[]{:S(2)}) %collective-permute-start.3) | collective-permute-done | bytes 50208 | tf_op jit(solution)/shard_map/ppermute | solution.py:91
  63.5 0.1 pad_maximum_fusion.2
  63.6 0.1 collective-permute-start.4
  64.3 3.8 %collective-permute-start.6 = (bf16[2,128,3072]{2,1,0:T(8,128)(2,1)S(1)}, bf16[2,128,3072]{2,1,0:T(8,128)(2,1)}, u32[]{:S(2)}, u32[]{:S(2)}) collective-permute-start(bf16[2,128,3072]{2,1,0:T(8,128)(2,1)S(1)} %collective-permute-done.1.k2.v2), channel_id=1, source_target_pairs={{0,1},{1,0},{2,3},{3,2},{4,5},{5,4},{6,7},{7,6},{8,9},{9,8},{10,11... | collective-permute-start | bytes 4718600 | tf_op jit(solution)/shard_map/ppermute | solution.py:118
  68.1 0.0 collective-permute-done.4
  68.1 1.0 %pad_maximum_fusion.1.ck0.cv0 = bf16[16,6272]{1,0:T(8,128)(2,1)S(1)} fusion(bf16[8,6272]{1,0:T(8,128)(2,1)} %collective-permute-done.4, bf16[4,6272]{1,0:T(4,128)(2,1)S(1)} %collective-permute-done.3, bf16[2,6272]{1,0:T(2,128)(2,1)S(1)} %collective-permute-done.2, bf16[2,6272]{1,0:T(2,128)(2,1)S(1)} %pad_maximum_fusion.4), kind=kLoop, calls=%fused_computation.1 | loop fusion | flops 802816 | bytes 401408 | tf_op jit(solution)/shard_map/concatenate | solution.py:92
  69.1 0.0 copy-start.2
  69.1 4.1 %collective-permute-start.5 = (bf16[16,6272]{1,0:T(8,128)(2,1)S(1)}, bf16[16,6272]{1,0:T(8,128)(2,1)S(1)}, u32[]{:S(2)}, u32[]{:S(2)}) collective-permute-start(bf16[16,6272]{1,0:T(8,128)(2,1)S(1)} %pad_maximum_fusion.1.ck0.cv0), channel_id=1, source_target_pairs={{0,1},{1,0},{2,3},{3,2},{4,5},{5,4},{6,7},{7,6},{8,9},{9,8},{10,11... | collective-permute-start | bytes 602120 | tf_op jit(solution)/shard_map/ppermute | solution.py:94
  73.2 0.0 copy-done.7
  73.2 0.7 fusion
  73.9 0.6 copy.17
  74.5 0.0 collective-permute-done.5.ck1.cv1
  74.5 0.0 copy-start.3
  74.5 0.6 copy.18
  75.1 0.7 pad_maximum_fusion.5
  75.8 0.2 select_reduce_fusion
  76.0 0.6 pad_add_fusion.table_ref
  76.6 0.0 collective-permute-done.6.k3.v3
  76.6 0.0 copy-done
  76.7 0.0 copy-done.1
  76.7 0.0 copy-done.2
  76.7 0.0 copy-done.3
  76.7 9.4 %shard_map.100 = bf16[128,3072]{1,0:T(8,128)(2,1)} custom-call(s32[5]{0:T(128)} %pad_add_fusion.table_ref, bf16[128,3072]{1,0:T(8,128)(2,1)} %q_ref.1, bf16[2,128,3072]{2,1,0:T(8,128)(2,1)} %copy-done, bf16[2,128,3072]{2,1,0:T(8,128)(2,1)} %copy-done, bf16[2,128,3072]{2,1,0:T(8,128)(2,1)} %collective-permute-done.k1.v1, ...), custom_call_target="tpu_custom_call" | custom-call | flops 855638016 | bytes 8454144 | tf_op jit(solution)/shard_map/pallas_call | solution.py:75
  (6 shorter events, 0.0 us)
Async XLA Ops:
  1.3 1.1 %copy-start.4 = (bf16[128,3072]{1,0:T(8,128)(2,1)S(1)}, bf16[128,3072]{1,0:T(8,128)(2,1)}, u32[]{:S(2)}) copy-start(bf16[128,3072]{1,0:T(8,128)(2,1)} %param.16) | copy-start | bytes 2359300
  2.4 10.0 %copy-start.5 = (bf16[2,3072]{1,0:T(2,128)(2,1)S(1)}, bf16[2,3072]{1,0:T(2,128)(2,1)}, u32[]{:S(2)}) copy-start(bf16[2,3072]{1,0:T(2,128)(2,1)} %param.18) | copy-start | bytes 36868
  2.4 10.0 %copy-start.6 = (bf16[2,3072]{1,0:T(2,128)(2,1)S(1)}, bf16[2,3072]{1,0:T(2,128)(2,1)}, u32[]{:S(2)}) copy-start(bf16[2,3072]{1,0:T(2,128)(2,1)} %param.17) | copy-start | bytes 36868
  2.4 70.8 %copy-start.7 = (s32[3]{0:T(128)S(1)}, s32[3]{0:T(128)}, u32[]{:S(2)}) copy-start(s32[3]{0:T(128)} %constant.76.clone) | copy-start | bytes 40
  2.6 74.1 %copy-start = (bf16[2,128,3072]{2,1,0:T(8,128)(2,1)}, bf16[2,128,3072]{2,1,0:T(8,128)(2,1)S(1)}, u32[]{:S(2)}) copy-start(bf16[2,128,3072]{2,1,0:T(8,128)(2,1)S(1)} %pad_maximum_fusion.k0.v0) | copy-start | bytes 4718596
  2.6 37.3 %collective-permute-start.1 = (bf16[2,128,3072]{2,1,0:T(8,128)(2,1)S(1)}, bf16[2,128,3072]{2,1,0:T(8,128)(2,1)S(1)}, u32[]{:S(2)}, u32[]{:S(2)}) collective-permute-start(bf16[2,128,3072]{2,1,0:T(8,128)(2,1)S(1)} %pad_maximum_fusion.k0.v0), channel_id=1, source_target_pairs={{0,2},{1,3},{2,4},{3,5},{4,6},{5,7},{6,8},{7,9},{8,10},{9,11},{10,... | collective-permute-start | bytes 4718600 | tf_op jit(solution)/shard_map/ppermute | solution.py:113
  5.8 51.0 %collective-permute-start = (bf16[2,128,3072]{2,1,0:T(8,128)(2,1)S(1)}, bf16[2,128,3072]{2,1,0:T(8,128)(2,1)}, u32[]{:S(2)}, u32[]{:S(2)}) collective-permute-start(bf16[2,128,3072]{2,1,0:T(8,128)(2,1)S(1)} %pad_maximum_fusion.k0.v0), channel_id=1, source_target_pairs={{0,1},{2,3},{4,5},{6,7},{8,9},{10,11},{12,13},{14,15},{1,4},{3,6},... | collective-permute-start | bytes 4718600 | tf_op jit(solution)/shard_map/ppermute | solution.py:114
  39.9 36.8 %copy-start.1 = (bf16[2,128,3072]{2,1,0:T(8,128)(2,1)}, bf16[2,128,3072]{2,1,0:T(8,128)(2,1)S(1)}, u32[]{:S(2)}) copy-start(bf16[2,128,3072]{2,1,0:T(8,128)(2,1)S(1)} %collective-permute-done.1.k2.v2) | copy-start | bytes 4718596
  56.8 3.6 %collective-permute-start.2 = (bf16[2,6272]{1,0:T(2,128)(2,1)S(1)}, bf16[2,6272]{1,0:T(2,128)(2,1)S(1)}, u32[]{:S(2)}, u32[]{:S(2)}) collective-permute-start(bf16[2,6272]{1,0:T(2,128)(2,1)S(1)} %pad_maximum_fusion.4), channel_id=1, source_target_pairs={{0,8},{1,9},{2,10},{3,11},{4,12},{5,13},{6,14},{7,15},{8,0},{9,1},... | collective-permute-start | bytes 75272 | tf_op jit(solution)/shard_map/ppermute | solution.py:91
  60.5 3.0 %collective-permute-start.3 = (bf16[4,6272]{1,0:T(4,128)(2,1)S(1)}, bf16[4,6272]{1,0:T(4,128)(2,1)S(1)}, u32[]{:S(2)}, u32[]{:S(2)}) collective-permute-start(bf16[4,6272]{1,0:T(4,128)(2,1)S(1)} %pad_maximum_fusion.3), channel_id=1, source_target_pairs={{0,4},{1,5},{2,6},{3,7},{4,0},{5,1},{6,2},{7,3},{8,12},{9,13},{10,... | collective-permute-start | bytes 150536 | tf_op jit(solution)/shard_map/ppermute | solution.py:91
  63.6 4.5 %collective-permute-start.4 = (bf16[8,6272]{1,0:T(8,128)(2,1)S(1)}, bf16[8,6272]{1,0:T(8,128)(2,1)}, u32[]{:S(2)}, u32[]{:S(2)}) collective-permute-start(bf16[8,6272]{1,0:T(8,128)(2,1)S(1)} %pad_maximum_fusion.2), channel_id=1, source_target_pairs={{0,2},{1,3},{2,0},{3,1},{4,6},{5,7},{6,4},{7,5},{8,10},{9,11},{10,... | collective-permute-start | bytes 301064 | tf_op jit(solution)/shard_map/ppermute | solution.py:91
  64.3 12.3 %collective-permute-start.6 = (bf16[2,128,3072]{2,1,0:T(8,128)(2,1)S(1)}, bf16[2,128,3072]{2,1,0:T(8,128)(2,1)}, u32[]{:S(2)}, u32[]{:S(2)}) collective-permute-start(bf16[2,128,3072]{2,1,0:T(8,128)(2,1)S(1)} %collective-permute-done.1.k2.v2), channel_id=1, source_target_pairs={{0,1},{1,0},{2,3},{3,2},{4,5},{5,4},{6,7},{7,6},{8,9},{9,8},{10,11... | collective-permute-start | bytes 4718600 | tf_op jit(solution)/shard_map/ppermute | solution.py:118
  69.1 7.5 %copy-start.2 = (bf16[16,6272]{1,0:T(8,128)(2,1)}, bf16[16,6272]{1,0:T(8,128)(2,1)S(1)}, u32[]{:S(2)}) copy-start(bf16[16,6272]{1,0:T(8,128)(2,1)S(1)} %pad_maximum_fusion.1.ck0.cv0) | copy-start | bytes 602116
  69.1 5.4 %collective-permute-start.5 = (bf16[16,6272]{1,0:T(8,128)(2,1)S(1)}, bf16[16,6272]{1,0:T(8,128)(2,1)S(1)}, u32[]{:S(2)}, u32[]{:S(2)}) collective-permute-start(bf16[16,6272]{1,0:T(8,128)(2,1)S(1)} %pad_maximum_fusion.1.ck0.cv0), channel_id=1, source_target_pairs={{0,1},{1,0},{2,3},{3,2},{4,5},{5,4},{6,7},{7,6},{8,9},{9,8},{10,11... | collective-permute-start | bytes 602120 | tf_op jit(solution)/shard_map/ppermute | solution.py:94
  74.5 2.2 %copy-start.3 = (bf16[16,6272]{1,0:T(8,128)(2,1)}, bf16[16,6272]{1,0:T(8,128)(2,1)S(1)}, u32[]{:S(2)}) copy-start(bf16[16,6272]{1,0:T(8,128)(2,1)S(1)} %collective-permute-done.5.ck1.cv1) | copy-start | bytes 602116

commit v7 on v6

--- a/solution.py
+++ b/solution.py
@@ -112,11 +112,10 @@
     pairs_mixed = [(i, i + 1) for i in range(0, size - 1, 2)] + [(i, i + 3) for i in range(1, size - 3, 2)]
     from_two = lax.ppermute(kv, "group", pairs_two)
     from_mixed = lax.ppermute(kv, "group", pairs_mixed)
-
-    packed, from_mixed, from_two = lax.optimization_barrier((packed, from_mixed, from_two))
     pairs_swap = [(i, i ^ 1) for i in range(size)]
     from_swap = lax.ppermute(from_two, "group", pairs_swap)
-    cache_low, cache_high = gather_pieces(packed, size)
+
+    cache_low, cache_high = lax.cond(me >= 0, lambda x: gather_pieces(x, size), lambda x: gather_pieces(x, size), packed)
     tags = jnp.concatenate([cache_low[:, 2 * feat_width:2 * feat_width + 2], cache_high[:, 2 * feat_width:2 * feat_width + 2]], 0)
     piece_lengths = tags[:, 0].astype(jnp.int32)
     piece_index = tags[:, 1].astype(jnp.int32)

time: 86.7 us -> 85.1 us (0.982)
  the two profiles are of different devices: /device:TPU:15 before, /device:TPU:0 now
where the time goes in v7:
time: 85.1 us; the launch traced here: 84.6 us
  waiting for transfers between devices  39.6 us (47%)
  starting transfers between devices  21.1 us (25%)
  local copies, waits for them, and re-layouts  9.72 us (11%)
  Pallas kernels  9.39 us (11%)
  other arithmetic  3.29 us (4%)
  between operations  1.41 us (2%)
    ppermute x1, waiting for transfers between devices, body(): from_two = lax.ppermute(kv, 'group', pairs_two)  30.3 us
    pallas_call x1, Pallas kernels, attend(): pl.pallas_call(functools.partial(attention_kernel, heads=HEADS_PER_STEP),...  9.39 us
    ppermute x3, waiting for transfers between devices, gather_pieces(): other = lax.ppermute(held, 'group', [(i, i ^ step) for i in range(size)])  8.8 us
    ppermute x3, starting transfers between devices, gather_pieces(): other = lax.ppermute(held, 'group', [(i, i ^ step) for i in range(size)])  7.63 us
    ppermute x1, starting transfers between devices, gather_pieces(): lax.ppermute(held, 'group', [(i, i ^ 1) for i in range(size)])  5.89 us
    ppermute x1, starting transfers between devices, body(): from_two = lax.ppermute(kv, 'group', pairs_two)  4.97 us
    ppermute x1, starting transfers between devices, body(): from_mixed = lax.ppermute(kv, 'group', pairs_mixed)  2.63 us
    unnamed x14, local copies, waits for them, and re-layouts  2 us
  transfers between devices with their start and end apart: 7, of which 5 were waited for; matrix products, arithmetic and copies ran while one was open for 12% of the time, Pallas kernels for 0%

profile of v7, /device:TPU:0, one launch (start us, length us, event | category | flops | bytes accessed | tf_op | source)
XLA Modules:
  0.0 84.6 jit_solution(1284746022780753287)
XLA Ops:
  0.0 1.3 %copy.19 = bf16[16,8,24,128]{3,2,1,0:T(8,128)(2,1)S(1)} copy(bf16[16,8,24,128]{3,1,2,0:T(8,128)(2,1)} %bitcast.16) | data formatting | bytes 1572864
  1.3 0.0 copy-start.2
  1.3 0.7 copy.18
  2.0 0.3 stack_reshape.3
  2.3 0.1 copy-done.2
  2.4 0.0 copy-start.3
  2.4 0.0 copy-start.4
  2.4 0.1 pad_maximum_fusion.6.k0.v0
  2.6 0.0 copy-start
  2.6 5.0 %collective-permute-start.9 = (bf16[2,128,3072]{2,1,0:T(8,128)(2,1)S(1)}, bf16[2,128,3072]{2,1,0:T(8,128)(2,1)S(1)}, u32[]{:S(2)}, u32[]{:S(2)}) collective-permute-start(bf16[2,128,3072]{2,1,0:T(8,128)(2,1)S(1)} %pad_maximum_fusion.6.k0.v0), channel_id=1, source_target_pairs={{0,2},{1,3},{2,4},{3,5},{4,6},{5,7},{6,8},{7,9},{8,10},{9,11},{10,... | collective-permute-start | bytes 4718600 | tf_op jit(solution)/shard_map/ppermute | solution.py:113
  7.6 2.6 %collective-permute-start.8 = (bf16[2,128,3072]{2,1,0:T(8,128)(2,1)S(1)}, bf16[2,128,3072]{2,1,0:T(8,128)(2,1)}, u32[]{:S(2)}, u32[]{:S(2)}) collective-permute-start(bf16[2,128,3072]{2,1,0:T(8,128)(2,1)S(1)} %pad_maximum_fusion.6.k0.v0), channel_id=1, source_target_pairs={{0,1},{2,3},{4,5},{6,7},{8,9},{10,11},{12,13},{14,15},{1,4},{3,6},... | collective-permute-start | bytes 4718600 | tf_op jit(solution)/shard_map/ppermute | solution.py:114
  10.2 0.6 fusion.1
  10.8 30.3 %collective-permute-done.9.k2.v2 = bf16[2,128,3072]{2,1,0:T(8,128)(2,1)S(1)} collective-permute-done((bf16[2,128,3072]{2,1,0:T(8,128)(2,1)S(1)}, bf16[2,128,3072]{2,1,0:T(8,128)(2,1)S(1)}, u32[]{:S(2)}, u32[]{:S(2)}) %collective-permute-start.9) | collective-permute-done | bytes 1572896 | tf_op jit(solution)/shard_map/ppermute | solution.py:113
  41.1 0.0 copy-start.1
  41.1 0.0 collective-permute-start.10
  41.8 1.3 %scatter.9 = bf16[2,128]{1,0:T(2,128)(2,1)S(1)} dynamic-update-slice(bf16[2,128]{1,0:T(2,128)(2,1)S(1)} %scatter.6, bf16[1,1]{1,0:T(2,128)(2,1)} %bitcast.1, s32[]{:T(128)} %bitcast.2, s32[]{:T(128)} %bitcast.3) | dynamic-update-slice | bytes 8 | tf_op jit(solution)/shard_map/scatter | solution.py:104
  43.1 0.0 copy-done.3
  43.1 0.0 copy-done.4
  43.2 25.7 %conditional.1 = (bf16[16,6272]{1,0:T(8,128)(2,1)}, bf16[16,6272]{1,0:T(8,128)(2,1)S(1)}, bf16[16,6272]{1,0:T(8,128)(2,1)}, bf16[16,6272]{1,0:T(8,128)(2,1)S(1)}) conditional(s32[]{:T(128)} %convert_element_type.30, bf16[2,6272]{1,0:T(2,128)(2,1)S(1)} %pad_maximum_fusion.7, bf16[2,6272]{1,0:T(2,128)(2,1)S(1)} %pad_maximum_fusion.7), branch_computations={%region_0.0_spmd, %region_1.0_spmd} | conditional | flops 1204224 | bytes 3010752 | solution.py:118
  43.2 5.7 %collective-permute-start.4 = (bf16[2,6272]{1,0:T(2,128)(2,1)S(1)}, bf16[2,6272]{1,0:T(2,128)(2,1)S(1)}, u32[]{:S(2)}, u32[]{:S(2)}) collective-permute-start(bf16[2,6272]{1,0:T(2,128)(2,1)S(1)} %param.5), channel_id=1, source_target_pairs={{0,8},{1,9},{2,10},{3,11},{4,12},{5,13},{6,14},{7,15},{8,0},{9,1},... | collective-permute-start | bytes 75272 | tf_op jit(solution)/shard_map/cond/branch_1_fun/ppermute | solution.py:91
  48.9 1.9 %collective-permute-done.4 = bf16[2,6272]{1,0:T(2,128)(2,1)S(1)} collective-permute-done((bf16[2,6272]{1,0:T(2,128)(2,1)S(1)}, bf16[2,6272]{1,0:T(2,128)(2,1)S(1)}, u32[]{:S(2)}, u32[]{:S(2)}) %collective-permute-start.4) | collective-permute-done | bytes 25120 | tf_op jit(solution)/shard_map/cond/branch_1_fun/ppermute | solution.py:91
  50.8 0.1 pad_maximum_fusion.5
  50.8 1.9 %collective-permute-start.5 = (bf16[4,6272]{1,0:T(4,128)(2,1)S(1)}, bf16[4,6272]{1,0:T(4,128)(2,1)S(1)}, u32[]{:S(2)}, u32[]{:S(2)}) collective-permute-start(bf16[4,6272]{1,0:T(4,128)(2,1)S(1)} %pad_maximum_fusion.5), channel_id=1, source_target_pairs={{0,4},{1,5},{2,6},{3,7},{4,0},{5,1},{6,2},{7,3},{8,12},{9,13},{10,... | collective-permute-start | bytes 150536 | tf_op jit(solution)/shard_map/cond/branch_1_fun/ppermute | solution.py:91
  52.7 2.3 %collective-permute-done.5 = bf16[4,6272]{1,0:T(4,128)(2,1)S(1)} collective-permute-done((bf16[4,6272]{1,0:T(4,128)(2,1)S(1)}, bf16[4,6272]{1,0:T(4,128)(2,1)S(1)}, u32[]{:S(2)}, u32[]{:S(2)}) %collective-permute-start.5) | collective-permute-done | bytes 50208 | tf_op jit(solution)/shard_map/cond/branch_1_fun/ppermute | solution.py:91
  55.0 0.1 pad_maximum_fusion.4
  55.1 0.1 collective-permute-start.6
  55.2 4.6 %collective-permute-done.6 = bf16[8,6272]{1,0:T(8,128)(2,1)S(1)} collective-permute-done((bf16[8,6272]{1,0:T(8,128)(2,1)S(1)}, bf16[8,6272]{1,0:T(8,128)(2,1)S(1)}, u32[]{:S(2)}, u32[]{:S(2)}) %collective-permute-start.6) | collective-permute-done | bytes 100384 | tf_op jit(solution)/shard_map/cond/branch_1_fun/ppermute | solution.py:91
  59.8 0.8 pad_maximum_fusion.3
  60.6 5.9 %collective-permute-start.7 = (bf16[16,6272]{1,0:T(8,128)(2,1)}, bf16[16,6272]{1,0:T(8,128)(2,1)}, u32[]{:S(2)}, u32[]{:S(2)}) collective-permute-start(bf16[16,6272]{1,0:T(8,128)(2,1)} %pad_maximum_fusion.3), channel_id=1, source_target_pairs={{0,1},{1,0},{2,3},{3,2},{4,5},{5,4},{6,7},{7,6},{8,9},{9,8},{10,11... | collective-permute-start | bytes 602120 | tf_op jit(solution)/shard_map/cond/branch_1_fun/ppermute | solution.py:94
  66.5 0.9 %copy.31 = bf16[16,6272]{1,0:T(8,128)(2,1)S(1)} copy(bf16[16,6272]{1,0:T(8,128)(2,1)} %pad_maximum_fusion.3) | data formatting | bytes 401408 | tf_op jit(solution)/shard_map/cond
  67.4 0.5 collective-permute-done.7
  67.9 0.9 %copy.36 = bf16[16,6272]{1,0:T(8,128)(2,1)S(1)} copy(bf16[16,6272]{1,0:T(8,128)(2,1)} %collective-permute-done.7) | data formatting | bytes 401408 | tf_op jit(solution)/shard_map/cond
  68.8 0.0 copy-start.5
  68.8 1.7 %copy.16 = bf16[16,6272]{0,1:T(8,128)(2,1)} copy(bf16[16,6272]{1,0:T(8,128)(2,1)S(1)} %get-tuple-element.47.ck0.cv0) | data formatting | bytes 401408 | tf_op jit(solution)/shard_map/cond | solution.py:118
  70.5 0.0 copy-done
  70.5 0.0 copy-done.1
  70.5 1.2 %slice.64 = bf16[16,2]{0,1:T(2,128)(2,1)} slice(bf16[16,6272]{0,1:T(8,128)(2,1)} %copy.16), slice={[0:16], [6144:6146]} | slice | bytes 128 | tf_op jit(solution)/shard_map/slice | solution.py:119
  71.7 0.6 copy.17
  73.0 0.7 pad_maximum_fusion.8
  73.7 0.0 copy-done.5
  73.7 0.7 fusion
  74.4 0.2 select_reduce_fusion
  74.6 0.6 pad_add_fusion.table_ref
  75.2 0.0 collective-permute-done.8.k1.v1
  75.2 0.0 collective-permute-done.10.k3.v3
  75.2 9.4 %shard_map.100 = bf16[128,3072]{1,0:T(8,128)(2,1)} custom-call(s32[5]{0:T(128)} %pad_add_fusion.table_ref, bf16[128,3072]{1,0:T(8,128)(2,1)} %q_ref.1, bf16[2,128,3072]{2,1,0:T(8,128)(2,1)} %copy-done, bf16[2,128,3072]{2,1,0:T(8,128)(2,1)} %copy-done, bf16[2,128,3072]{2,1,0:T(8,128)(2,1)} %collective-permute-done.8.k1.v1, ...), custom_call_target="tpu_custom_call" | custom-call | flops 855638016 | bytes 8454144 | tf_op jit(solution)/shard_map/pallas_call | solution.py:75
  (5 shorter events, 0.0 us)
Async XLA Ops:
  1.3 1.1 %copy-start.2 = (bf16[128,3072]{1,0:T(8,128)(2,1)S(1)}, bf16[128,3072]{1,0:T(8,128)(2,1)}, u32[]{:S(2)}) copy-start(bf16[128,3072]{1,0:T(8,128)(2,1)} %param.18) | copy-start | bytes 2359300
  2.4 40.7 %copy-start.3 = (bf16[2,3072]{1,0:T(2,128)(2,1)S(1)}, bf16[2,3072]{1,0:T(2,128)(2,1)}, u32[]{:S(2)}) copy-start(bf16[2,3072]{1,0:T(2,128)(2,1)} %param.20) | copy-start | bytes 36868
  2.4 40.7 %copy-start.4 = (bf16[2,3072]{1,0:T(2,128)(2,1)S(1)}, bf16[2,3072]{1,0:T(2,128)(2,1)}, u32[]{:S(2)}) copy-start(bf16[2,3072]{1,0:T(2,128)(2,1)} %param.19) | copy-start | bytes 36868
  2.6 68.0 %copy-start = (bf16[2,128,3072]{2,1,0:T(8,128)(2,1)}, bf16[2,128,3072]{2,1,0:T(8,128)(2,1)S(1)}, u32[]{:S(2)}) copy-start(bf16[2,128,3072]{2,1,0:T(8,128)(2,1)S(1)} %pad_maximum_fusion.6.k0.v0) | copy-start | bytes 4718596
  2.6 38.5 %collective-permute-start.9 = (bf16[2,128,3072]{2,1,0:T(8,128)(2,1)S(1)}, bf16[2,128,3072]{2,1,0:T(8,128)(2,1)S(1)}, u32[]{:S(2)}, u32[]{:S(2)}) collective-permute-start(bf16[2,128,3072]{2,1,0:T(8,128)(2,1)S(1)} %pad_maximum_fusion.6.k0.v0), channel_id=1, source_target_pairs={{0,2},{1,3},{2,4},{3,5},{4,6},{5,7},{6,8},{7,9},{8,10},{9,11},{10,... | collective-permute-start | bytes 4718600 | tf_op jit(solution)/shard_map/ppermute | solution.py:113
  7.6 67.6 %collective-permute-start.8 = (bf16[2,128,3072]{2,1,0:T(8,128)(2,1)S(1)}, bf16[2,128,3072]{2,1,0:T(8,128)(2,1)}, u32[]{:S(2)}, u32[]{:S(2)}) collective-permute-start(bf16[2,128,3072]{2,1,0:T(8,128)(2,1)S(1)} %pad_maximum_fusion.6.k0.v0), channel_id=1, source_target_pairs={{0,1},{2,3},{4,5},{6,7},{8,9},{10,11},{12,13},{14,15},{1,4},{3,6},... | collective-permute-start | bytes 4718600 | tf_op jit(solution)/shard_map/ppermute | solution.py:114
  41.1 29.4 %copy-start.1 = (bf16[2,128,3072]{2,1,0:T(8,128)(2,1)}, bf16[2,128,3072]{2,1,0:T(8,128)(2,1)S(1)}, u32[]{:S(2)}) copy-start(bf16[2,128,3072]{2,1,0:T(8,128)(2,1)S(1)} %collective-permute-done.9.k2.v2) | copy-start | bytes 4718596
  41.1 34.1 %collective-permute-start.10 = (bf16[2,128,3072]{2,1,0:T(8,128)(2,1)S(1)}, bf16[2,128,3072]{2,1,0:T(8,128)(2,1)}, u32[]{:S(2)}, u32[]{:S(2)}) collective-permute-start(bf16[2,128,3072]{2,1,0:T(8,128)(2,1)S(1)} %collective-permute-done.9.k2.v2), channel_id=1, source_target_pairs={{0,1},{1,0},{2,3},{3,2},{4,5},{5,4},{6,7},{7,6},{8,9},{9,8},{10,11... | collective-permute-start | bytes 4718600 | tf_op jit(solution)/shard_map/ppermute | solution.py:116
  43.2 7.6 %collective-permute-start.4 = (bf16[2,6272]{1,0:T(2,128)(2,1)S(1)}, bf16[2,6272]{1,0:T(2,128)(2,1)S(1)}, u32[]{:S(2)}, u32[]{:S(2)}) collective-permute-start(bf16[2,6272]{1,0:T(2,128)(2,1)S(1)} %param.5), channel_id=1, source_target_pairs={{0,8},{1,9},{2,10},{3,11},{4,12},{5,13},{6,14},{7,15},{8,0},{9,1},... | collective-permute-start | bytes 75272 | tf_op jit(solution)/shard_map/cond/branch_1_fun/ppermute | solution.py:91
  50.8 4.2 %collective-permute-start.5 = (bf16[4,6272]{1,0:T(4,128)(2,1)S(1)}, bf16[4,6272]{1,0:T(4,128)(2,1)S(1)}, u32[]{:S(2)}, u32[]{:S(2)}) collective-permute-start(bf16[4,6272]{1,0:T(4,128)(2,1)S(1)} %pad_maximum_fusion.5), channel_id=1, source_target_pairs={{0,4},{1,5},{2,6},{3,7},{4,0},{5,1},{6,2},{7,3},{8,12},{9,13},{10,... | collective-permute-start | bytes 150536 | tf_op jit(solution)/shard_map/cond/branch_1_fun/ppermute | solution.py:91
  55.1 4.7 %collective-permute-start.6 = (bf16[8,6272]{1,0:T(8,128)(2,1)S(1)}, bf16[8,6272]{1,0:T(8,128)(2,1)S(1)}, u32[]{:S(2)}, u32[]{:S(2)}) collective-permute-start(bf16[8,6272]{1,0:T(8,128)(2,1)S(1)} %pad_maximum_fusion.4), channel_id=1, source_target_pairs={{0,2},{1,3},{2,0},{3,1},{4,6},{5,7},{6,4},{7,5},{8,10},{9,11},{10,... | collective-permute-start | bytes 301064 | tf_op jit(solution)/shard_map/cond/branch_1_fun/ppermute | solution.py:91
  60.6 7.3 %collective-permute-start.7 = (bf16[16,6272]{1,0:T(8,128)(2,1)}, bf16[16,6272]{1,0:T(8,128)(2,1)}, u32[]{:S(2)}, u32[]{:S(2)}) collective-permute-start(bf16[16,6272]{1,0:T(8,128)(2,1)} %pad_maximum_fusion.3), channel_id=1, source_target_pairs={{0,1},{1,0},{2,3},{3,2},{4,5},{5,4},{6,7},{7,6},{8,9},{9,8},{10,11... | collective-permute-start | bytes 602120 | tf_op jit(solution)/shard_map/cond/branch_1_fun/ppermute | solution.py:94
  68.8 4.9 %copy-start.5 = (s32[3]{0:T(128)S(1)}, s32[3]{0:T(128)}, u32[]{:S(2)}) copy-start(s32[3]{0:T(128)} %constant.75.clone) | copy-start | bytes 40

commit v8 on v5

--- a/solution.py
+++ b/solution.py
@@ -53,8 +53,8 @@
     cache_rows = cache.shape[0]
     levels = gate_table.shape[0]
     row_block = pl.BlockSpec((rows, width), lambda h, t: (0, h))
-    k_block = pl.BlockSpec((None, rows, width), lambda h, t: (0, 0, h))
-    v_block = pl.BlockSpec((None, rows, width), lambda h, t: (1, 0, h))
+    k_block = pl.BlockSpec((rows, width), lambda h, t: (0, h))
+    v_block = pl.BlockSpec((rows, width), lambda h, t: (1, h))
     cache_k_block = pl.BlockSpec((cache_rows, width), lambda h, t: (0, h))
     cache_v_block = pl.BlockSpec((cache_rows, width), lambda h, t: (0, steps + h))
     gate_block = pl.BlockSpec((levels, width), lambda h, t: (0, h))
@@ -79,16 +79,15 @@
     )(table, queries, kv_own, kv_own, kv_a, kv_a, kv_b, kv_b, kv_c, kv_c, cache, cache, gate_table)
 
 
-def gather_pieces(piece, size):
-    if size & (size - 1):
-        return lax.all_gather(piece, "group", axis=0, tiled=True)
-    held = piece
-    step = size // 2
-    while step >= 1:
-        other = lax.ppermute(held, "group", [(i, i ^ step) for i in range(size)])
+def shift_gather(held, size, shifts):
+    for step in shifts:
+        other = lax.ppermute(held, "group", [(i, (i + step) % size) for i in range(size)])
         held = jnp.concatenate([held, other], 0)
-        step //= 2
     return held
+
+
+def keys_by_head_of(keys, rows, heads):
+    return keys.reshape(rows, heads, HEAD_DIM).transpose(2, 1, 0).reshape(HEAD_DIM, heads * rows)
 
 
 def body(queries, fresh_keys, fresh_values, cache_keys, cache_values, lengths, levels, gate_table):
@@ -100,26 +99,33 @@
     tag = jnp.zeros((cache_rows, HEAD_DIM), jnp.bfloat16)
     tag = tag.at[0, 0].set(lengths[0].astype(jnp.bfloat16)).at[0, 1].set(me.astype(jnp.bfloat16))
     packed = jnp.concatenate([cache_keys, cache_values, tag], 1)
-    gathered = gather_pieces(packed, size)
+    head_count = feat_width // HEAD_DIM
+    keys_by_head = keys_by_head_of(fresh_keys, row_count, head_count)
+    piece_size = packed.size
+    piece_rows = -(-piece_size // feat_width)
+    piece_rows = -(-piece_rows // 8) * 8
+    flat_piece = jnp.pad(packed.reshape(-1), (0, piece_rows * feat_width - piece_size)).reshape(piece_rows, feat_width)
+    carrier = jnp.concatenate([keys_by_head, fresh_values, flat_piece], 0)
+    pairs_two = [(i, (i + 2) % size) for i in range(size)]
+    pairs_mixed = [(i, i + 1) for i in range(0, size - 1, 2)] + [(i, i + 3) for i in range(1, size - 3, 2)]
+    from_two = lax.ppermute(carrier, "group", pairs_two)
+    from_mixed = lax.ppermute(carrier, "group", pairs_mixed)
+    from_two, from_mixed = lax.optimization_barrier((from_two, from_mixed))
+    pairs_swap = [(i, i ^ 1) for i in range(size)]
+    from_swap = lax.ppermute(from_two, "group", pairs_swap)
+
+    piece_two = from_two[2 * row_count:].reshape(-1)[:piece_size].reshape(packed.shape)
+    shifts = [1] + [1 << k for k in range(2, size.bit_length() - 1)]
+    gathered = shift_gather(jnp.concatenate([packed, piece_two], 0), size, shifts)
     piece_lengths = gathered[:, 2 * feat_width].astype(jnp.int32)
     piece_index = gathered[:, 2 * feat_width + 1].astype(jnp.int32)
-
-    head_count = feat_width // HEAD_DIM
-    keys_by_head = fresh_keys.reshape(row_count, head_count, HEAD_DIM).transpose(2, 1, 0).reshape(HEAD_DIM, head_count * row_count)
-    kv = jnp.stack([keys_by_head, fresh_values], 0)
-    pairs_two = [(i, i + 2) for i in range(size - 2)]
-    pairs_mixed = [(i, i + 1) for i in range(0, size - 1, 2)] + [(i, i + 3) for i in range(1, size - 3, 2)]
-    from_two = lax.ppermute(kv, "group", pairs_two)
-    from_mixed = lax.ppermute(kv, "group", pairs_mixed)
-    pairs_swap = [(i, i ^ 1) for i in range(size)]
-    from_swap = lax.ppermute(from_two, "group", pairs_swap)
 
     odd = (me % 2) == 1
     offsets = jnp.where(odd, jnp.array([1, 2, 3], jnp.int32), jnp.array([3, 2, 1], jnp.int32))
     sources = me - offsets
     previous = jnp.sum(jnp.where(piece_index[None, :] == sources[:, None], piece_lengths[None, :], 0), axis=1)
     table = jnp.concatenate([lengths[:1], previous, levels[:1]]).astype(jnp.int32)
-    return attend(table, queries, kv, from_mixed, from_two, from_swap, gathered, gate_table)
+    return attend(table, queries, carrier, from_mixed, from_two, from_swap, gathered, gate_table)
 
 
 def solution(mesh):

time: 76 us -> 99.7 us (1.31)
  the two profiles are of different devices: /device:TPU:15 before, /device:TPU:0 now
where the time goes in v8:
time: 99.7 us; the launch traced here: 99.2 us
  waiting for transfers between devices  57.1 us (57%)
  starting transfers between devices  18.9 us (19%)
  Pallas kernels  9.33 us (9%)
  local copies, waits for them, and re-layouts  8.82 us (9%)
  other arithmetic  3.46 us (3%)
  between operations  1.48 us (1%)
    ppermute x1, waiting for transfers between devices, body(): from_two = lax.ppermute(carrier, 'group', pairs_two)  36.7 us
    ppermute x3, waiting for transfers between devices, shift_gather(): lax.ppermute(held, 'group', [(i, (i + step) % size) for i in range(size)])  19.8 us
    ppermute x3, starting transfers between devices, shift_gather(): lax.ppermute(held, 'group', [(i, (i + step) % size) for i in range(size)])  14 us
    pallas_call x1, Pallas kernels, attend(): pl.pallas_call(functools.partial(attention_kernel, heads=HEADS_PER_STEP),...  9.33 us
    concatenate x1, local copies, waits for them, and re-layouts, shift_gather(): held = jnp.concatenate([held, other], 0)  2.99 us
    unnamed x21, local copies, waits for them, and re-layouts  2.95 us
    ppermute x1, starting transfers between devices, body(): from_mixed = lax.ppermute(carrier, 'group', pairs_mixed)  2.5 us
    ppermute x1, starting transfers between devices, body(): from_two = lax.ppermute(carrier, 'group', pairs_two)  2.36 us
  transfers between devices with their start and end apart: 6, of which 5 were waited for; matrix products, arithmetic and copies ran while one was open for 6% of the time, Pallas kernels for 0%

profile of v8, /device:TPU:0, one launch (start us, length us, event | category | flops | bytes accessed | tf_op | source)
XLA Modules:
  0.0 99.2 jit_solution(15801762049589741929)
XLA Ops:
  0.7 0.7 fusion.1
  1.3 1.4 %scatter.9 = bf16[2,128]{1,0:T(2,128)(2,1)S(1)} dynamic-update-slice(bf16[2,128]{1,0:T(2,128)(2,1)S(1)} %scatter.6, bf16[1,1]{1,0:T(2,128)(2,1)} %bitcast.1, s32[]{:T(128)} %bitcast.2, s32[]{:T(128)} %bitcast.3) | dynamic-update-slice | bytes 8 | tf_op jit(solution)/shard_map/scatter | solution.py:100
  2.8 0.8 pad_maximum_fusion.3
  3.5 0.1 reshape.103
  3.6 1.3 %copy.14 = bf16[16,8,24,128]{3,2,1,0:T(8,128)(2,1)S(1)} copy(bf16[16,8,24,128]{3,1,2,0:T(8,128)(2,1)} %bitcast.15) | data formatting | bytes 1572864
  4.9 0.0 copy-start.3
  4.9 0.7 copy.13
  5.6 0.0 copy-start.4
  5.6 0.0 copy-start.5
  5.6 0.1 bitcast_dynamic-update-slice_fusion
  5.7 0.3 copy-done.3
  6.0 0.0 copy-start.6
  6.0 0.0 copy-start.7
  6.0 0.1 constant_dynamic-update-slice_fusion.1
  6.1 0.0 copy-start
  6.1 2.5 %collective-permute-start.1 = (bf16[264,3072]{1,0:T(8,128)(2,1)S(1)}, bf16[264,3072]{1,0:T(8,128)(2,1)S(1)}, u32[]{:S(2)}, u32[]{:S(2)}) collective-permute-start(bf16[264,3072]{1,0:T(8,128)(2,1)S(1)} %constant_dynamic-update-slice_fusion.k0.v0), channel_id=1, source_target_pairs={{0,1},{2,3},{4,5},{6,7},{8,9},{10,11},{12,13},{14,15},{1,4},{3,6},... | collective-permute-start | bytes 4866056 | tf_op jit(solution)/shard_map/ppermute | solution.py:112
  8.6 2.4 %collective-permute-start = (bf16[264,3072]{1,0:T(8,128)(2,1)S(1)}, bf16[264,3072]{1,0:T(8,128)(2,1)S(1)}, u32[]{:S(2)}, u32[]{:S(2)}) collective-permute-start(bf16[264,3072]{1,0:T(8,128)(2,1)S(1)} %constant_dynamic-update-slice_fusion.k0.v0), channel_id=1, source_target_pairs={{0,2},{1,3},{2,4},{3,5},{4,6},{5,7},{6,8},{7,9},{8,10},{9,11},{10,... | collective-permute-start | bytes 4866056 | tf_op jit(solution)/shard_map/ppermute | solution.py:111
  11.0 0.6 collective-permute-done.1.k1.v1
  11.6 0.0 copy-start.2
  11.6 1.2 %copy-done.2 = bf16[264,3072]{1,0:T(8,128)(2,1)} copy-done((bf16[264,3072]{1,0:T(8,128)(2,1)}, bf16[264,3072]{1,0:T(8,128)(2,1)S(1)}, u32[]{:S(2)}) %copy-start.2) | copy-done | bytes 1622040
  12.8 36.7 %collective-permute-done.k2.v2 = bf16[264,3072]{1,0:T(8,128)(2,1)S(1)} collective-permute-done((bf16[264,3072]{1,0:T(8,128)(2,1)S(1)}, bf16[264,3072]{1,0:T(8,128)(2,1)S(1)}, u32[]{:S(2)}, u32[]{:S(2)}) %collective-permute-start) | collective-permute-done | bytes 1622048 | tf_op jit(solution)/shard_map/ppermute | solution.py:111
  49.5 0.0 copy-start.1
  49.6 0.0 copy-done.4
  49.6 0.0 copy-done.5
  49.6 0.1 pad_maximum_fusion.2
  49.7 0.8 collective-permute-start.2
  50.4 0.1 collective-permute-start.5
  50.5 5.4 %collective-permute-done.2 = bf16[4,6272]{1,0:T(4,128)(2,1)S(1)} collective-permute-done((bf16[4,6272]{1,0:T(4,128)(2,1)S(1)}, bf16[4,6272]{1,0:T(4,128)(2,1)S(1)}, u32[]{:S(2)}, u32[]{:S(2)}) %collective-permute-start.2) | collective-permute-done | bytes 50208 | tf_op jit(solution)/shard_map/ppermute | solution.py:84
  55.9 0.7 pad_maximum_fusion.1
  56.7 12.4 %collective-permute-start.3 = (bf16[8,6272]{1,0:T(8,128)(2,1)}, bf16[8,6272]{1,0:T(8,128)(2,1)S(1)}, u32[]{:S(2)}, u32[]{:S(2)}) collective-permute-start(bf16[8,6272]{1,0:T(8,128)(2,1)} %pad_maximum_fusion.1), channel_id=1, source_target_pairs={{0,4},{1,5},{2,6},{3,7},{4,8},{5,9},{6,10},{7,11},{8,12},{9,13},{1... | collective-permute-start | bytes 301064 | tf_op jit(solution)/shard_map/ppermute | solution.py:84
  69.8 4.6 %collective-permute-done.3 = bf16[8,6272]{1,0:T(8,128)(2,1)S(1)} collective-permute-done((bf16[8,6272]{1,0:T(8,128)(2,1)}, bf16[8,6272]{1,0:T(8,128)(2,1)S(1)}, u32[]{:S(2)}, u32[]{:S(2)}) %collective-permute-start.3) | collective-permute-done | bytes 100384 | tf_op jit(solution)/shard_map/ppermute | solution.py:84
  74.4 0.1 pad_maximum_fusion
  74.5 0.8 collective-permute-start.4
  75.3 0.0 copy-done.6
  75.3 0.0 copy-done.7
  75.3 9.8 %collective-permute-done.4 = bf16[16,6272]{1,0:T(8,128)(2,1)} collective-permute-done((bf16[16,6272]{1,0:T(8,128)(2,1)S(1)}, bf16[16,6272]{1,0:T(8,128)(2,1)}, u32[]{:S(2)}, u32[]{:S(2)}) %collective-permute-start.4) | collective-permute-done | bytes 200736 | tf_op jit(solution)/shard_map/ppermute | solution.py:84
  85.1 3.0 %concatenate.33.ck.cv = bf16[32,6272]{1,0:T(8,128)(2,1)} concatenate(bf16[2,6272]{1,0:T(2,128)(2,1)S(1)} %pad_maximum_fusion.3, bf16[2,6272]{1,0:T(2,128)(2,1)S(1)} %reshape.106, bf16[4,6272]{1,0:T(4,128)(2,1)S(1)} %collective-permute-done.2, bf16[8,6272]{1,0:T(8,128)(2,1)S(1)} %collective-permute-done.3, bf16[16,6272]{1,0:T(8,128)(2,1)} %collective-permute-done.4), dimensions={0} | concatenate | bytes 802816 | tf_op jit(solution)/shard_map/concatenate | solution.py:85
  88.0 1.0 convert_reduce_fusion.1
  89.0 0.2 select_reduce_fusion
  89.2 0.6 pad_add_fusion.table_ref
  89.8 0.0 collective-permute-done.5.k3.v3
  89.8 0.0 copy-done
  89.8 0.0 copy-done.1
  89.8 9.3 %shard_map.100 = bf16[128,3072]{1,0:T(8,128)(2,1)} custom-call(s32[5]{0:T(128)} %pad_add_fusion.table_ref, bf16[128,3072]{1,0:T(8,128)(2,1)} %q_ref.1, bf16[264,3072]{1,0:T(8,128)(2,1)} %copy-done, bf16[264,3072]{1,0:T(8,128)(2,1)} %copy-done, bf16[264,3072]{1,0:T(8,128)(2,1)} %copy-done.2, bf16[264,3072]{1,0:T(8,128)(2,1)} %copy-done.2, ...), custom_call_target="tpu_custom_call" | custom-call | flops 855638016 | bytes 8454144 | tf_op jit(solution)/shard_map/pallas_call | solution.py:74
  (10 shorter events, 0.1 us)
Async XLA Ops:
  4.9 1.1 %copy-start.3 = (bf16[128,3072]{1,0:T(8,128)(2,1)S(1)}, bf16[128,3072]{1,0:T(8,128)(2,1)}, u32[]{:S(2)}) copy-start(bf16[128,3072]{1,0:T(8,128)(2,1)} %param.16) | copy-start | bytes 2359300
  5.6 44.0 %copy-start.4 = (bf16[2,3072]{1,0:T(2,128)(2,1)S(1)}, bf16[2,3072]{1,0:T(2,128)(2,1)}, u32[]{:S(2)}) copy-start(bf16[2,3072]{1,0:T(2,128)(2,1)} %param.18) | copy-start | bytes 36868
  5.6 44.0 %copy-start.5 = (bf16[2,3072]{1,0:T(2,128)(2,1)S(1)}, bf16[2,3072]{1,0:T(2,128)(2,1)}, u32[]{:S(2)}) copy-start(bf16[2,3072]{1,0:T(2,128)(2,1)} %param.17) | copy-start | bytes 36868
  6.0 69.3 %copy-start.6 = (s32[3]{0:T(128)S(1)}, s32[3]{0:T(128)}, u32[]{:S(2)}) copy-start(s32[3]{0:T(128)} %constant.77.clone) | copy-start | bytes 40
  6.0 69.3 %copy-start.7 = (s32[3]{0:T(128)S(1)}, s32[3]{0:T(128)}, u32[]{:S(2)}) copy-start(s32[3]{0:T(128)} %constant.76.clone) | copy-start | bytes 40
  6.1 83.7 %copy-start = (bf16[264,3072]{1,0:T(8,128)(2,1)}, bf16[264,3072]{1,0:T(8,128)(2,1)S(1)}, u32[]{:S(2)}) copy-start(bf16[264,3072]{1,0:T(8,128)(2,1)S(1)} %constant_dynamic-update-slice_fusion.k0.v0) | copy-start | bytes 4866052
  6.1 5.5 %collective-permute-start.1 = (bf16[264,3072]{1,0:T(8,128)(2,1)S(1)}, bf16[264,3072]{1,0:T(8,128)(2,1)S(1)}, u32[]{:S(2)}, u32[]{:S(2)}) collective-permute-start(bf16[264,3072]{1,0:T(8,128)(2,1)S(1)} %constant_dynamic-update-slice_fusion.k0.v0), channel_id=1, source_target_pairs={{0,1},{2,3},{4,5},{6,7},{8,9},{10,11},{12,13},{14,15},{1,4},{3,6},... | collective-permute-start | bytes 4866056 | tf_op jit(solution)/shard_map/ppermute | solution.py:112
  8.6 40.9 %collective-permute-start = (bf16[264,3072]{1,0:T(8,128)(2,1)S(1)}, bf16[264,3072]{1,0:T(8,128)(2,1)S(1)}, u32[]{:S(2)}, u32[]{:S(2)}) collective-permute-start(bf16[264,3072]{1,0:T(8,128)(2,1)S(1)} %constant_dynamic-update-slice_fusion.k0.v0), channel_id=1, source_target_pairs={{0,2},{1,3},{2,4},{3,5},{4,6},{5,7},{6,8},{7,9},{8,10},{9,11},{10,... | collective-permute-start | bytes 4866056 | tf_op jit(solution)/shard_map/ppermute | solution.py:111
  11.6 1.2 %copy-start.2 = (bf16[264,3072]{1,0:T(8,128)(2,1)}, bf16[264,3072]{1,0:T(8,128)(2,1)S(1)}, u32[]{:S(2)}) copy-start(bf16[264,3072]{1,0:T(8,128)(2,1)S(1)} %collective-permute-done.1.k1.v1) | copy-start | bytes 4866052
  49.5 40.3 %copy-start.1 = (bf16[264,3072]{1,0:T(8,128)(2,1)}, bf16[264,3072]{1,0:T(8,128)(2,1)S(1)}, u32[]{:S(2)}) copy-start(bf16[264,3072]{1,0:T(8,128)(2,1)S(1)} %collective-permute-done.k2.v2) | copy-start | bytes 4866052
  49.7 6.3 %collective-permute-start.2 = (bf16[4,6272]{1,0:T(4,128)(2,1)S(1)}, bf16[4,6272]{1,0:T(4,128)(2,1)S(1)}, u32[]{:S(2)}, u32[]{:S(2)}) collective-permute-start(bf16[4,6272]{1,0:T(4,128)(2,1)S(1)} %pad_maximum_fusion.2), channel_id=1, source_target_pairs={{0,1},{1,2},{2,3},{3,4},{4,5},{5,6},{6,7},{7,8},{8,9},{9,10},{10,1... | collective-permute-start | bytes 150536 | tf_op jit(solution)/shard_map/ppermute | solution.py:84
  50.4 39.4 %collective-permute-start.5 = (bf16[264,3072]{1,0:T(8,128)(2,1)S(1)}, bf16[264,3072]{1,0:T(8,128)(2,1)}, u32[]{:S(2)}, u32[]{:S(2)}) collective-permute-start(bf16[264,3072]{1,0:T(8,128)(2,1)S(1)} %collective-permute-done.k2.v2), channel_id=1, source_target_pairs={{0,1},{1,0},{2,3},{3,2},{4,5},{5,4},{6,7},{7,6},{8,9},{9,8},{10,11... | collective-permute-start | bytes 4866056 | tf_op jit(solution)/shard_map/ppermute | solution.py:115
  56.7 17.7 %collective-permute-start.3 = (bf16[8,6272]{1,0:T(8,128)(2,1)}, bf16[8,6272]{1,0:T(8,128)(2,1)S(1)}, u32[]{:S(2)}, u32[]{:S(2)}) collective-permute-start(bf16[8,6272]{1,0:T(8,128)(2,1)} %pad_maximum_fusion.1), channel_id=1, source_target_pairs={{0,4},{1,5},{2,6},{3,7},{4,8},{5,9},{6,10},{7,11},{8,12},{9,13},{1... | collective-permute-start | bytes 301064 | tf_op jit(solution)/shard_map/ppermute | solution.py:84
  74.5 10.6 %collective-permute-start.4 = (bf16[16,6272]{1,0:T(8,128)(2,1)S(1)}, bf16[16,6272]{1,0:T(8,128)(2,1)}, u32[]{:S(2)}, u32[]{:S(2)}) collective-permute-start(bf16[16,6272]{1,0:T(8,128)(2,1)S(1)} %pad_maximum_fusion), channel_id=1, source_target_pairs={{0,8},{1,9},{2,10},{3,11},{4,12},{5,13},{6,14},{7,15},{8,0},{9,1},... | collective-permute-start | bytes 602120 | tf_op jit(solution)/shard_map/ppermute | solution.py:84

commit v9 on v5

--- a/solution.py
+++ b/solution.py
@@ -83,11 +83,11 @@
     if size & (size - 1):
         return lax.all_gather(piece, "group", axis=0, tiled=True)
     held = piece
-    step = size // 2
-    while step >= 1:
+    step = 1
+    while step < size:
         other = lax.ppermute(held, "group", [(i, i ^ step) for i in range(size)])
         held = jnp.concatenate([held, other], 0)
-        step //= 2
+        step *= 2
     return held
 
 

time: 76 us -> 84 us (1.11)
  waiting for transfers between devices: 39.3 us -> 47.2 us
    ppermute x1, waiting for transfers between devices: 0.01 us -> 23.7 us  [body(): from_two = lax.ppermute(kv, 'group', pairs_two)]
    ppermute x4, waiting for transfers between devices: 34.6 us -> 23.4 us  [gather_pieces(): other = lax.ppermute(held, 'group', [(i, i ^ step) for i in range(size)])]
    ppermute x1, waiting for transfers between devices: 4.68 us -> 0.01 us  [body(): from_mixed = lax.ppermute(kv, 'group', pairs_mixed)]
    ppermute x1, starting transfers between devices: 7.45 us -> 3.71 us  [body(): from_mixed = lax.ppermute(kv, 'group', pairs_mixed)]
    ppermute x1, starting transfers between devices: 0.07 us -> 2.07 us  [body(): from_swap = lax.ppermute(from_two, 'group', pairs_swap)]
    ppermute x4, starting transfers between devices: 1.95 us -> 3.83 us  [gather_pieces(): other = lax.ppermute(held, 'group', [(i, i ^ step) for i in range(size)])]
  transfers between devices with their start and end apart: 7 -> 7, of which waited for: 4 -> 4; matrix products, arithmetic and copies ran while one was open for 12% -> 11% of each run, Pallas kernels for 0% -> 0%
where the time goes in v9:
time: 84 us; the launch traced here: 82.5 us
  waiting for transfers between devices  47.2 us (56%)
  starting transfers between devices  12.8 us (15%)
  Pallas kernels  9.33 us (11%)
  local copies, waits for them, and re-layouts  7.2 us (9%)
  other arithmetic  4.55 us (5%)
  between operations  1.47 us (2%)
    ppermute x1, waiting for transfers between devices, body(): from_two = lax.ppermute(kv, 'group', pairs_two)  23.7 us
    ppermute x4, waiting for transfers between devices, gather_pieces(): other = lax.ppermute(held, 'group', [(i, i ^ step) for i in range(size)])  23.4 us
    pallas_call x1, Pallas kernels, attend(): pl.pallas_call(functools.partial(attention_kernel, heads=HEADS_PER_STEP),...  9.33 us
    ppermute x4, starting transfers between devices, gather_pieces(): other = lax.ppermute(held, 'group', [(i, i ^ step) for i in range(size)])  3.83 us
    ppermute x1, starting transfers between devices, body(): from_mixed = lax.ppermute(kv, 'group', pairs_mixed)  3.71 us
    ppermute x1, starting transfers between devices, body(): from_two = lax.ppermute(kv, 'group', pairs_two)  3.18 us
    concatenate x1, local copies, waits for them, and re-layouts, gather_pieces(): held = jnp.concatenate([held, other], 0)  2.79 us
    concatenate x3, other arithmetic, gather_pieces(): held = jnp.concatenate([held, other], 0)  2.75 us
  transfers between devices with their start and end apart: 7, of which 4 were waited for; matrix products, arithmetic and copies ran while one was open for 11% of the time, Pallas kernels for 0%

profile of v9, /device:TPU:15, one launch (start us, length us, event | category | flops | bytes accessed | tf_op | source)
XLA Modules:
  0.0 82.5 jit_solution(2788942378961550401)
XLA Ops:
  0.0 1.3 %copy.14 = bf16[16,8,24,128]{3,2,1,0:T(8,128)(2,1)S(1)} copy(bf16[16,8,24,128]{3,1,2,0:T(8,128)(2,1)} %bitcast.10) | data formatting | bytes 1572864
  1.3 0.0 copy-start.3
  1.3 0.7 copy.13
  2.0 0.3 stack_reshape.3
  2.3 0.1 copy-done.3
  2.4 0.0 copy-start.4
  2.4 0.0 copy-start.5
  2.4 0.0 copy-start.6
  2.4 0.0 copy-start.7
  2.4 0.1 pad_maximum_fusion.k0.v0
  2.6 0.0 copy-start
  2.6 3.2 %collective-permute-start.5 = (bf16[2,128,3072]{2,1,0:T(8,128)(2,1)S(1)}, bf16[2,128,3072]{2,1,0:T(8,128)(2,1)S(1)}, u32[]{:S(2)}, u32[]{:S(2)}) collective-permute-start(bf16[2,128,3072]{2,1,0:T(8,128)(2,1)S(1)} %pad_maximum_fusion.k0.v0), channel_id=1, source_target_pairs={{0,2},{1,3},{2,4},{3,5},{4,6},{5,7},{6,8},{7,9},{8,10},{9,11},{10,... | collective-permute-start | bytes 4718600 | tf_op jit(solution)/shard_map/ppermute | solution.py:112
  6.5 0.6 fusion.1
  7.1 1.3 %scatter.9 = bf16[2,128]{1,0:T(2,128)(2,1)S(1)} dynamic-update-slice(bf16[2,128]{1,0:T(2,128)(2,1)S(1)} %scatter.6, bf16[1,1]{1,0:T(2,128)(2,1)} %bitcast.1, s32[]{:T(128)} %bitcast.2, s32[]{:T(128)} %bitcast.3) | dynamic-update-slice | bytes 8 | tf_op jit(solution)/shard_map/scatter | solution.py:101
  8.5 0.0 copy-done.4
  8.5 0.0 copy-done.5
  8.5 0.6 pad_maximum_fusion.4
  9.1 1.0 %collective-permute-start = (bf16[2,6272]{1,0:T(2,128)(2,1)}, bf16[2,6272]{1,0:T(2,128)(2,1)}, u32[]{:S(2)}, u32[]{:S(2)}) collective-permute-start(bf16[2,6272]{1,0:T(2,128)(2,1)} %pad_maximum_fusion.4), channel_id=1, source_target_pairs={{0,1},{1,0},{2,3},{3,2},{4,5},{5,4},{6,7},{7,6},{8,9},{9,8},{10,11... | collective-permute-start | bytes 75272 | tf_op jit(solution)/shard_map/ppermute | solution.py:88
  10.1 1.2 %collective-permute-done = bf16[2,6272]{1,0:T(2,128)(2,1)} collective-permute-done((bf16[2,6272]{1,0:T(2,128)(2,1)}, bf16[2,6272]{1,0:T(2,128)(2,1)}, u32[]{:S(2)}, u32[]{:S(2)}) %collective-permute-start) | collective-permute-done | bytes 25120 | tf_op jit(solution)/shard_map/ppermute | solution.py:88
  11.3 0.8 pad_maximum_fusion.3
  12.1 0.3 collective-permute-start.1
  12.3 3.7 %collective-permute-start.4 = (bf16[2,128,3072]{2,1,0:T(8,128)(2,1)S(1)}, bf16[2,128,3072]{2,1,0:T(8,128)(2,1)}, u32[]{:S(2)}, u32[]{:S(2)}) collective-permute-start(bf16[2,128,3072]{2,1,0:T(8,128)(2,1)S(1)} %pad_maximum_fusion.k0.v0), channel_id=1, source_target_pairs={{0,1},{2,3},{4,5},{6,7},{8,9},{10,11},{12,13},{14,15},{1,4},{3,6},... | collective-permute-start | bytes 4718600 | tf_op jit(solution)/shard_map/ppermute | solution.py:113
  16.0 23.7 %collective-permute-done.5.k2.v2 = bf16[2,128,3072]{2,1,0:T(8,128)(2,1)S(1)} collective-permute-done((bf16[2,128,3072]{2,1,0:T(8,128)(2,1)S(1)}, bf16[2,128,3072]{2,1,0:T(8,128)(2,1)S(1)}, u32[]{:S(2)}, u32[]{:S(2)}) %collective-permute-start.5) | collective-permute-done | bytes 1572896 | tf_op jit(solution)/shard_map/ppermute | solution.py:112
  39.8 0.0 copy-start.1
  39.8 2.1 %collective-permute-start.6 = (bf16[2,128,3072]{2,1,0:T(8,128)(2,1)S(1)}, bf16[2,128,3072]{2,1,0:T(8,128)(2,1)}, u32[]{:S(2)}, u32[]{:S(2)}) collective-permute-start(bf16[2,128,3072]{2,1,0:T(8,128)(2,1)S(1)} %collective-permute-done.5.k2.v2), channel_id=1, source_target_pairs={{0,1},{1,0},{2,3},{3,2},{4,5},{5,4},{6,7},{7,6},{8,9},{9,8},{10,11... | collective-permute-start | bytes 4718600 | tf_op jit(solution)/shard_map/ppermute | solution.py:115
  41.8 0.0 collective-permute-done.1
  41.8 0.9 %pad_maximum_fusion.2 = bf16[8,6272]{1,0:T(8,128)(2,1)S(1)} fusion(bf16[4,6272]{1,0:T(4,128)(2,1)} %collective-permute-done.1, bf16[2,6272]{1,0:T(2,128)(2,1)} %collective-permute-done, bf16[2,128]{1,0:T(2,128)(2,1)S(1)} %scatter.9, bf16[2,3072]{1,0:T(2,128)(2,1)S(1)} %copy-done.4, bf16[2,3072]{1,0:T(2,128)(2,1)S(1)} %copy-done.5), kind=kLoop, calls=%fused_computation.2 | loop fusion | flops 501760 | bytes 200704 | tf_op jit(solution)/shard_map/concatenate | solution.py:89
  42.7 0.2 collective-permute-start.2
  43.6 18.3 %collective-permute-done.2 = bf16[8,6272]{1,0:T(8,128)(2,1)} collective-permute-done((bf16[8,6272]{1,0:T(8,128)(2,1)S(1)}, bf16[8,6272]{1,0:T(8,128)(2,1)}, u32[]{:S(2)}, u32[]{:S(2)}) %collective-permute-start.2) | collective-permute-done | bytes 100384 | tf_op jit(solution)/shard_map/ppermute | solution.py:88
  61.9 1.1 %pad_maximum_fusion.1 = bf16[16,6272]{1,0:T(8,128)(2,1)S(1)} fusion(bf16[8,6272]{1,0:T(8,128)(2,1)} %collective-permute-done.2, bf16[4,6272]{1,0:T(4,128)(2,1)} %collective-permute-done.1, bf16[2,6272]{1,0:T(2,128)(2,1)} %collective-permute-done, bf16[2,128]{1,0:T(2,128)(2,1)S(1)} %scatter.9, bf16[2,3072]{1,0:T(2,128)(2,1)S(1)} %copy-done.4, ...), kind=kLoop, calls=%fused_computation.1 | loop fusion | flops 1204224 | bytes 401408 | tf_op jit(solution)/shard_map/concatenate | solution.py:89
  63.0 2.4 %collective-permute-start.3 = (bf16[16,6272]{1,0:T(8,128)(2,1)S(1)}, bf16[16,6272]{1,0:T(8,128)(2,1)}, u32[]{:S(2)}, u32[]{:S(2)}) collective-permute-start(bf16[16,6272]{1,0:T(8,128)(2,1)S(1)} %pad_maximum_fusion.1), channel_id=1, source_target_pairs={{0,8},{1,9},{2,10},{3,11},{4,12},{5,13},{6,14},{7,15},{8,0},{9,1},... | collective-permute-start | bytes 602120 | tf_op jit(solution)/shard_map/ppermute | solution.py:88
  65.3 0.0 copy-done.6
  65.3 0.0 copy-done.7
  65.3 4.0 %collective-permute-done.3 = bf16[16,6272]{1,0:T(8,128)(2,1)} collective-permute-done((bf16[16,6272]{1,0:T(8,128)(2,1)S(1)}, bf16[16,6272]{1,0:T(8,128)(2,1)}, u32[]{:S(2)}, u32[]{:S(2)}) %collective-permute-start.3) | collective-permute-done | bytes 200736 | tf_op jit(solution)/shard_map/ppermute | solution.py:88
  69.3 2.8 %concatenate.29.ck.cv = bf16[32,6272]{1,0:T(8,128)(2,1)S(1)} concatenate(bf16[2,6272]{1,0:T(2,128)(2,1)} %pad_maximum_fusion.4, bf16[2,6272]{1,0:T(2,128)(2,1)} %collective-permute-done, bf16[4,6272]{1,0:T(4,128)(2,1)} %collective-permute-done.1, bf16[8,6272]{1,0:T(8,128)(2,1)} %collective-permute-done.2, bf16[16,6272]{1,0:T(8,128)(2,1)} %collective-permute-done.3), dimensions={0} | concatenate | bytes 802816 | tf_op jit(solution)/shard_map/concatenate | solution.py:89
  72.1 0.0 copy-start.2
  72.1 0.2 convert_reduce_fusion.1
  72.3 0.2 select_reduce_fusion
  72.5 0.7 pad_add_fusion.table_ref
  73.1 0.0 collective-permute-done.4.k1.v1
  73.1 0.0 collective-permute-done.6.k3.v3
  73.1 0.0 copy-done
  73.2 0.0 copy-done.1
  73.2 0.0 copy-done.2
  73.2 9.3 %shard_map.100 = bf16[128,3072]{1,0:T(8,128)(2,1)} custom-call(s32[5]{0:T(128)} %pad_add_fusion.table_ref, bf16[128,3072]{1,0:T(8,128)(2,1)} %q_ref.1, bf16[2,128,3072]{2,1,0:T(8,128)(2,1)} %copy-done, bf16[2,128,3072]{2,1,0:T(8,128)(2,1)} %copy-done, bf16[2,128,3072]{2,1,0:T(8,128)(2,1)} %collective-permute-done.4.k1.v1, ...), custom_call_target="tpu_custom_call" | custom-call | flops 855638016 | bytes 8454144 | tf_op jit(solution)/shard_map/pallas_call | solution.py:74
  (3 shorter events, 0.0 us)
Async XLA Ops:
  1.3 1.1 %copy-start.3 = (bf16[128,3072]{1,0:T(8,128)(2,1)S(1)}, bf16[128,3072]{1,0:T(8,128)(2,1)}, u32[]{:S(2)}) copy-start(bf16[128,3072]{1,0:T(8,128)(2,1)} %param.16) | copy-start | bytes 2359300
  2.4 6.0 %copy-start.4 = (bf16[2,3072]{1,0:T(2,128)(2,1)S(1)}, bf16[2,3072]{1,0:T(2,128)(2,1)}, u32[]{:S(2)}) copy-start(bf16[2,3072]{1,0:T(2,128)(2,1)} %param.18) | copy-start | bytes 36868
  2.4 6.0 %copy-start.5 = (bf16[2,3072]{1,0:T(2,128)(2,1)S(1)}, bf16[2,3072]{1,0:T(2,128)(2,1)}, u32[]{:S(2)}) copy-start(bf16[2,3072]{1,0:T(2,128)(2,1)} %param.17) | copy-start | bytes 36868
  2.4 62.9 %copy-start.6 = (s32[3]{0:T(128)S(1)}, s32[3]{0:T(128)}, u32[]{:S(2)}) copy-start(s32[3]{0:T(128)} %constant.76.clone) | copy-start | bytes 40
  2.4 62.9 %copy-start.7 = (s32[3]{0:T(128)S(1)}, s32[3]{0:T(128)}, u32[]{:S(2)}) copy-start(s32[3]{0:T(128)} %constant.75.clone) | copy-start | bytes 40
  2.6 70.6 %copy-start = (bf16[2,128,3072]{2,1,0:T(8,128)(2,1)}, bf16[2,128,3072]{2,1,0:T(8,128)(2,1)S(1)}, u32[]{:S(2)}) copy-start(bf16[2,128,3072]{2,1,0:T(8,128)(2,1)S(1)} %pad_maximum_fusion.k0.v0) | copy-start | bytes 4718596
  2.6 37.2 %collective-permute-start.5 = (bf16[2,128,3072]{2,1,0:T(8,128)(2,1)S(1)}, bf16[2,128,3072]{2,1,0:T(8,128)(2,1)S(1)}, u32[]{:S(2)}, u32[]{:S(2)}) collective-permute-start(bf16[2,128,3072]{2,1,0:T(8,128)(2,1)S(1)} %pad_maximum_fusion.k0.v0), channel_id=1, source_target_pairs={{0,2},{1,3},{2,4},{3,5},{4,6},{5,7},{6,8},{7,9},{8,10},{9,11},{10,... | collective-permute-start | bytes 4718600 | tf_op jit(solution)/shard_map/ppermute | solution.py:112
  9.1 2.1 %collective-permute-start = (bf16[2,6272]{1,0:T(2,128)(2,1)}, bf16[2,6272]{1,0:T(2,128)(2,1)}, u32[]{:S(2)}, u32[]{:S(2)}) collective-permute-start(bf16[2,6272]{1,0:T(2,128)(2,1)} %pad_maximum_fusion.4), channel_id=1, source_target_pairs={{0,1},{1,0},{2,3},{3,2},{4,5},{5,4},{6,7},{7,6},{8,9},{9,8},{10,11... | collective-permute-start | bytes 75272 | tf_op jit(solution)/shard_map/ppermute | solution.py:88
  12.1 29.8 %collective-permute-start.1 = (bf16[4,6272]{1,0:T(4,128)(2,1)S(1)}, bf16[4,6272]{1,0:T(4,128)(2,1)}, u32[]{:S(2)}, u32[]{:S(2)}) collective-permute-start(bf16[4,6272]{1,0:T(4,128)(2,1)S(1)} %pad_maximum_fusion.3), channel_id=1, source_target_pairs={{0,2},{1,3},{2,0},{3,1},{4,6},{5,7},{6,4},{7,5},{8,10},{9,11},{10,... | collective-permute-start | bytes 150536 | tf_op jit(solution)/shard_map/ppermute | solution.py:88
  12.3 60.8 %collective-permute-start.4 = (bf16[2,128,3072]{2,1,0:T(8,128)(2,1)S(1)}, bf16[2,128,3072]{2,1,0:T(8,128)(2,1)}, u32[]{:S(2)}, u32[]{:S(2)}) collective-permute-start(bf16[2,128,3072]{2,1,0:T(8,128)(2,1)S(1)} %pad_maximum_fusion.k0.v0), channel_id=1, source_target_pairs={{0,1},{2,3},{4,5},{6,7},{8,9},{10,11},{12,13},{14,15},{1,4},{3,6},... | collective-permute-start | bytes 4718600 | tf_op jit(solution)/shard_map/ppermute | solution.py:113
  39.8 33.4 %copy-start.1 = (bf16[2,128,3072]{2,1,0:T(8,128)(2,1)}, bf16[2,128,3072]{2,1,0:T(8,128)(2,1)S(1)}, u32[]{:S(2)}) copy-start(bf16[2,128,3072]{2,1,0:T(8,128)(2,1)S(1)} %collective-permute-done.5.k2.v2) | copy-start | bytes 4718596
  39.8 33.4 %collective-permute-start.6 = (bf16[2,128,3072]{2,1,0:T(8,128)(2,1)S(1)}, bf16[2,128,3072]{2,1,0:T(8,128)(2,1)}, u32[]{:S(2)}, u32[]{:S(2)}) collective-permute-start(bf16[2,128,3072]{2,1,0:T(8,128)(2,1)S(1)} %collective-permute-done.5.k2.v2), channel_id=1, source_target_pairs={{0,1},{1,0},{2,3},{3,2},{4,5},{5,4},{6,7},{7,6},{8,9},{9,8},{10,11... | collective-permute-start | bytes 4718600 | tf_op jit(solution)/shard_map/ppermute | solution.py:115
  42.7 19.1 %collective-permute-start.2 = (bf16[8,6272]{1,0:T(8,128)(2,1)S(1)}, bf16[8,6272]{1,0:T(8,128)(2,1)}, u32[]{:S(2)}, u32[]{:S(2)}) collective-permute-start(bf16[8,6272]{1,0:T(8,128)(2,1)S(1)} %pad_maximum_fusion.2), channel_id=1, source_target_pairs={{0,4},{1,5},{2,6},{3,7},{4,0},{5,1},{6,2},{7,3},{8,12},{9,13},{10,... | collective-permute-start | bytes 301064 | tf_op jit(solution)/shard_map/ppermute | solution.py:88
  63.0 6.4 %collective-permute-start.3 = (bf16[16,6272]{1,0:T(8,128)(2,1)S(1)}, bf16[16,6272]{1,0:T(8,128)(2,1)}, u32[]{:S(2)}, u32[]{:S(2)}) collective-permute-start(bf16[16,6272]{1,0:T(8,128)(2,1)S(1)} %pad_maximum_fusion.1), channel_id=1, source_target_pairs={{0,8},{1,9},{2,10},{3,11},{4,12},{5,13},{6,14},{7,15},{8,0},{9,1},... | collective-permute-start | bytes 602120 | tf_op jit(solution)/shard_map/ppermute | solution.py:88
  72.1 1.1 %copy-start.2 = (bf16[32,6272]{1,0:T(8,128)(2,1)}, bf16[32,6272]{1,0:T(8,128)(2,1)S(1)}, u32[]{:S(2)}) copy-start(bf16[32,6272]{1,0:T(8,128)(2,1)S(1)} %concatenate.29.ck.cv) | copy-start | bytes 1204228

commit v10 on v9

--- a/solution.py
+++ b/solution.py
@@ -83,11 +83,10 @@
     if size & (size - 1):
         return lax.all_gather(piece, "group", axis=0, tiled=True)
     held = piece
-    step = 1
-    while step < size:
+    steps = [1] + [size >> k for k in range(1, size.bit_length() - 1)]
+    for step in steps:
         other = lax.ppermute(held, "group", [(i, i ^ step) for i in range(size)])
         held = jnp.concatenate([held, other], 0)
-        step *= 2
     return held
 
 

time: 84 us -> 80.5 us (0.958)
  starting transfers between devices: 12.8 us -> 10.5 us
    ppermute x4, starting transfers between devices: 3.83 us -> 1.31 us  [gather_pieces(): other = lax.ppermute(held, 'group', [(i, i ^ step) for i in range(size)])]
  transfers between devices with their start and end apart: 7 -> 7, of which waited for: 4 -> 4; matrix products, arithmetic and copies ran while one was open for 11% -> 12% of each run, Pallas kernels for 0% -> 0%
where the time goes in v10:
time: 80.5 us; the launch traced here: 79.8 us
  waiting for transfers between devices  46.7 us (58%)
  starting transfers between devices  10.5 us (13%)
  Pallas kernels  9.33 us (12%)
  local copies, waits for them, and re-layouts  7.2 us (9%)
  other arithmetic  4.55 us (6%)
  between operations  1.51 us (2%)
    ppermute x1, waiting for transfers between devices, body(): from_two = lax.ppermute(kv, 'group', pairs_two)  23.9 us
    ppermute x4, waiting for transfers between devices, gather_pieces(): other = lax.ppermute(held, 'group', [(i, i ^ step) for i in range(size)])  22.8 us
    pallas_call x1, Pallas kernels, attend(): pl.pallas_call(functools.partial(attention_kernel, heads=HEADS_PER_STEP),...  9.33 us
    ppermute x1, starting transfers between devices, body(): from_mixed = lax.ppermute(kv, 'group', pairs_mixed)  3.62 us
    ppermute x1, starting transfers between devices, body(): from_two = lax.ppermute(kv, 'group', pairs_two)  3.18 us
    concatenate x1, local copies, waits for them, and re-layouts, gather_pieces(): held = jnp.concatenate([held, other], 0)  2.79 us
    concatenate x3, other arithmetic, gather_pieces(): held = jnp.concatenate([held, other], 0)  2.75 us
    ppermute x1, starting transfers between devices, body(): from_swap = lax.ppermute(from_two, 'group', pairs_swap)  2.41 us
  transfers between devices with their start and end apart: 7, of which 4 were waited for; matrix products, arithmetic and copies ran while one was open for 12% of the time, Pallas kernels for 0%

profile of v10, /device:TPU:15, one launch (start us, length us, event | category | flops | bytes accessed | tf_op | source)
XLA Modules:
  0.0 79.8 jit_solution(2413992824713482116)
XLA Ops:
  0.0 1.3 %copy.14 = bf16[16,8,24,128]{3,2,1,0:T(8,128)(2,1)S(1)} copy(bf16[16,8,24,128]{3,1,2,0:T(8,128)(2,1)} %bitcast.10) | data formatting | bytes 1572864
  1.3 0.0 copy-start.3
  1.3 0.7 copy.13
  2.0 0.3 stack_reshape.3
  2.3 0.1 copy-done.3
  2.4 0.0 copy-start.4
  2.4 0.0 copy-start.5
  2.4 0.0 copy-start.6
  2.4 0.0 copy-start.7
  2.4 0.1 pad_maximum_fusion.k0.v0
  2.6 0.0 copy-start
  2.6 3.2 %collective-permute-start.5 = (bf16[2,128,3072]{2,1,0:T(8,128)(2,1)S(1)}, bf16[2,128,3072]{2,1,0:T(8,128)(2,1)S(1)}, u32[]{:S(2)}, u32[]{:S(2)}) collective-permute-start(bf16[2,128,3072]{2,1,0:T(8,128)(2,1)S(1)} %pad_maximum_fusion.k0.v0), channel_id=1, source_target_pairs={{0,2},{1,3},{2,4},{3,5},{4,6},{5,7},{6,8},{7,9},{8,10},{9,11},{10,... | collective-permute-start | bytes 4718600 | tf_op jit(solution)/shard_map/ppermute | solution.py:111
  6.5 0.6 fusion.1
  7.1 1.3 %scatter.9 = bf16[2,128]{1,0:T(2,128)(2,1)S(1)} dynamic-update-slice(bf16[2,128]{1,0:T(2,128)(2,1)S(1)} %scatter.6, bf16[1,1]{1,0:T(2,128)(2,1)} %bitcast.1, s32[]{:T(128)} %bitcast.2, s32[]{:T(128)} %bitcast.3) | dynamic-update-slice | bytes 8 | tf_op jit(solution)/shard_map/scatter | solution.py:100
  8.5 0.0 copy-done.4
  8.5 0.0 copy-done.5
  8.5 0.6 pad_maximum_fusion.4
  9.1 1.0 %collective-permute-start = (bf16[2,6272]{1,0:T(2,128)(2,1)}, bf16[2,6272]{1,0:T(2,128)(2,1)}, u32[]{:S(2)}, u32[]{:S(2)}) collective-permute-start(bf16[2,6272]{1,0:T(2,128)(2,1)} %pad_maximum_fusion.4), channel_id=1, source_target_pairs={{0,1},{1,0},{2,3},{3,2},{4,5},{5,4},{6,7},{7,6},{8,9},{9,8},{10,11... | collective-permute-start | bytes 75272 | tf_op jit(solution)/shard_map/ppermute | solution.py:88
  10.1 1.2 %collective-permute-done = bf16[2,6272]{1,0:T(2,128)(2,1)} collective-permute-done((bf16[2,6272]{1,0:T(2,128)(2,1)}, bf16[2,6272]{1,0:T(2,128)(2,1)}, u32[]{:S(2)}, u32[]{:S(2)}) %collective-permute-start) | collective-permute-done | bytes 25120 | tf_op jit(solution)/shard_map/ppermute | solution.py:88
  11.3 0.8 pad_maximum_fusion.3
  12.1 0.2 collective-permute-start.1
  12.3 3.6 %collective-permute-start.4 = (bf16[2,128,3072]{2,1,0:T(8,128)(2,1)S(1)}, bf16[2,128,3072]{2,1,0:T(8,128)(2,1)}, u32[]{:S(2)}, u32[]{:S(2)}) collective-permute-start(bf16[2,128,3072]{2,1,0:T(8,128)(2,1)S(1)} %pad_maximum_fusion.k0.v0), channel_id=1, source_target_pairs={{0,1},{2,3},{4,5},{6,7},{8,9},{10,11},{12,13},{14,15},{1,4},{3,6},... | collective-permute-start | bytes 4718600 | tf_op jit(solution)/shard_map/ppermute | solution.py:112
  15.9 23.9 %collective-permute-done.5.k2.v2 = bf16[2,128,3072]{2,1,0:T(8,128)(2,1)S(1)} collective-permute-done((bf16[2,128,3072]{2,1,0:T(8,128)(2,1)S(1)}, bf16[2,128,3072]{2,1,0:T(8,128)(2,1)S(1)}, u32[]{:S(2)}, u32[]{:S(2)}) %collective-permute-start.5) | collective-permute-done | bytes 1572896 | tf_op jit(solution)/shard_map/ppermute | solution.py:111
  39.8 0.0 copy-start.1
  39.8 2.4 %collective-permute-start.6 = (bf16[2,128,3072]{2,1,0:T(8,128)(2,1)S(1)}, bf16[2,128,3072]{2,1,0:T(8,128)(2,1)}, u32[]{:S(2)}, u32[]{:S(2)}) collective-permute-start(bf16[2,128,3072]{2,1,0:T(8,128)(2,1)S(1)} %collective-permute-done.5.k2.v2), channel_id=1, source_target_pairs={{0,1},{1,0},{2,3},{3,2},{4,5},{5,4},{6,7},{7,6},{8,9},{9,8},{10,11... | collective-permute-start | bytes 4718600 | tf_op jit(solution)/shard_map/ppermute | solution.py:114
  42.2 0.0 collective-permute-done.1
  42.2 0.9 %pad_maximum_fusion.2 = bf16[8,6272]{1,0:T(8,128)(2,1)S(1)} fusion(bf16[4,6272]{1,0:T(4,128)(2,1)} %collective-permute-done.1, bf16[2,6272]{1,0:T(2,128)(2,1)} %collective-permute-done, bf16[2,128]{1,0:T(2,128)(2,1)S(1)} %scatter.9, bf16[2,3072]{1,0:T(2,128)(2,1)S(1)} %copy-done.4, bf16[2,3072]{1,0:T(2,128)(2,1)S(1)} %copy-done.5), kind=kLoop, calls=%fused_computation.2 | loop fusion | flops 501760 | bytes 200704 | tf_op jit(solution)/shard_map/concatenate | solution.py:89
  43.1 0.1 collective-permute-start.2
  43.8 16.9 %collective-permute-done.2 = bf16[8,6272]{1,0:T(8,128)(2,1)} collective-permute-done((bf16[8,6272]{1,0:T(8,128)(2,1)S(1)}, bf16[8,6272]{1,0:T(8,128)(2,1)}, u32[]{:S(2)}, u32[]{:S(2)}) %collective-permute-start.2) | collective-permute-done | bytes 100384 | tf_op jit(solution)/shard_map/ppermute | solution.py:88
  60.8 1.1 %pad_maximum_fusion.1 = bf16[16,6272]{1,0:T(8,128)(2,1)S(1)} fusion(bf16[8,6272]{1,0:T(8,128)(2,1)} %collective-permute-done.2, bf16[4,6272]{1,0:T(4,128)(2,1)} %collective-permute-done.1, bf16[2,6272]{1,0:T(2,128)(2,1)} %collective-permute-done, bf16[2,128]{1,0:T(2,128)(2,1)S(1)} %scatter.9, bf16[2,3072]{1,0:T(2,128)(2,1)S(1)} %copy-done.4, ...), kind=kLoop, calls=%fused_computation.1 | loop fusion | flops 1204224 | bytes 401408 | tf_op jit(solution)/shard_map/concatenate | solution.py:89
  61.8 0.1 collective-permute-start.3
  61.9 0.0 copy-done.6
  61.9 0.0 copy-done.7
  61.9 4.6 %collective-permute-done.3 = bf16[16,6272]{1,0:T(8,128)(2,1)} collective-permute-done((bf16[16,6272]{1,0:T(8,128)(2,1)S(1)}, bf16[16,6272]{1,0:T(8,128)(2,1)}, u32[]{:S(2)}, u32[]{:S(2)}) %collective-permute-start.3) | collective-permute-done | bytes 200736 | tf_op jit(solution)/shard_map/ppermute | solution.py:88
  66.6 2.8 %concatenate.29.ck.cv = bf16[32,6272]{1,0:T(8,128)(2,1)S(1)} concatenate(bf16[2,6272]{1,0:T(2,128)(2,1)} %pad_maximum_fusion.4, bf16[2,6272]{1,0:T(2,128)(2,1)} %collective-permute-done, bf16[4,6272]{1,0:T(4,128)(2,1)} %collective-permute-done.1, bf16[8,6272]{1,0:T(8,128)(2,1)} %collective-permute-done.2, bf16[16,6272]{1,0:T(8,128)(2,1)} %collective-permute-done.3), dimensions={0} | concatenate | bytes 802816 | tf_op jit(solution)/shard_map/concatenate | solution.py:89
  69.4 0.0 copy-start.2
  69.4 0.2 convert_reduce_fusion.1
  69.6 0.2 select_reduce_fusion
  69.7 0.7 pad_add_fusion.table_ref
  70.4 0.0 collective-permute-done.4.k1.v1
  70.4 0.0 collective-permute-done.6.k3.v3
  70.4 0.0 copy-done
  70.4 0.0 copy-done.1
  70.4 0.0 copy-done.2
  70.4 9.3 %shard_map.100 = bf16[128,3072]{1,0:T(8,128)(2,1)} custom-call(s32[5]{0:T(128)} %pad_add_fusion.table_ref, bf16[128,3072]{1,0:T(8,128)(2,1)} %q_ref.1, bf16[2,128,3072]{2,1,0:T(8,128)(2,1)} %copy-done, bf16[2,128,3072]{2,1,0:T(8,128)(2,1)} %copy-done, bf16[2,128,3072]{2,1,0:T(8,128)(2,1)} %collective-permute-done.4.k1.v1, ...), custom_call_target="tpu_custom_call" | custom-call | flops 855638016 | bytes 8454144 | tf_op jit(solution)/shard_map/pallas_call | solution.py:74
  (3 shorter events, 0.0 us)
Async XLA Ops:
  1.3 1.1 %copy-start.3 = (bf16[128,3072]{1,0:T(8,128)(2,1)S(1)}, bf16[128,3072]{1,0:T(8,128)(2,1)}, u32[]{:S(2)}) copy-start(bf16[128,3072]{1,0:T(8,128)(2,1)} %param.16) | copy-start | bytes 2359300
  2.4 6.0 %copy-start.4 = (bf16[2,3072]{1,0:T(2,128)(2,1)S(1)}, bf16[2,3072]{1,0:T(2,128)(2,1)}, u32[]{:S(2)}) copy-start(bf16[2,3072]{1,0:T(2,128)(2,1)} %param.18) | copy-start | bytes 36868
  2.4 6.0 %copy-start.5 = (bf16[2,3072]{1,0:T(2,128)(2,1)S(1)}, bf16[2,3072]{1,0:T(2,128)(2,1)}, u32[]{:S(2)}) copy-start(bf16[2,3072]{1,0:T(2,128)(2,1)} %param.17) | copy-start | bytes 36868
  2.4 59.5 %copy-start.6 = (s32[3]{0:T(128)S(1)}, s32[3]{0:T(128)}, u32[]{:S(2)}) copy-start(s32[3]{0:T(128)} %constant.76.clone) | copy-start | bytes 40
  2.4 59.5 %copy-start.7 = (s32[3]{0:T(128)S(1)}, s32[3]{0:T(128)}, u32[]{:S(2)}) copy-start(s32[3]{0:T(128)} %constant.75.clone) | copy-start | bytes 40
  2.6 67.8 %copy-start = (bf16[2,128,3072]{2,1,0:T(8,128)(2,1)}, bf16[2,128,3072]{2,1,0:T(8,128)(2,1)S(1)}, u32[]{:S(2)}) copy-start(bf16[2,128,3072]{2,1,0:T(8,128)(2,1)S(1)} %pad_maximum_fusion.k0.v0) | copy-start | bytes 4718596
  2.6 37.2 %collective-permute-start.5 = (bf16[2,128,3072]{2,1,0:T(8,128)(2,1)S(1)}, bf16[2,128,3072]{2,1,0:T(8,128)(2,1)S(1)}, u32[]{:S(2)}, u32[]{:S(2)}) collective-permute-start(bf16[2,128,3072]{2,1,0:T(8,128)(2,1)S(1)} %pad_maximum_fusion.k0.v0), channel_id=1, source_target_pairs={{0,2},{1,3},{2,4},{3,5},{4,6},{5,7},{6,8},{7,9},{8,10},{9,11},{10,... | collective-permute-start | bytes 4718600 | tf_op jit(solution)/shard_map/ppermute | solution.py:111
  9.1 2.1 %collective-permute-start = (bf16[2,6272]{1,0:T(2,128)(2,1)}, bf16[2,6272]{1,0:T(2,128)(2,1)}, u32[]{:S(2)}, u32[]{:S(2)}) collective-permute-start(bf16[2,6272]{1,0:T(2,128)(2,1)} %pad_maximum_fusion.4), channel_id=1, source_target_pairs={{0,1},{1,0},{2,3},{3,2},{4,5},{5,4},{6,7},{7,6},{8,9},{9,8},{10,11... | collective-permute-start | bytes 75272 | tf_op jit(solution)/shard_map/ppermute | solution.py:88
  12.1 30.1 %collective-permute-start.1 = (bf16[4,6272]{1,0:T(4,128)(2,1)S(1)}, bf16[4,6272]{1,0:T(4,128)(2,1)}, u32[]{:S(2)}, u32[]{:S(2)}) collective-permute-start(bf16[4,6272]{1,0:T(4,128)(2,1)S(1)} %pad_maximum_fusion.3), channel_id=1, source_target_pairs={{0,8},{1,9},{2,10},{3,11},{4,12},{5,13},{6,14},{7,15},{8,0},{9,1},... | collective-permute-start | bytes 150536 | tf_op jit(solution)/shard_map/ppermute | solution.py:88
  12.3 58.1 %collective-permute-start.4 = (bf16[2,128,3072]{2,1,0:T(8,128)(2,1)S(1)}, bf16[2,128,3072]{2,1,0:T(8,128)(2,1)}, u32[]{:S(2)}, u32[]{:S(2)}) collective-permute-start(bf16[2,128,3072]{2,1,0:T(8,128)(2,1)S(1)} %pad_maximum_fusion.k0.v0), channel_id=1, source_target_pairs={{0,1},{2,3},{4,5},{6,7},{8,9},{10,11},{12,13},{14,15},{1,4},{3,6},... | collective-permute-start | bytes 4718600 | tf_op jit(solution)/shard_map/ppermute | solution.py:112
  39.8 30.6 %copy-start.1 = (bf16[2,128,3072]{2,1,0:T(8,128)(2,1)}, bf16[2,128,3072]{2,1,0:T(8,128)(2,1)S(1)}, u32[]{:S(2)}) copy-start(bf16[2,128,3072]{2,1,0:T(8,128)(2,1)S(1)} %collective-permute-done.5.k2.v2) | copy-start | bytes 4718596
  39.8 30.6 %collective-permute-start.6 = (bf16[2,128,3072]{2,1,0:T(8,128)(2,1)S(1)}, bf16[2,128,3072]{2,1,0:T(8,128)(2,1)}, u32[]{:S(2)}, u32[]{:S(2)}) collective-permute-start(bf16[2,128,3072]{2,1,0:T(8,128)(2,1)S(1)} %collective-permute-done.5.k2.v2), channel_id=1, source_target_pairs={{0,1},{1,0},{2,3},{3,2},{4,5},{5,4},{6,7},{7,6},{8,9},{9,8},{10,11... | collective-permute-start | bytes 4718600 | tf_op jit(solution)/shard_map/ppermute | solution.py:114
  43.1 17.7 %collective-permute-start.2 = (bf16[8,6272]{1,0:T(8,128)(2,1)S(1)}, bf16[8,6272]{1,0:T(8,128)(2,1)}, u32[]{:S(2)}, u32[]{:S(2)}) collective-permute-start(bf16[8,6272]{1,0:T(8,128)(2,1)S(1)} %pad_maximum_fusion.2), channel_id=1, source_target_pairs={{0,4},{1,5},{2,6},{3,7},{4,0},{5,1},{6,2},{7,3},{8,12},{9,13},{10,... | collective-permute-start | bytes 301064 | tf_op jit(solution)/shard_map/ppermute | solution.py:88
  61.8 4.7 %collective-permute-start.3 = (bf16[16,6272]{1,0:T(8,128)(2,1)S(1)}, bf16[16,6272]{1,0:T(8,128)(2,1)}, u32[]{:S(2)}, u32[]{:S(2)}) collective-permute-start(bf16[16,6272]{1,0:T(8,128)(2,1)S(1)} %pad_maximum_fusion.1), channel_id=1, source_target_pairs={{0,2},{1,3},{2,0},{3,1},{4,6},{5,7},{6,4},{7,5},{8,10},{9,11},{10,... | collective-permute-start | bytes 602120 | tf_op jit(solution)/shard_map/ppermute | solution.py:88
  69.4 1.1 %copy-start.2 = (bf16[32,6272]{1,0:T(8,128)(2,1)}, bf16[32,6272]{1,0:T(8,128)(2,1)S(1)}, u32[]{:S(2)}) copy-start(bf16[32,6272]{1,0:T(8,128)(2,1)S(1)} %concatenate.29.ck.cv) | copy-start | bytes 1204228

commit v11 on v5

--- a/solution.py
+++ b/solution.py
@@ -10,7 +10,7 @@
 
 HEAD_DIM = 128
 WIN = 4
-HEADS_PER_STEP = 4
+HEADS_PER_STEP = 8
 
 
 def attention_kernel(table_ref, q_ref, k0, v0, k1, v1, k2, v2, k3, v3, ck, cv, gate_ref, o_ref, *, heads):

time: 76 us -> 75.7 us (level)
  no operation moved by 1% of the time
where the time goes in v11:
time: 75.7 us; the launch traced here: 74.4 us
  waiting for transfers between devices  39.3 us (52%)
  starting transfers between devices  12.7 us (17%)
  Pallas kernels  9.13 us (12%)
  local copies, waits for them, and re-layouts  7.2 us (10%)
  other arithmetic  4.61 us (6%)
  between operations  1.5 us (2%)
    ppermute x4, waiting for transfers between devices, gather_pieces(): other = lax.ppermute(held, 'group', [(i, i ^ step) for i in range(size)])  34.6 us
    pallas_call x1, Pallas kernels, attend(): pl.pallas_call(functools.partial(attention_kernel, heads=HEADS_PER_STEP),...  9.13 us
    ppermute x1, starting transfers between devices, body(): from_mixed = lax.ppermute(kv, 'group', pairs_mixed)  7.45 us
    ppermute x1, waiting for transfers between devices, body(): from_mixed = lax.ppermute(kv, 'group', pairs_mixed)  4.68 us
    ppermute x1, starting transfers between devices, body(): from_two = lax.ppermute(kv, 'group', pairs_two)  3.18 us
    concatenate x3, other arithmetic, gather_pieces(): held = jnp.concatenate([held, other], 0)  2.81 us
    concatenate x1, local copies, waits for them, and re-layouts, gather_pieces(): held = jnp.concatenate([held, other], 0)  2.79 us
    ppermute x4, starting transfers between devices, gather_pieces(): other = lax.ppermute(held, 'group', [(i, i ^ step) for i in range(size)])  1.95 us
  transfers between devices with their start and end apart: 7, of which 4 were waited for; matrix products, arithmetic and copies ran while one was open for 12% of the time, Pallas kernels for 0%

profile of v11, /device:TPU:15, one launch (start us, length us, event | category | flops | bytes accessed | tf_op | source)
XLA Modules:
  0.0 74.4 jit_solution(13627403983521172247)
XLA Ops:
  0.0 1.3 %copy.14 = bf16[16,8,24,128]{3,2,1,0:T(8,128)(2,1)S(1)} copy(bf16[16,8,24,128]{3,1,2,0:T(8,128)(2,1)} %bitcast.10) | data formatting | bytes 1572864
  1.3 0.0 copy-start.3
  1.3 0.7 copy.13
  2.0 0.3 stack_reshape.3
  2.3 0.1 copy-done.3
  2.4 0.0 copy-start.4
  2.4 0.0 copy-start.5
  2.4 0.0 copy-start.6
  2.4 0.0 copy-start.7
  2.4 0.1 pad_maximum_fusion.k0.v0
  2.6 0.0 copy-start
  2.6 3.2 %collective-permute-start.5 = (bf16[2,128,3072]{2,1,0:T(8,128)(2,1)S(1)}, bf16[2,128,3072]{2,1,0:T(8,128)(2,1)S(1)}, u32[]{:S(2)}, u32[]{:S(2)}) collective-permute-start(bf16[2,128,3072]{2,1,0:T(8,128)(2,1)S(1)} %pad_maximum_fusion.k0.v0), channel_id=1, source_target_pairs={{0,2},{1,3},{2,4},{3,5},{4,6},{5,7},{6,8},{7,9},{8,10},{9,11},{10,... | collective-permute-start | bytes 4718600 | tf_op jit(solution)/shard_map/ppermute | solution.py:112
  6.5 0.6 fusion.1
  7.1 1.3 %scatter.9 = bf16[2,128]{1,0:T(2,128)(2,1)S(1)} dynamic-update-slice(bf16[2,128]{1,0:T(2,128)(2,1)S(1)} %scatter.6, bf16[1,1]{1,0:T(2,128)(2,1)} %bitcast.1, s32[]{:T(128)} %bitcast.2, s32[]{:T(128)} %bitcast.3) | dynamic-update-slice | bytes 8 | tf_op jit(solution)/shard_map/scatter | solution.py:101
  8.5 0.0 copy-done.4
  8.5 0.0 copy-done.5
  8.5 0.6 pad_maximum_fusion.4
  9.1 0.4 collective-permute-start
  9.5 30.0 %collective-permute-done = bf16[2,6272]{1,0:T(2,128)(2,1)} collective-permute-done((bf16[2,6272]{1,0:T(2,128)(2,1)}, bf16[2,6272]{1,0:T(2,128)(2,1)}, u32[]{:S(2)}, u32[]{:S(2)}) %collective-permute-start) | collective-permute-done | bytes 25120 | tf_op jit(solution)/shard_map/ppermute | solution.py:88
  39.5 0.8 %pad_maximum_fusion.3 = bf16[4,6272]{1,0:T(4,128)(2,1)S(1)} fusion(bf16[2,6272]{1,0:T(2,128)(2,1)} %collective-permute-done, bf16[2,128]{1,0:T(2,128)(2,1)S(1)} %scatter.9, bf16[2,3072]{1,0:T(2,128)(2,1)S(1)} %copy-done.4, bf16[2,3072]{1,0:T(2,128)(2,1)S(1)} %copy-done.5), kind=kLoop, calls=%fused_computation.3 | loop fusion | flops 200704 | bytes 100352 | tf_op jit(solution)/shard_map/concatenate | solution.py:89
  40.3 0.1 collective-permute-start.1
  40.4 7.4 %collective-permute-start.4 = (bf16[2,128,3072]{2,1,0:T(8,128)(2,1)S(1)}, bf16[2,128,3072]{2,1,0:T(8,128)(2,1)}, u32[]{:S(2)}, u32[]{:S(2)}) collective-permute-start(bf16[2,128,3072]{2,1,0:T(8,128)(2,1)S(1)} %pad_maximum_fusion.k0.v0), channel_id=1, source_target_pairs={{0,1},{2,3},{4,5},{6,7},{8,9},{10,11},{12,13},{14,15},{1,4},{3,6},... | collective-permute-start | bytes 4718600 | tf_op jit(solution)/shard_map/ppermute | solution.py:113
  47.9 0.0 collective-permute-done.5.k2.v2
  47.9 0.0 copy-start.1
  47.9 0.1 collective-permute-start.6
  48.0 0.0 collective-permute-done.1
  48.0 1.0 %pad_maximum_fusion.2 = bf16[8,6272]{1,0:T(8,128)(2,1)S(1)} fusion(bf16[4,6272]{1,0:T(4,128)(2,1)} %collective-permute-done.1, bf16[2,6272]{1,0:T(2,128)(2,1)} %collective-permute-done, bf16[2,128]{1,0:T(2,128)(2,1)S(1)} %scatter.9, bf16[2,3072]{1,0:T(2,128)(2,1)S(1)} %copy-done.4, bf16[2,3072]{1,0:T(2,128)(2,1)S(1)} %copy-done.5), kind=kLoop, calls=%fused_computation.2 | loop fusion | flops 501760 | bytes 200704 | tf_op jit(solution)/shard_map/concatenate | solution.py:89
  48.9 0.1 collective-permute-start.2
  49.7 3.4 %collective-permute-done.2 = bf16[8,6272]{1,0:T(8,128)(2,1)} collective-permute-done((bf16[8,6272]{1,0:T(8,128)(2,1)S(1)}, bf16[8,6272]{1,0:T(8,128)(2,1)}, u32[]{:S(2)}, u32[]{:S(2)}) %collective-permute-start.2) | collective-permute-done | bytes 100384 | tf_op jit(solution)/shard_map/ppermute | solution.py:88
  53.1 1.1 %pad_maximum_fusion.1 = bf16[16,6272]{1,0:T(8,128)(2,1)S(1)} fusion(bf16[8,6272]{1,0:T(8,128)(2,1)} %collective-permute-done.2, bf16[4,6272]{1,0:T(4,128)(2,1)} %collective-permute-done.1, bf16[2,6272]{1,0:T(2,128)(2,1)} %collective-permute-done, bf16[2,128]{1,0:T(2,128)(2,1)S(1)} %scatter.9, bf16[2,3072]{1,0:T(2,128)(2,1)S(1)} %copy-done.4, ...), kind=kLoop, calls=%fused_computation.1 | loop fusion | flops 1204224 | bytes 401408 | tf_op jit(solution)/shard_map/concatenate | solution.py:89
  54.1 1.3 %collective-permute-start.3 = (bf16[16,6272]{1,0:T(8,128)(2,1)S(1)}, bf16[16,6272]{1,0:T(8,128)(2,1)}, u32[]{:S(2)}, u32[]{:S(2)}) collective-permute-start(bf16[16,6272]{1,0:T(8,128)(2,1)S(1)} %pad_maximum_fusion.1), channel_id=1, source_target_pairs={{0,1},{1,0},{2,3},{3,2},{4,5},{5,4},{6,7},{7,6},{8,9},{9,8},{10,11... | collective-permute-start | bytes 602120 | tf_op jit(solution)/shard_map/ppermute | solution.py:88
  55.5 0.0 copy-done.6
  55.5 0.0 copy-done.7
  55.5 1.2 %collective-permute-done.3 = bf16[16,6272]{1,0:T(8,128)(2,1)} collective-permute-done((bf16[16,6272]{1,0:T(8,128)(2,1)S(1)}, bf16[16,6272]{1,0:T(8,128)(2,1)}, u32[]{:S(2)}, u32[]{:S(2)}) %collective-permute-start.3) | collective-permute-done | bytes 200736 | tf_op jit(solution)/shard_map/ppermute | solution.py:88
  56.7 2.8 %concatenate.29.ck.cv = bf16[32,6272]{1,0:T(8,128)(2,1)S(1)} concatenate(bf16[2,6272]{1,0:T(2,128)(2,1)} %pad_maximum_fusion.4, bf16[2,6272]{1,0:T(2,128)(2,1)} %collective-permute-done, bf16[4,6272]{1,0:T(4,128)(2,1)} %collective-permute-done.1, bf16[8,6272]{1,0:T(8,128)(2,1)} %collective-permute-done.2, bf16[16,6272]{1,0:T(8,128)(2,1)} %collective-permute-done.3), dimensions={0} | concatenate | bytes 802816 | tf_op jit(solution)/shard_map/concatenate | solution.py:89
  59.5 0.0 copy-start.2
  59.5 0.2 convert_reduce_fusion.1
  59.7 0.2 select_reduce_fusion
  59.9 0.7 pad_add_fusion.table_ref
  60.5 4.7 %collective-permute-done.4.k1.v1 = bf16[2,128,3072]{2,1,0:T(8,128)(2,1)} collective-permute-done((bf16[2,128,3072]{2,1,0:T(8,128)(2,1)S(1)}, bf16[2,128,3072]{2,1,0:T(8,128)(2,1)}, u32[]{:S(2)}, u32[]{:S(2)}) %collective-permute-start.4) | collective-permute-done | bytes 1572896 | tf_op jit(solution)/shard_map/ppermute | solution.py:113
  65.2 0.0 collective-permute-done.6.k3.v3
  65.2 0.0 copy-done
  65.2 0.0 copy-done.1
  65.2 0.0 copy-done.2
  65.2 9.1 %shard_map.100 = bf16[128,3072]{1,0:T(8,128)(2,1)} custom-call(s32[5]{0:T(128)} %pad_add_fusion.table_ref, bf16[128,3072]{1,0:T(8,128)(2,1)} %q_ref.1, bf16[2,128,3072]{2,1,0:T(8,128)(2,1)} %copy-done, bf16[2,128,3072]{2,1,0:T(8,128)(2,1)} %copy-done, bf16[2,128,3072]{2,1,0:T(8,128)(2,1)} %collective-permute-done.4.k1.v1, ...), custom_call_target="tpu_custom_call" | custom-call | flops 855638016 | bytes 8454144 | tf_op jit(solution)/shard_map/pallas_call | solution.py:74
  (3 shorter events, 0.0 us)
Async XLA Ops:
  1.3 1.1 %copy-start.3 = (bf16[128,3072]{1,0:T(8,128)(2,1)S(1)}, bf16[128,3072]{1,0:T(8,128)(2,1)}, u32[]{:S(2)}) copy-start(bf16[128,3072]{1,0:T(8,128)(2,1)} %param.16) | copy-start | bytes 2359300
  2.4 6.0 %copy-start.4 = (bf16[2,3072]{1,0:T(2,128)(2,1)S(1)}, bf16[2,3072]{1,0:T(2,128)(2,1)}, u32[]{:S(2)}) copy-start(bf16[2,3072]{1,0:T(2,128)(2,1)} %param.18) | copy-start | bytes 36868
  2.4 6.0 %copy-start.5 = (bf16[2,3072]{1,0:T(2,128)(2,1)S(1)}, bf16[2,3072]{1,0:T(2,128)(2,1)}, u32[]{:S(2)}) copy-start(bf16[2,3072]{1,0:T(2,128)(2,1)} %param.17) | copy-start | bytes 36868
  2.4 53.1 %copy-start.6 = (s32[3]{0:T(128)S(1)}, s32[3]{0:T(128)}, u32[]{:S(2)}) copy-start(s32[3]{0:T(128)} %constant.76.clone) | copy-start | bytes 40
  2.4 53.1 %copy-start.7 = (s32[3]{0:T(128)S(1)}, s32[3]{0:T(128)}, u32[]{:S(2)}) copy-start(s32[3]{0:T(128)} %constant.75.clone) | copy-start | bytes 40
  2.6 62.6 %copy-start = (bf16[2,128,3072]{2,1,0:T(8,128)(2,1)}, bf16[2,128,3072]{2,1,0:T(8,128)(2,1)S(1)}, u32[]{:S(2)}) copy-start(bf16[2,128,3072]{2,1,0:T(8,128)(2,1)S(1)} %pad_maximum_fusion.k0.v0) | copy-start | bytes 4718596
  2.6 45.3 %collective-permute-start.5 = (bf16[2,128,3072]{2,1,0:T(8,128)(2,1)S(1)}, bf16[2,128,3072]{2,1,0:T(8,128)(2,1)S(1)}, u32[]{:S(2)}, u32[]{:S(2)}) collective-permute-start(bf16[2,128,3072]{2,1,0:T(8,128)(2,1)S(1)} %pad_maximum_fusion.k0.v0), channel_id=1, source_target_pairs={{0,2},{1,3},{2,4},{3,5},{4,6},{5,7},{6,8},{7,9},{8,10},{9,11},{10,... | collective-permute-start | bytes 4718600 | tf_op jit(solution)/shard_map/ppermute | solution.py:112
  9.1 30.4 %collective-permute-start = (bf16[2,6272]{1,0:T(2,128)(2,1)}, bf16[2,6272]{1,0:T(2,128)(2,1)}, u32[]{:S(2)}, u32[]{:S(2)}) collective-permute-start(bf16[2,6272]{1,0:T(2,128)(2,1)} %pad_maximum_fusion.4), channel_id=1, source_target_pairs={{0,8},{1,9},{2,10},{3,11},{4,12},{5,13},{6,14},{7,15},{8,0},{9,1},... | collective-permute-start | bytes 75272 | tf_op jit(solution)/shard_map/ppermute | solution.py:88
  40.3 7.7 %collective-permute-start.1 = (bf16[4,6272]{1,0:T(4,128)(2,1)S(1)}, bf16[4,6272]{1,0:T(4,128)(2,1)}, u32[]{:S(2)}, u32[]{:S(2)}) collective-permute-start(bf16[4,6272]{1,0:T(4,128)(2,1)S(1)} %pad_maximum_fusion.3), channel_id=1, source_target_pairs={{0,4},{1,5},{2,6},{3,7},{4,0},{5,1},{6,2},{7,3},{8,12},{9,13},{10,... | collective-permute-start | bytes 150536 | tf_op jit(solution)/shard_map/ppermute | solution.py:88
  40.4 24.8 %collective-permute-start.4 = (bf16[2,128,3072]{2,1,0:T(8,128)(2,1)S(1)}, bf16[2,128,3072]{2,1,0:T(8,128)(2,1)}, u32[]{:S(2)}, u32[]{:S(2)}) collective-permute-start(bf16[2,128,3072]{2,1,0:T(8,128)(2,1)S(1)} %pad_maximum_fusion.k0.v0), channel_id=1, source_target_pairs={{0,1},{2,3},{4,5},{6,7},{8,9},{10,11},{12,13},{14,15},{1,4},{3,6},... | collective-permute-start | bytes 4718600 | tf_op jit(solution)/shard_map/ppermute | solution.py:113
  47.9 17.3 %copy-start.1 = (bf16[2,128,3072]{2,1,0:T(8,128)(2,1)}, bf16[2,128,3072]{2,1,0:T(8,128)(2,1)S(1)}, u32[]{:S(2)}) copy-start(bf16[2,128,3072]{2,1,0:T(8,128)(2,1)S(1)} %collective-permute-done.5.k2.v2) | copy-start | bytes 4718596
  47.9 17.3 %collective-permute-start.6 = (bf16[2,128,3072]{2,1,0:T(8,128)(2,1)S(1)}, bf16[2,128,3072]{2,1,0:T(8,128)(2,1)}, u32[]{:S(2)}, u32[]{:S(2)}) collective-permute-start(bf16[2,128,3072]{2,1,0:T(8,128)(2,1)S(1)} %collective-permute-done.5.k2.v2), channel_id=1, source_target_pairs={{0,1},{1,0},{2,3},{3,2},{4,5},{5,4},{6,7},{7,6},{8,9},{9,8},{10,11... | collective-permute-start | bytes 4718600 | tf_op jit(solution)/shard_map/ppermute | solution.py:115
  48.9 4.1 %collective-permute-start.2 = (bf16[8,6272]{1,0:T(8,128)(2,1)S(1)}, bf16[8,6272]{1,0:T(8,128)(2,1)}, u32[]{:S(2)}, u32[]{:S(2)}) collective-permute-start(bf16[8,6272]{1,0:T(8,128)(2,1)S(1)} %pad_maximum_fusion.2), channel_id=1, source_target_pairs={{0,2},{1,3},{2,0},{3,1},{4,6},{5,7},{6,4},{7,5},{8,10},{9,11},{10,... | collective-permute-start | bytes 301064 | tf_op jit(solution)/shard_map/ppermute | solution.py:88
  54.1 2.6 %collective-permute-start.3 = (bf16[16,6272]{1,0:T(8,128)(2,1)S(1)}, bf16[16,6272]{1,0:T(8,128)(2,1)}, u32[]{:S(2)}, u32[]{:S(2)}) collective-permute-start(bf16[16,6272]{1,0:T(8,128)(2,1)S(1)} %pad_maximum_fusion.1), channel_id=1, source_target_pairs={{0,1},{1,0},{2,3},{3,2},{4,5},{5,4},{6,7},{7,6},{8,9},{9,8},{10,11... | collective-permute-start | bytes 602120 | tf_op jit(solution)/shard_map/ppermute | solution.py:88
  59.5 5.7 %copy-start.2 = (bf16[32,6272]{1,0:T(8,128)(2,1)}, bf16[32,6272]{1,0:T(8,128)(2,1)S(1)}, u32[]{:S(2)}) copy-start(bf16[32,6272]{1,0:T(8,128)(2,1)S(1)} %concatenate.29.ck.cv) | copy-start | bytes 1204228

commit v12 on v11

--- a/solution.py
+++ b/solution.py
@@ -13,37 +13,53 @@
 HEADS_PER_STEP = 8
 
 
-def attention_kernel(table_ref, q_ref, k0, v0, k1, v1, k2, v2, k3, v3, ck, cv, gate_ref, o_ref, *, heads):
+def partial_kernel(table_ref, q_ref, k0, v0, k2, v2, k3, v3, ck, cv, m_ref, l_ref, acc_ref, *, heads):
+    scale = 1.0 / math.sqrt(HEAD_DIM)
+    rows = q_ref.shape[0]
+    slot = lax.broadcasted_iota(jnp.int32, (1, rows), 1)
+    dims = (((1,), (1,)), ((), ()))
+    blocks = ((k0, v0, 0), (k2, v2, 2), (k3, v3, 3))
+    for h in range(heads):
+        cols = slice(h * HEAD_DIM, (h + 1) * HEAD_DIM)
+        q = q_ref[:, cols]
+        scores = []
+        for k_ref, _, j in blocks:
+            s = jnp.dot(q, k_ref[:, cols], preferred_element_type=jnp.float32) * scale
+            scores.append(jnp.where(slot < table_ref[j], s, -jnp.inf))
+        scores.append(lax.dot_general(q, ck[:, cols], dims, preferred_element_type=jnp.float32) * scale)
+        window = jnp.maximum(jnp.maximum(scores[0], scores[1]), scores[2])
+        row_max = jnp.maximum(window.max(axis=1, keepdims=True), scores[3].max(axis=1, keepdims=True))
+        values = [v_ref[:, cols] for _, v_ref, _ in blocks] + [cv[:, cols]]
+        probabilities = [jnp.exp(s - row_max) for s in scores]
+        window_sum = (probabilities[0] + probabilities[1]) + probabilities[2]
+        denominator = window_sum.sum(axis=1, keepdims=True) + probabilities[3].sum(axis=1, keepdims=True)
+        attended = jnp.zeros((rows, HEAD_DIM), jnp.float32)
+        for p, v in zip(probabilities, values):
+            attended = attended + jnp.dot(p.astype(jnp.bfloat16), v, preferred_element_type=jnp.float32)
+        m_ref[:, h:h + 1] = row_max
+        l_ref[:, h:h + 1] = denominator
+        acc_ref[:, cols] = attended
+
+
+def finish_kernel(table_ref, q_ref, k1, v1, m_ref, l_ref, acc_ref, gate_ref, o_ref, *, heads):
     scale = 1.0 / math.sqrt(HEAD_DIM)
     rows = q_ref.shape[0]
     slot = lax.broadcasted_iota(jnp.int32, (1, rows), 1)
     row = lax.broadcasted_iota(jnp.int32, (rows, 1), 0)
-    level = table_ref[4]
-    gate = gate_ref[pl.ds(level, 1), :]
+    gate = gate_ref[pl.ds(table_ref[4], 1), :]
     live_row = row < table_ref[0]
-    blocks = ((k0, v0), (k1, v1), (k2, v2), (k3, v3))
-    dims = (((1,), (1,)), ((), ()))
     for h in range(heads):
         cols = slice(h * HEAD_DIM, (h + 1) * HEAD_DIM)
-        q = q_ref[:, cols]
-        scores = []
-        for j, (k_ref, _) in enumerate(blocks):
-            s = jnp.dot(q, k_ref[:, cols], preferred_element_type=jnp.float32) * scale
-            scores.append(jnp.where(slot < table_ref[j], s, -jnp.inf))
-        scores.append(lax.dot_general(q, ck[:, cols], dims, preferred_element_type=jnp.float32) * scale)
-        row_max = scores[0].max(axis=1, keepdims=True)
-        for s in scores[1:]:
-            row_max = jnp.maximum(row_max, s.max(axis=1, keepdims=True))
-        values = [v_ref for _, v_ref in blocks] + [cv]
-        denominator = jnp.zeros((rows, 1), jnp.float32)
-        attended = jnp.zeros((rows, HEAD_DIM), jnp.float32)
-        for s, v_ref in zip(scores, values):
-            p = jnp.exp(s - row_max)
-            denominator = denominator + p.sum(axis=1, keepdims=True)
-            attended = attended + jnp.dot(p.astype(jnp.bfloat16), v_ref[:, cols], preferred_element_type=jnp.float32)
+        s = jnp.dot(q_ref[:, cols], k1[:, cols], preferred_element_type=jnp.float32) * scale
+        s = jnp.where(slot < table_ref[1], s, -jnp.inf)
+        old_max = m_ref[:, h:h + 1]
+        new_max = jnp.maximum(old_max, s.max(axis=1, keepdims=True))
+        rescale = jnp.exp(old_max - new_max)
+        p = jnp.exp(s - new_max)
+        denominator = l_ref[:, h:h + 1] * rescale + p.sum(axis=1, keepdims=True)
+        attended = acc_ref[:, cols] * rescale + jnp.dot(p.astype(jnp.bfloat16), v1[:, cols], preferred_element_type=jnp.float32)
         attended = attended / denominator
-        out = jnp.where(live_row, attended * gate[:, cols], 0.0)
-        o_ref[:, cols] = out.astype(o_ref.dtype)
+        o_ref[:, cols] = jnp.where(live_row, attended * gate[:, cols], 0.0).astype(o_ref.dtype)
 
 
 def attend(table, queries, kv_own, kv_a, kv_b, kv_c, cache, gate_table):
@@ -58,25 +74,39 @@
     cache_k_block = pl.BlockSpec((cache_rows, width), lambda h, t: (0, h))
     cache_v_block = pl.BlockSpec((cache_rows, width), lambda h, t: (0, steps + h))
     gate_block = pl.BlockSpec((levels, width), lambda h, t: (0, h))
-    grid_spec = pltpu.PrefetchScalarGridSpec(
-        num_scalar_prefetch=1,
-        grid=(steps,),
-        in_specs=[row_block, k_block, v_block, k_block, v_block, k_block, v_block, k_block, v_block,
-                  cache_k_block, cache_v_block, gate_block],
-        out_specs=row_block,
-    )
-    keys = 4 * rows + cache_rows
-    cost = pl.CostEstimate(
-        flops=4 * rows * keys * feat,
-        transcendentals=rows * keys * (feat // HEAD_DIM),
-        bytes_accessed=2 * (2 * rows * feat + 8 * rows * feat + 2 * cache_rows * feat) + 4 * levels * feat,
-    )
+    stat_block = pl.BlockSpec((None, rows, HEADS_PER_STEP), lambda h, t: (h, 0, 0))
+    stat_shape = jax.ShapeDtypeStruct((steps, rows, HEADS_PER_STEP), jnp.float32)
+    keys = 3 * rows + cache_rows
+    m, l, acc = pl.pallas_call(
+        functools.partial(partial_kernel, heads=HEADS_PER_STEP),
+        out_shape=(stat_shape, stat_shape, jax.ShapeDtypeStruct((rows, feat), jnp.float32)),
+        grid_spec=pltpu.PrefetchScalarGridSpec(
+            num_scalar_prefetch=1,
+            grid=(steps,),
+            in_specs=[row_block, k_block, v_block, k_block, v_block, k_block, v_block, cache_k_block, cache_v_block],
+            out_specs=(stat_block, stat_block, row_block),
+        ),
+        cost_estimate=pl.CostEstimate(
+            flops=4 * rows * keys * feat,
+            transcendentals=rows * keys * (feat // HEAD_DIM),
+            bytes_accessed=2 * (7 * rows * feat + 2 * cache_rows * feat) + 4 * rows * feat,
+        ),
+    )(table, queries, kv_own, kv_own, kv_b, kv_b, kv_c, kv_c, cache, cache)
     return pl.pallas_call(
-        functools.partial(attention_kernel, heads=HEADS_PER_STEP),
+        functools.partial(finish_kernel, heads=HEADS_PER_STEP),
         out_shape=jax.ShapeDtypeStruct((rows, feat), jnp.bfloat16),
-        grid_spec=grid_spec,
-        cost_estimate=cost,
-    )(table, queries, kv_own, kv_own, kv_a, kv_a, kv_b, kv_b, kv_c, kv_c, cache, cache, gate_table)
+        grid_spec=pltpu.PrefetchScalarGridSpec(
+            num_scalar_prefetch=1,
+            grid=(steps,),
+            in_specs=[row_block, k_block, v_block, stat_block, stat_block, row_block, gate_block],
+            out_specs=row_block,
+        ),
+        cost_estimate=pl.CostEstimate(
+            flops=4 * rows * rows * feat,
+            transcendentals=rows * rows * (feat // HEAD_DIM),
+            bytes_accessed=2 * (4 * rows * feat) + 4 * rows * feat + 4 * levels * feat,
+        ),
+    )(table, queries, kv_a, kv_a, m, l, acc, gate_table)
 
 
 def gather_pieces(piece, size):

time: 75.7 us -> 75.5 us (level)
  Pallas kernels: 9.13 us -> 15.8 us
  waiting for transfers between devices: 39.3 us -> 34.4 us
  other arithmetic: 4.61 us -> 2.02 us
  local copies, waits for them, and re-layouts: 7.2 us -> 8.34 us
    pallas_call x1 -> x2, Pallas kernels: 9.13 us -> 15.8 us  [the longest x1 8.81 us: attend(): pl.pallas_call(functools.partial(finish_kernel, heads=HEADS_PER_STEP), ou...]
    ppermute x1, waiting for transfers between devices: 4.68 us -> 0.01 us  [body(): from_mixed = lax.ppermute(kv, 'group', pairs_mixed)]
    concatenate x3, other arithmetic: 2.81 us -> 0.28 us  [gather_pieces(): held = jnp.concatenate([held, other], 0)]
    unnamed x17 -> x23, local copies, waits for them, and re-layouts: 1.41 us -> 2.58 us
  transfers between devices with their start and end apart: 7 -> 7, of which waited for: 4 -> 3; matrix products, arithmetic and copies ran while one was open for 12% -> 9% of each run, Pallas kernels for 0% -> 9%
where the time goes in v12:
time: 75.5 us; the launch traced here: 74.7 us
  waiting for transfers between devices  34.4 us (46%)
  Pallas kernels  15.8 us (21%)
  starting transfers between devices  12.6 us (17%)
  local copies, waits for them, and re-layouts  8.34 us (11%)
  other arithmetic  2.02 us (3%)
  between operations  1.54 us (2%)
    ppermute x4, waiting for transfers between devices, gather_pieces(): other = lax.ppermute(held, 'group', [(i, i ^ step) for i in range(size)])  34.4 us
    pallas_call x1, Pallas kernels, attend(): pl.pallas_call(functools.partial(finish_kernel, heads=HEADS_PER_STEP), ou...  8.81 us
    ppermute x1, starting transfers between devices, body(): from_mixed = lax.ppermute(kv, 'group', pairs_mixed)  7.34 us
    pallas_call x1, Pallas kernels, attend(): pl.pallas_call(functools.partial(partial_kernel, heads=HEADS_PER_STEP), o...  6.98 us
    ppermute x1, starting transfers between devices, body(): from_two = lax.ppermute(kv, 'group', pairs_two)  3.18 us
    concatenate x1, local copies, waits for them, and re-layouts, gather_pieces(): held = jnp.concatenate([held, other], 0)  2.79 us
    unnamed x23, local copies, waits for them, and re-layouts  2.58 us
    ppermute x4, starting transfers between devices, gather_pieces(): other = lax.ppermute(held, 'group', [(i, i ^ step) for i in range(size)])  2 us
  transfers between devices with their start and end apart: 7, of which 3 were waited for; matrix products, arithmetic and copies ran while one was open for 9% of the time, Pallas kernels for 9%

profile of v12, /device:TPU:15, one launch (start us, length us, event | category | flops | bytes accessed | tf_op | source)
XLA Modules:
  0.0 74.7 jit_solution(5893018670012973966)
XLA Ops:
  0.0 1.3 %copy.14 = bf16[16,8,24,128]{3,2,1,0:T(8,128)(2,1)S(1)} copy(bf16[16,8,24,128]{3,1,2,0:T(8,128)(2,1)} %bitcast.10) | data formatting | bytes 1572864
  1.3 0.0 copy-start.3
  1.3 0.7 copy.13
  2.0 0.3 stack_reshape.3
  2.3 0.1 copy-done.3
  2.4 0.0 copy-start.7
  2.4 0.0 copy-start.8
  2.4 0.0 copy-start.9
  2.4 0.0 copy-start.10
  2.4 0.1 pad_maximum_fusion.k0.v0
  2.6 0.0 copy-start
  2.6 3.2 %collective-permute-start.5 = (bf16[2,128,3072]{2,1,0:T(8,128)(2,1)S(1)}, bf16[2,128,3072]{2,1,0:T(8,128)(2,1)}, u32[]{:S(2)}, u32[]{:S(2)}) collective-permute-start(bf16[2,128,3072]{2,1,0:T(8,128)(2,1)S(1)} %pad_maximum_fusion.k0.v0), channel_id=1, source_target_pairs={{0,2},{1,3},{2,4},{3,5},{4,6},{5,7},{6,8},{7,9},{8,10},{9,11},{10,... | collective-permute-start | bytes 4718600 | tf_op jit(solution)/shard_map/ppermute | solution.py:142
  6.5 0.6 fusion.1
  7.1 1.4 %scatter.9 = bf16[2,128]{1,0:T(2,128)(2,1)S(1)} dynamic-update-slice(bf16[2,128]{1,0:T(2,128)(2,1)S(1)} %scatter.6, bf16[1,1]{1,0:T(2,128)(2,1)} %bitcast.1, s32[]{:T(128)} %bitcast.2, s32[]{:T(128)} %bitcast.3) | dynamic-update-slice | bytes 8 | tf_op jit(solution)/shard_map/scatter | solution.py:131
  8.4 0.0 copy-done.7
  8.4 0.0 copy-done.8
  8.4 0.6 pad_maximum_fusion.4
  9.1 0.4 collective-permute-start
  9.5 30.0 %collective-permute-done = bf16[2,6272]{1,0:T(2,128)(2,1)S(1)} collective-permute-done((bf16[2,6272]{1,0:T(2,128)(2,1)}, bf16[2,6272]{1,0:T(2,128)(2,1)S(1)}, u32[]{:S(2)}, u32[]{:S(2)}) %collective-permute-start) | collective-permute-done | bytes 25120 | tf_op jit(solution)/shard_map/ppermute | solution.py:118
  39.5 0.0 copy-start.5
  39.5 0.1 pad_maximum_fusion.3
  39.6 0.1 collective-permute-start.1
  39.7 7.3 %collective-permute-start.4 = (bf16[2,128,3072]{2,1,0:T(8,128)(2,1)S(1)}, bf16[2,128,3072]{2,1,0:T(8,128)(2,1)S(1)}, u32[]{:S(2)}, u32[]{:S(2)}) collective-permute-start(bf16[2,128,3072]{2,1,0:T(8,128)(2,1)S(1)} %pad_maximum_fusion.k0.v0), channel_id=1, source_target_pairs={{0,1},{2,3},{4,5},{6,7},{8,9},{10,11},{12,13},{14,15},{1,4},{3,6},... | collective-permute-start | bytes 4718600 | tf_op jit(solution)/shard_map/ppermute | solution.py:143
  47.0 0.0 collective-permute-done.5.k2.v2
  47.0 0.1 collective-permute-start.6
  47.1 0.0 collective-permute-done.1
  47.1 0.0 copy-start.4
  47.1 0.1 pad_maximum_fusion.2
  47.2 0.1 collective-permute-start.2
  48.0 3.2 %collective-permute-done.2 = bf16[8,6272]{1,0:T(8,128)(2,1)S(1)} collective-permute-done((bf16[8,6272]{1,0:T(8,128)(2,1)S(1)}, bf16[8,6272]{1,0:T(8,128)(2,1)S(1)}, u32[]{:S(2)}, u32[]{:S(2)}) %collective-permute-start.2) | collective-permute-done | bytes 100384 | tf_op jit(solution)/shard_map/ppermute | solution.py:118
  51.2 0.0 copy-start.6
  51.2 0.1 pad_maximum_fusion.1
  51.4 1.4 %collective-permute-start.3 = (bf16[16,6272]{1,0:T(8,128)(2,1)S(1)}, bf16[16,6272]{1,0:T(8,128)(2,1)}, u32[]{:S(2)}, u32[]{:S(2)}) collective-permute-start(bf16[16,6272]{1,0:T(8,128)(2,1)S(1)} %pad_maximum_fusion.1), channel_id=1, source_target_pairs={{0,1},{1,0},{2,3},{3,2},{4,5},{5,4},{6,7},{7,6},{8,9},{9,8},{10,11... | collective-permute-start | bytes 602120 | tf_op jit(solution)/shard_map/ppermute | solution.py:118
  52.8 0.0 copy-done.9
  52.8 0.0 copy-done.10
  52.8 0.0 copy-done.5
  52.8 0.0 copy-done.4
  52.8 0.0 copy-done.6
  52.8 1.2 %collective-permute-done.3 = bf16[16,6272]{1,0:T(8,128)(2,1)} collective-permute-done((bf16[16,6272]{1,0:T(8,128)(2,1)S(1)}, bf16[16,6272]{1,0:T(8,128)(2,1)}, u32[]{:S(2)}, u32[]{:S(2)}) %collective-permute-start.3) | collective-permute-done | bytes 200736 | tf_op jit(solution)/shard_map/ppermute | solution.py:118
  54.0 2.8 %concatenate.29.ck.cv = bf16[32,6272]{1,0:T(8,128)(2,1)S(1)} concatenate(bf16[2,6272]{1,0:T(2,128)(2,1)} %pad_maximum_fusion.4, bf16[2,6272]{1,0:T(2,128)(2,1)} %copy-done.5, bf16[4,6272]{1,0:T(4,128)(2,1)} %copy-done.4, bf16[8,6272]{1,0:T(8,128)(2,1)} %copy-done.6, bf16[16,6272]{1,0:T(8,128)(2,1)} %collective-permute-done.3), dimensions={0} | concatenate | bytes 802816 | tf_op jit(solution)/shard_map/concatenate | solution.py:119
  56.8 0.0 copy-start.2
  56.8 0.2 convert_reduce_fusion.1
  57.0 0.2 select_reduce_fusion
  57.1 0.6 pad_add_fusion.table_ref
  57.8 0.0 collective-permute-done.6.k3.v3
  57.8 0.0 copy-done
  57.8 0.0 copy-done.2
  57.8 7.0 %shard_map.100 = (f32[3,128,8]{2,1,0:T(8,128)}, f32[3,128,8]{2,1,0:T(8,128)}, f32[128,3072]{1,0:T(8,128)}) custom-call(s32[5]{0:T(128)} %pad_add_fusion.table_ref, bf16[128,3072]{1,0:T(8,128)(2,1)} %q_ref.3, bf16[2,128,3072]{2,1,0:T(8,128)(2,1)} %copy-done, bf16[2,128,3072]{2,1,0:T(8,128)(2,1)} %copy-done, ...), custom_call_target="tpu_custom_call" | custom-call | flops 654311424 | bytes 7471104 | tf_op jit(solution)/shard_map/pallas_call | solution.py:80
  64.7 0.0 collective-permute-done.4.k1.v1
  64.8 0.0 copy-start.1
  64.8 1.2 %copy-done.1 = bf16[2,128,3072]{2,1,0:T(8,128)(2,1)} copy-done((bf16[2,128,3072]{2,1,0:T(8,128)(2,1)}, bf16[2,128,3072]{2,1,0:T(8,128)(2,1)S(1)}, u32[]{:S(2)}) %copy-start.1) | copy-done | bytes 1572888
  65.9 8.8 %shard_map.101 = bf16[128,3072]{1,0:T(8,128)(2,1)} custom-call(s32[5]{0:T(128)} %pad_add_fusion.table_ref, bf16[128,3072]{1,0:T(8,128)(2,1)} %q_ref.3, bf16[2,128,3072]{2,1,0:T(8,128)(2,1)} %copy-done.1, bf16[2,128,3072]{2,1,0:T(8,128)(2,1)} %copy-done.1, f32[3,128,8]{2,1,0:T(8,128)} %get-tuple-element.32.m_ref, f32[3,128,8]{2,1,0:T(8,128)} %get-tuple-element.33.l_ref, ...), custom_call_target="tpu_custom_call" | custom-call | flops 201326592 | bytes 4915200 | tf_op jit(solution)/shard_map/pallas_call | solution.py:95
  (3 shorter events, 0.0 us)
Async XLA Ops:
  1.3 1.1 %copy-start.3 = (bf16[128,3072]{1,0:T(8,128)(2,1)S(1)}, bf16[128,3072]{1,0:T(8,128)(2,1)}, u32[]{:S(2)}) copy-start(bf16[128,3072]{1,0:T(8,128)(2,1)} %param.16) | copy-start | bytes 2359300
  2.4 6.0 %copy-start.7 = (bf16[2,3072]{1,0:T(2,128)(2,1)S(1)}, bf16[2,3072]{1,0:T(2,128)(2,1)}, u32[]{:S(2)}) copy-start(bf16[2,3072]{1,0:T(2,128)(2,1)} %param.18) | copy-start | bytes 36868
  2.4 6.0 %copy-start.8 = (bf16[2,3072]{1,0:T(2,128)(2,1)S(1)}, bf16[2,3072]{1,0:T(2,128)(2,1)}, u32[]{:S(2)}) copy-start(bf16[2,3072]{1,0:T(2,128)(2,1)} %param.17) | copy-start | bytes 36868
  2.4 50.3 %copy-start.9 = (s32[3]{0:T(128)S(1)}, s32[3]{0:T(128)}, u32[]{:S(2)}) copy-start(s32[3]{0:T(128)} %constant.76.clone) | copy-start | bytes 40
  2.4 50.3 %copy-start.10 = (s32[3]{0:T(128)S(1)}, s32[3]{0:T(128)}, u32[]{:S(2)}) copy-start(s32[3]{0:T(128)} %constant.75.clone) | copy-start | bytes 40
  2.6 55.2 %copy-start = (bf16[2,128,3072]{2,1,0:T(8,128)(2,1)}, bf16[2,128,3072]{2,1,0:T(8,128)(2,1)S(1)}, u32[]{:S(2)}) copy-start(bf16[2,128,3072]{2,1,0:T(8,128)(2,1)S(1)} %pad_maximum_fusion.k0.v0) | copy-start | bytes 4718596
  2.6 44.4 %collective-permute-start.5 = (bf16[2,128,3072]{2,1,0:T(8,128)(2,1)S(1)}, bf16[2,128,3072]{2,1,0:T(8,128)(2,1)}, u32[]{:S(2)}, u32[]{:S(2)}) collective-permute-start(bf16[2,128,3072]{2,1,0:T(8,128)(2,1)S(1)} %pad_maximum_fusion.k0.v0), channel_id=1, source_target_pairs={{0,2},{1,3},{2,4},{3,5},{4,6},{5,7},{6,8},{7,9},{8,10},{9,11},{10,... | collective-permute-start | bytes 4718600 | tf_op jit(solution)/shard_map/ppermute | solution.py:142
  9.1 30.4 %collective-permute-start = (bf16[2,6272]{1,0:T(2,128)(2,1)}, bf16[2,6272]{1,0:T(2,128)(2,1)S(1)}, u32[]{:S(2)}, u32[]{:S(2)}) collective-permute-start(bf16[2,6272]{1,0:T(2,128)(2,1)} %pad_maximum_fusion.4), channel_id=1, source_target_pairs={{0,8},{1,9},{2,10},{3,11},{4,12},{5,13},{6,14},{7,15},{8,0},{9,1},... | collective-permute-start | bytes 75272 | tf_op jit(solution)/shard_map/ppermute | solution.py:118
  39.5 13.3 %copy-start.5 = (bf16[2,6272]{1,0:T(2,128)(2,1)}, bf16[2,6272]{1,0:T(2,128)(2,1)S(1)}, u32[]{:S(2)}) copy-start(bf16[2,6272]{1,0:T(2,128)(2,1)S(1)} %collective-permute-done) | copy-start | bytes 75268
  39.6 7.6 %collective-permute-start.1 = (bf16[4,6272]{1,0:T(4,128)(2,1)S(1)}, bf16[4,6272]{1,0:T(4,128)(2,1)S(1)}, u32[]{:S(2)}, u32[]{:S(2)}) collective-permute-start(bf16[4,6272]{1,0:T(4,128)(2,1)S(1)} %pad_maximum_fusion.3), channel_id=1, source_target_pairs={{0,4},{1,5},{2,6},{3,7},{4,0},{5,1},{6,2},{7,3},{8,12},{9,13},{10,... | collective-permute-start | bytes 150536 | tf_op jit(solution)/shard_map/ppermute | solution.py:118
  39.7 25.1 %collective-permute-start.4 = (bf16[2,128,3072]{2,1,0:T(8,128)(2,1)S(1)}, bf16[2,128,3072]{2,1,0:T(8,128)(2,1)S(1)}, u32[]{:S(2)}, u32[]{:S(2)}) collective-permute-start(bf16[2,128,3072]{2,1,0:T(8,128)(2,1)S(1)} %pad_maximum_fusion.k0.v0), channel_id=1, source_target_pairs={{0,1},{2,3},{4,5},{6,7},{8,9},{10,11},{12,13},{14,15},{1,4},{3,6},... | collective-permute-start | bytes 4718600 | tf_op jit(solution)/shard_map/ppermute | solution.py:143
  47.0 10.7 %collective-permute-start.6 = (bf16[2,128,3072]{2,1,0:T(8,128)(2,1)}, bf16[2,128,3072]{2,1,0:T(8,128)(2,1)}, u32[]{:S(2)}, u32[]{:S(2)}) collective-permute-start(bf16[2,128,3072]{2,1,0:T(8,128)(2,1)} %collective-permute-done.5.k2.v2), channel_id=1, source_target_pairs={{0,1},{1,0},{2,3},{3,2},{4,5},{5,4},{6,7},{7,6},{8,9},{9,8},{10,11... | collective-permute-start | bytes 4718600 | tf_op jit(solution)/shard_map/ppermute | solution.py:145
  47.1 5.7 %copy-start.4 = (bf16[4,6272]{1,0:T(4,128)(2,1)}, bf16[4,6272]{1,0:T(4,128)(2,1)S(1)}, u32[]{:S(2)}) copy-start(bf16[4,6272]{1,0:T(4,128)(2,1)S(1)} %collective-permute-done.1) | copy-start | bytes 150532
  47.2 4.0 %collective-permute-start.2 = (bf16[8,6272]{1,0:T(8,128)(2,1)S(1)}, bf16[8,6272]{1,0:T(8,128)(2,1)S(1)}, u32[]{:S(2)}, u32[]{:S(2)}) collective-permute-start(bf16[8,6272]{1,0:T(8,128)(2,1)S(1)} %pad_maximum_fusion.2), channel_id=1, source_target_pairs={{0,2},{1,3},{2,0},{3,1},{4,6},{5,7},{6,4},{7,5},{8,10},{9,11},{10,... | collective-permute-start | bytes 301064 | tf_op jit(solution)/shard_map/ppermute | solution.py:118
  51.2 1.6 %copy-start.6 = (bf16[8,6272]{1,0:T(8,128)(2,1)}, bf16[8,6272]{1,0:T(8,128)(2,1)S(1)}, u32[]{:S(2)}) copy-start(bf16[8,6272]{1,0:T(8,128)(2,1)S(1)} %collective-permute-done.2) | copy-start | bytes 301060
  51.4 2.6 %collective-permute-start.3 = (bf16[16,6272]{1,0:T(8,128)(2,1)S(1)}, bf16[16,6272]{1,0:T(8,128)(2,1)}, u32[]{:S(2)}, u32[]{:S(2)}) collective-permute-start(bf16[16,6272]{1,0:T(8,128)(2,1)S(1)} %pad_maximum_fusion.1), channel_id=1, source_target_pairs={{0,1},{1,0},{2,3},{3,2},{4,5},{5,4},{6,7},{7,6},{8,9},{9,8},{10,11... | collective-permute-start | bytes 602120 | tf_op jit(solution)/shard_map/ppermute | solution.py:118
  56.8 1.0 %copy-start.2 = (bf16[32,6272]{1,0:T(8,128)(2,1)}, bf16[32,6272]{1,0:T(8,128)(2,1)S(1)}, u32[]{:S(2)}) copy-start(bf16[32,6272]{1,0:T(8,128)(2,1)S(1)} %concatenate.29.ck.cv) | copy-start | bytes 1204228
  64.8 1.2 %copy-start.1 = (bf16[2,128,3072]{2,1,0:T(8,128)(2,1)}, bf16[2,128,3072]{2,1,0:T(8,128)(2,1)S(1)}, u32[]{:S(2)}) copy-start(bf16[2,128,3072]{2,1,0:T(8,128)(2,1)S(1)} %collective-permute-done.4.k1.v1) | copy-start | bytes 4718596

commit v13 on v12

--- a/solution.py
+++ b/solution.py
@@ -10,7 +10,7 @@
 
 HEAD_DIM = 128
 WIN = 4
-HEADS_PER_STEP = 8
+HEADS_PER_STEP = 4
 
 
 def partial_kernel(table_ref, q_ref, k0, v0, k2, v2, k3, v3, ck, cv, m_ref, l_ref, acc_ref, *, heads):

time: 75.5 us -> 75.7 us (level)
    pallas_call x1, Pallas kernels: 6.98 us -> 8.23 us  [attend(): pl.pallas_call(functools.partial(partial_kernel, heads=HEADS_PER_STEP), o...]
    pallas_call x1, Pallas kernels: 8.81 us -> 7.8 us  [attend(): pl.pallas_call(functools.partial(finish_kernel, heads=HEADS_PER_STEP), ou...]
  transfers between devices with their start and end apart: 7 -> 7, of which waited for: 3 -> 3; matrix products, arithmetic and copies ran while one was open for 9% -> 9% of each run, Pallas kernels for 9% -> 11%
where the time goes in v13:
time: 75.7 us; the launch traced here: 75 us
  waiting for transfers between devices  34.4 us (45%)
  Pallas kernels  16 us (21%)
  starting transfers between devices  12.6 us (17%)
  local copies, waits for them, and re-layouts  8.34 us (11%)
  other arithmetic  2.08 us (3%)
  between operations  1.54 us (2%)
    ppermute x4, waiting for transfers between devices, gather_pieces(): other = lax.ppermute(held, 'group', [(i, i ^ step) for i in range(size)])  34.4 us
    pallas_call x1, Pallas kernels, attend(): pl.pallas_call(functools.partial(partial_kernel, heads=HEADS_PER_STEP), o...  8.23 us
    pallas_call x1, Pallas kernels, attend(): pl.pallas_call(functools.partial(finish_kernel, heads=HEADS_PER_STEP), ou...  7.8 us
    ppermute x1, starting transfers between devices, body(): from_mixed = lax.ppermute(kv, 'group', pairs_mixed)  7.34 us
    ppermute x1, starting transfers between devices, body(): from_two = lax.ppermute(kv, 'group', pairs_two)  3.18 us
    concatenate x1, local copies, waits for them, and re-layouts, gather_pieces(): held = jnp.concatenate([held, other], 0)  2.79 us
    unnamed x23, local copies, waits for them, and re-layouts  2.58 us
    ppermute x4, starting transfers between devices, gather_pieces(): other = lax.ppermute(held, 'group', [(i, i ^ step) for i in range(size)])  2 us
  transfers between devices with their start and end apart: 7, of which 3 were waited for; matrix products, arithmetic and copies ran while one was open for 9% of the time, Pallas kernels for 11%

profile of v13, /device:TPU:15, one launch (start us, length us, event | category | flops | bytes accessed | tf_op | source)
XLA Modules:
  0.0 75.0 jit_solution(2848238223131464631)
XLA Ops:
  0.0 1.3 %copy.14 = bf16[16,8,24,128]{3,2,1,0:T(8,128)(2,1)S(1)} copy(bf16[16,8,24,128]{3,1,2,0:T(8,128)(2,1)} %bitcast.10) | data formatting | bytes 1572864
  1.3 0.0 copy-start.3
  1.3 0.7 copy.13
  2.0 0.3 stack_reshape.3
  2.3 0.1 copy-done.3
  2.4 0.0 copy-start.7
  2.4 0.0 copy-start.8
  2.4 0.0 copy-start.9
  2.4 0.0 copy-start.10
  2.4 0.1 pad_maximum_fusion.k0.v0
  2.6 0.0 copy-start
  2.6 3.2 %collective-permute-start.5 = (bf16[2,128,3072]{2,1,0:T(8,128)(2,1)S(1)}, bf16[2,128,3072]{2,1,0:T(8,128)(2,1)}, u32[]{:S(2)}, u32[]{:S(2)}) collective-permute-start(bf16[2,128,3072]{2,1,0:T(8,128)(2,1)S(1)} %pad_maximum_fusion.k0.v0), channel_id=1, source_target_pairs={{0,2},{1,3},{2,4},{3,5},{4,6},{5,7},{6,8},{7,9},{8,10},{9,11},{10,... | collective-permute-start | bytes 4718600 | tf_op jit(solution)/shard_map/ppermute | solution.py:142
  6.5 0.6 fusion.1
  7.1 1.4 %scatter.9 = bf16[2,128]{1,0:T(2,128)(2,1)S(1)} dynamic-update-slice(bf16[2,128]{1,0:T(2,128)(2,1)S(1)} %scatter.6, bf16[1,1]{1,0:T(2,128)(2,1)} %bitcast.1, s32[]{:T(128)} %bitcast.2, s32[]{:T(128)} %bitcast.3) | dynamic-update-slice | bytes 8 | tf_op jit(solution)/shard_map/scatter | solution.py:131
  8.4 0.0 copy-done.7
  8.4 0.0 copy-done.8
  8.4 0.6 pad_maximum_fusion.4
  9.1 0.4 collective-permute-start
  9.5 30.0 %collective-permute-done = bf16[2,6272]{1,0:T(2,128)(2,1)S(1)} collective-permute-done((bf16[2,6272]{1,0:T(2,128)(2,1)}, bf16[2,6272]{1,0:T(2,128)(2,1)S(1)}, u32[]{:S(2)}, u32[]{:S(2)}) %collective-permute-start) | collective-permute-done | bytes 25120 | tf_op jit(solution)/shard_map/ppermute | solution.py:118
  39.5 0.0 copy-start.5
  39.5 0.1 pad_maximum_fusion.3
  39.6 0.1 collective-permute-start.1
  39.7 7.3 %collective-permute-start.4 = (bf16[2,128,3072]{2,1,0:T(8,128)(2,1)S(1)}, bf16[2,128,3072]{2,1,0:T(8,128)(2,1)S(1)}, u32[]{:S(2)}, u32[]{:S(2)}) collective-permute-start(bf16[2,128,3072]{2,1,0:T(8,128)(2,1)S(1)} %pad_maximum_fusion.k0.v0), channel_id=1, source_target_pairs={{0,1},{2,3},{4,5},{6,7},{8,9},{10,11},{12,13},{14,15},{1,4},{3,6},... | collective-permute-start | bytes 4718600 | tf_op jit(solution)/shard_map/ppermute | solution.py:143
  47.0 0.0 collective-permute-done.5.k2.v2
  47.0 0.1 collective-permute-start.6
  47.1 0.0 collective-permute-done.1
  47.1 0.0 copy-start.4
  47.1 0.1 pad_maximum_fusion.2
  47.2 0.1 collective-permute-start.2
  48.0 3.2 %collective-permute-done.2 = bf16[8,6272]{1,0:T(8,128)(2,1)S(1)} collective-permute-done((bf16[8,6272]{1,0:T(8,128)(2,1)S(1)}, bf16[8,6272]{1,0:T(8,128)(2,1)S(1)}, u32[]{:S(2)}, u32[]{:S(2)}) %collective-permute-start.2) | collective-permute-done | bytes 100384 | tf_op jit(solution)/shard_map/ppermute | solution.py:118
  51.2 0.0 copy-start.6
  51.2 0.1 pad_maximum_fusion.1
  51.4 1.4 %collective-permute-start.3 = (bf16[16,6272]{1,0:T(8,128)(2,1)S(1)}, bf16[16,6272]{1,0:T(8,128)(2,1)}, u32[]{:S(2)}, u32[]{:S(2)}) collective-permute-start(bf16[16,6272]{1,0:T(8,128)(2,1)S(1)} %pad_maximum_fusion.1), channel_id=1, source_target_pairs={{0,1},{1,0},{2,3},{3,2},{4,5},{5,4},{6,7},{7,6},{8,9},{9,8},{10,11... | collective-permute-start | bytes 602120 | tf_op jit(solution)/shard_map/ppermute | solution.py:118
  52.8 0.0 copy-done.9
  52.8 0.0 copy-done.10
  52.8 0.0 copy-done.5
  52.8 0.0 copy-done.4
  52.8 0.0 copy-done.6
  52.8 1.2 %collective-permute-done.3 = bf16[16,6272]{1,0:T(8,128)(2,1)} collective-permute-done((bf16[16,6272]{1,0:T(8,128)(2,1)S(1)}, bf16[16,6272]{1,0:T(8,128)(2,1)}, u32[]{:S(2)}, u32[]{:S(2)}) %collective-permute-start.3) | collective-permute-done | bytes 200736 | tf_op jit(solution)/shard_map/ppermute | solution.py:118
  54.0 2.8 %concatenate.29.ck.cv = bf16[32,6272]{1,0:T(8,128)(2,1)S(1)} concatenate(bf16[2,6272]{1,0:T(2,128)(2,1)} %pad_maximum_fusion.4, bf16[2,6272]{1,0:T(2,128)(2,1)} %copy-done.5, bf16[4,6272]{1,0:T(4,128)(2,1)} %copy-done.4, bf16[8,6272]{1,0:T(8,128)(2,1)} %copy-done.6, bf16[16,6272]{1,0:T(8,128)(2,1)} %collective-permute-done.3), dimensions={0} | concatenate | bytes 802816 | tf_op jit(solution)/shard_map/concatenate | solution.py:119
  56.8 0.0 copy-start.2
  56.8 0.2 convert_reduce_fusion.1
  57.0 0.2 select_reduce_fusion
  57.1 0.7 pad_add_fusion.table_ref
  57.8 0.0 collective-permute-done.6.k3.v3
  57.8 0.0 copy-done
  57.8 0.0 copy-done.2
  57.8 8.2 %shard_map.100 = (f32[6,128,4]{2,1,0:T(8,128)}, f32[6,128,4]{2,1,0:T(8,128)}, f32[128,3072]{1,0:T(8,128)}) custom-call(s32[5]{0:T(128)} %pad_add_fusion.table_ref, bf16[128,3072]{1,0:T(8,128)(2,1)} %q_ref.3, bf16[2,128,3072]{2,1,0:T(8,128)(2,1)} %copy-done, bf16[2,128,3072]{2,1,0:T(8,128)(2,1)} %copy-done, ...), custom_call_target="tpu_custom_call" | custom-call | flops 654311424 | bytes 7471104 | tf_op jit(solution)/shard_map/pallas_call | solution.py:80
  66.1 0.0 collective-permute-done.4.k1.v1
  66.1 0.0 copy-start.1
  66.1 1.2 %copy-done.1 = bf16[2,128,3072]{2,1,0:T(8,128)(2,1)} copy-done((bf16[2,128,3072]{2,1,0:T(8,128)(2,1)}, bf16[2,128,3072]{2,1,0:T(8,128)(2,1)S(1)}, u32[]{:S(2)}) %copy-start.1) | copy-done | bytes 1572888
  67.2 7.8 %shard_map.101 = bf16[128,3072]{1,0:T(8,128)(2,1)} custom-call(s32[5]{0:T(128)} %pad_add_fusion.table_ref, bf16[128,3072]{1,0:T(8,128)(2,1)} %q_ref.3, bf16[2,128,3072]{2,1,0:T(8,128)(2,1)} %copy-done.1, bf16[2,128,3072]{2,1,0:T(8,128)(2,1)} %copy-done.1, f32[6,128,4]{2,1,0:T(8,128)} %get-tuple-element.32.m_ref, f32[6,128,4]{2,1,0:T(8,128)} %get-tuple-element.33.l_ref, ...), custom_call_target="tpu_custom_call" | custom-call | flops 201326592 | bytes 4915200 | tf_op jit(solution)/shard_map/pallas_call | solution.py:95
  (3 shorter events, 0.0 us)
Async XLA Ops:
  1.3 1.1 %copy-start.3 = (bf16[128,3072]{1,0:T(8,128)(2,1)S(1)}, bf16[128,3072]{1,0:T(8,128)(2,1)}, u32[]{:S(2)}) copy-start(bf16[128,3072]{1,0:T(8,128)(2,1)} %param.16) | copy-start | bytes 2359300
  2.4 6.0 %copy-start.7 = (bf16[2,3072]{1,0:T(2,128)(2,1)S(1)}, bf16[2,3072]{1,0:T(2,128)(2,1)}, u32[]{:S(2)}) copy-start(bf16[2,3072]{1,0:T(2,128)(2,1)} %param.18) | copy-start | bytes 36868
  2.4 6.0 %copy-start.8 = (bf16[2,3072]{1,0:T(2,128)(2,1)S(1)}, bf16[2,3072]{1,0:T(2,128)(2,1)}, u32[]{:S(2)}) copy-start(bf16[2,3072]{1,0:T(2,128)(2,1)} %param.17) | copy-start | bytes 36868
  2.4 50.3 %copy-start.9 = (s32[3]{0:T(128)S(1)}, s32[3]{0:T(128)}, u32[]{:S(2)}) copy-start(s32[3]{0:T(128)} %constant.76.clone) | copy-start | bytes 40
  2.4 50.3 %copy-start.10 = (s32[3]{0:T(128)S(1)}, s32[3]{0:T(128)}, u32[]{:S(2)}) copy-start(s32[3]{0:T(128)} %constant.75.clone) | copy-start | bytes 40
  2.6 55.2 %copy-start = (bf16[2,128,3072]{2,1,0:T(8,128)(2,1)}, bf16[2,128,3072]{2,1,0:T(8,128)(2,1)S(1)}, u32[]{:S(2)}) copy-start(bf16[2,128,3072]{2,1,0:T(8,128)(2,1)S(1)} %pad_maximum_fusion.k0.v0) | copy-start | bytes 4718596
  2.6 44.4 %collective-permute-start.5 = (bf16[2,128,3072]{2,1,0:T(8,128)(2,1)S(1)}, bf16[2,128,3072]{2,1,0:T(8,128)(2,1)}, u32[]{:S(2)}, u32[]{:S(2)}) collective-permute-start(bf16[2,128,3072]{2,1,0:T(8,128)(2,1)S(1)} %pad_maximum_fusion.k0.v0), channel_id=1, source_target_pairs={{0,2},{1,3},{2,4},{3,5},{4,6},{5,7},{6,8},{7,9},{8,10},{9,11},{10,... | collective-permute-start | bytes 4718600 | tf_op jit(solution)/shard_map/ppermute | solution.py:142
  9.1 30.4 %collective-permute-start = (bf16[2,6272]{1,0:T(2,128)(2,1)}, bf16[2,6272]{1,0:T(2,128)(2,1)S(1)}, u32[]{:S(2)}, u32[]{:S(2)}) collective-permute-start(bf16[2,6272]{1,0:T(2,128)(2,1)} %pad_maximum_fusion.4), channel_id=1, source_target_pairs={{0,8},{1,9},{2,10},{3,11},{4,12},{5,13},{6,14},{7,15},{8,0},{9,1},... | collective-permute-start | bytes 75272 | tf_op jit(solution)/shard_map/ppermute | solution.py:118
  39.5 13.3 %copy-start.5 = (bf16[2,6272]{1,0:T(2,128)(2,1)}, bf16[2,6272]{1,0:T(2,128)(2,1)S(1)}, u32[]{:S(2)}) copy-start(bf16[2,6272]{1,0:T(2,128)(2,1)S(1)} %collective-permute-done) | copy-start | bytes 75268
  39.6 7.6 %collective-permute-start.1 = (bf16[4,6272]{1,0:T(4,128)(2,1)S(1)}, bf16[4,6272]{1,0:T(4,128)(2,1)S(1)}, u32[]{:S(2)}, u32[]{:S(2)}) collective-permute-start(bf16[4,6272]{1,0:T(4,128)(2,1)S(1)} %pad_maximum_fusion.3), channel_id=1, source_target_pairs={{0,4},{1,5},{2,6},{3,7},{4,0},{5,1},{6,2},{7,3},{8,12},{9,13},{10,... | collective-permute-start | bytes 150536 | tf_op jit(solution)/shard_map/ppermute | solution.py:118
  39.7 26.4 %collective-permute-start.4 = (bf16[2,128,3072]{2,1,0:T(8,128)(2,1)S(1)}, bf16[2,128,3072]{2,1,0:T(8,128)(2,1)S(1)}, u32[]{:S(2)}, u32[]{:S(2)}) collective-permute-start(bf16[2,128,3072]{2,1,0:T(8,128)(2,1)S(1)} %pad_maximum_fusion.k0.v0), channel_id=1, source_target_pairs={{0,1},{2,3},{4,5},{6,7},{8,9},{10,11},{12,13},{14,15},{1,4},{3,6},... | collective-permute-start | bytes 4718600 | tf_op jit(solution)/shard_map/ppermute | solution.py:143
  47.0 10.8 %collective-permute-start.6 = (bf16[2,128,3072]{2,1,0:T(8,128)(2,1)}, bf16[2,128,3072]{2,1,0:T(8,128)(2,1)}, u32[]{:S(2)}, u32[]{:S(2)}) collective-permute-start(bf16[2,128,3072]{2,1,0:T(8,128)(2,1)} %collective-permute-done.5.k2.v2), channel_id=1, source_target_pairs={{0,1},{1,0},{2,3},{3,2},{4,5},{5,4},{6,7},{7,6},{8,9},{9,8},{10,11... | collective-permute-start | bytes 4718600 | tf_op jit(solution)/shard_map/ppermute | solution.py:145
  47.1 5.7 %copy-start.4 = (bf16[4,6272]{1,0:T(4,128)(2,1)}, bf16[4,6272]{1,0:T(4,128)(2,1)S(1)}, u32[]{:S(2)}) copy-start(bf16[4,6272]{1,0:T(4,128)(2,1)S(1)} %collective-permute-done.1) | copy-start | bytes 150532
  47.2 4.0 %collective-permute-start.2 = (bf16[8,6272]{1,0:T(8,128)(2,1)S(1)}, bf16[8,6272]{1,0:T(8,128)(2,1)S(1)}, u32[]{:S(2)}, u32[]{:S(2)}) collective-permute-start(bf16[8,6272]{1,0:T(8,128)(2,1)S(1)} %pad_maximum_fusion.2), channel_id=1, source_target_pairs={{0,2},{1,3},{2,0},{3,1},{4,6},{5,7},{6,4},{7,5},{8,10},{9,11},{10,... | collective-permute-start | bytes 301064 | tf_op jit(solution)/shard_map/ppermute | solution.py:118
  51.2 1.6 %copy-start.6 = (bf16[8,6272]{1,0:T(8,128)(2,1)}, bf16[8,6272]{1,0:T(8,128)(2,1)S(1)}, u32[]{:S(2)}) copy-start(bf16[8,6272]{1,0:T(8,128)(2,1)S(1)} %collective-permute-done.2) | copy-start | bytes 301060
  51.4 2.6 %collective-permute-start.3 = (bf16[16,6272]{1,0:T(8,128)(2,1)S(1)}, bf16[16,6272]{1,0:T(8,128)(2,1)}, u32[]{:S(2)}, u32[]{:S(2)}) collective-permute-start(bf16[16,6272]{1,0:T(8,128)(2,1)S(1)} %pad_maximum_fusion.1), channel_id=1, source_target_pairs={{0,1},{1,0},{2,3},{3,2},{4,5},{5,4},{6,7},{7,6},{8,9},{9,8},{10,11... | collective-permute-start | bytes 602120 | tf_op jit(solution)/shard_map/ppermute | solution.py:118
  56.8 1.1 %copy-start.2 = (bf16[32,6272]{1,0:T(8,128)(2,1)}, bf16[32,6272]{1,0:T(8,128)(2,1)S(1)}, u32[]{:S(2)}) copy-start(bf16[32,6272]{1,0:T(8,128)(2,1)S(1)} %concatenate.29.ck.cv) | copy-start | bytes 1204228
  66.1 1.2 %copy-start.1 = (bf16[2,128,3072]{2,1,0:T(8,128)(2,1)}, bf16[2,128,3072]{2,1,0:T(8,128)(2,1)S(1)}, u32[]{:S(2)}) copy-start(bf16[2,128,3072]{2,1,0:T(8,128)(2,1)S(1)} %collective-permute-done.4.k1.v1) | copy-start | bytes 4718596

commit v14 on v11

--- a/solution.py
+++ b/solution.py
@@ -23,24 +23,30 @@
     live_row = row < table_ref[0]
     blocks = ((k0, v0), (k1, v1), (k2, v2), (k3, v3))
     dims = (((1,), (1,)), ((), ()))
-    for h in range(heads):
-        cols = slice(h * HEAD_DIM, (h + 1) * HEAD_DIM)
+    head_cols = [slice(h * HEAD_DIM, (h + 1) * HEAD_DIM) for h in range(heads)]
+    all_scores = []
+    for cols in head_cols:
         q = q_ref[:, cols]
         scores = []
         for j, (k_ref, _) in enumerate(blocks):
             s = jnp.dot(q, k_ref[:, cols], preferred_element_type=jnp.float32) * scale
             scores.append(jnp.where(slot < table_ref[j], s, -jnp.inf))
         scores.append(lax.dot_general(q, ck[:, cols], dims, preferred_element_type=jnp.float32) * scale)
-        row_max = scores[0].max(axis=1, keepdims=True)
-        for s in scores[1:]:
-            row_max = jnp.maximum(row_max, s.max(axis=1, keepdims=True))
+        all_scores.append(scores)
+    all_probabilities = []
+    all_denominators = []
+    for scores in all_scores:
+        window = jnp.maximum(jnp.maximum(scores[0], scores[1]), jnp.maximum(scores[2], scores[3]))
+        row_max = jnp.maximum(window.max(axis=1, keepdims=True), scores[4].max(axis=1, keepdims=True))
+        probabilities = [jnp.exp(s - row_max) for s in scores]
+        window_sum = (probabilities[0] + probabilities[1]) + (probabilities[2] + probabilities[3])
+        all_denominators.append(window_sum.sum(axis=1, keepdims=True) + probabilities[4].sum(axis=1, keepdims=True))
+        all_probabilities.append([p.astype(jnp.bfloat16) for p in probabilities])
+    for cols, weights, denominator in zip(head_cols, all_probabilities, all_denominators):
         values = [v_ref for _, v_ref in blocks] + [cv]
-        denominator = jnp.zeros((rows, 1), jnp.float32)
         attended = jnp.zeros((rows, HEAD_DIM), jnp.float32)
-        for s, v_ref in zip(scores, values):
-            p = jnp.exp(s - row_max)
-            denominator = denominator + p.sum(axis=1, keepdims=True)
-            attended = attended + jnp.dot(p.astype(jnp.bfloat16), v_ref[:, cols], preferred_element_type=jnp.float32)
+        for w, v_ref in zip(weights, values):
+            attended = attended + jnp.dot(w, v_ref[:, cols], preferred_element_type=jnp.float32)
         attended = attended / denominator
         out = jnp.where(live_row, attended * gate[:, cols], 0.0)
         o_ref[:, cols] = out.astype(o_ref.dtype)

time: 75.7 us -> 74.3 us (0.982)
  Pallas kernels: 9.13 us -> 7.67 us
    pallas_call x1, Pallas kernels: 9.13 us -> 7.67 us  [attend(): pl.pallas_call(functools.partial(attention_kernel, heads=HEADS_PER_STEP),...]
  transfers between devices with their start and end apart: 7 -> 7, of which waited for: 4 -> 4; matrix products, arithmetic and copies ran while one was open for 12% -> 13% of each run, Pallas kernels for 0% -> 0%
where the time goes in v14:
time: 74.3 us; the launch traced here: 72.9 us
  waiting for transfers between devices  39.3 us (53%)
  starting transfers between devices  12.7 us (17%)
  Pallas kernels  7.67 us (10%)
  local copies, waits for them, and re-layouts  7.2 us (10%)
  other arithmetic  4.61 us (6%)
  between operations  1.5 us (2%)
    ppermute x4, waiting for transfers between devices, gather_pieces(): other = lax.ppermute(held, 'group', [(i, i ^ step) for i in range(size)])  34.6 us
    pallas_call x1, Pallas kernels, attend(): pl.pallas_call(functools.partial(attention_kernel, heads=HEADS_PER_STEP),...  7.67 us
    ppermute x1, starting transfers between devices, body(): from_mixed = lax.ppermute(kv, 'group', pairs_mixed)  7.45 us
    ppermute x1, waiting for transfers between devices, body(): from_mixed = lax.ppermute(kv, 'group', pairs_mixed)  4.68 us
    ppermute x1, starting transfers between devices, body(): from_two = lax.ppermute(kv, 'group', pairs_two)  3.18 us
    concatenate x3, other arithmetic, gather_pieces(): held = jnp.concatenate([held, other], 0)  2.81 us
    concatenate x1, local copies, waits for them, and re-layouts, gather_pieces(): held = jnp.concatenate([held, other], 0)  2.79 us
    ppermute x4, starting transfers between devices, gather_pieces(): other = lax.ppermute(held, 'group', [(i, i ^ step) for i in range(size)])  1.95 us
  transfers between devices with their start and end apart: 7, of which 4 were waited for; matrix products, arithmetic and copies ran while one was open for 13% of the time, Pallas kernels for 0%

profile of v14, /device:TPU:15, one launch (start us, length us, event | category | flops | bytes accessed | tf_op | source)
XLA Modules:
  0.0 72.9 jit_solution(3938308277439690421)
XLA Ops:
  0.0 1.3 %copy.14 = bf16[16,8,24,128]{3,2,1,0:T(8,128)(2,1)S(1)} copy(bf16[16,8,24,128]{3,1,2,0:T(8,128)(2,1)} %bitcast.10) | data formatting | bytes 1572864
  1.3 0.0 copy-start.3
  1.3 0.7 copy.13
  2.0 0.3 stack_reshape.3
  2.3 0.1 copy-done.3
  2.4 0.0 copy-start.4
  2.4 0.0 copy-start.5
  2.4 0.0 copy-start.6
  2.4 0.0 copy-start.7
  2.4 0.1 pad_maximum_fusion.k0.v0
  2.6 0.0 copy-start
  2.6 3.2 %collective-permute-start.5 = (bf16[2,128,3072]{2,1,0:T(8,128)(2,1)S(1)}, bf16[2,128,3072]{2,1,0:T(8,128)(2,1)S(1)}, u32[]{:S(2)}, u32[]{:S(2)}) collective-permute-start(bf16[2,128,3072]{2,1,0:T(8,128)(2,1)S(1)} %pad_maximum_fusion.k0.v0), channel_id=1, source_target_pairs={{0,2},{1,3},{2,4},{3,5},{4,6},{5,7},{6,8},{7,9},{8,10},{9,11},{10,... | collective-permute-start | bytes 4718600 | tf_op jit(solution)/shard_map/ppermute | solution.py:118
  6.5 0.6 fusion.1
  7.1 1.3 %scatter.9 = bf16[2,128]{1,0:T(2,128)(2,1)S(1)} dynamic-update-slice(bf16[2,128]{1,0:T(2,128)(2,1)S(1)} %scatter.6, bf16[1,1]{1,0:T(2,128)(2,1)} %bitcast.1, s32[]{:T(128)} %bitcast.2, s32[]{:T(128)} %bitcast.3) | dynamic-update-slice | bytes 8 | tf_op jit(solution)/shard_map/scatter | solution.py:107
  8.5 0.0 copy-done.4
  8.5 0.0 copy-done.5
  8.5 0.6 pad_maximum_fusion.4
  9.1 0.4 collective-permute-start
  9.5 30.0 %collective-permute-done = bf16[2,6272]{1,0:T(2,128)(2,1)} collective-permute-done((bf16[2,6272]{1,0:T(2,128)(2,1)}, bf16[2,6272]{1,0:T(2,128)(2,1)}, u32[]{:S(2)}, u32[]{:S(2)}) %collective-permute-start) | collective-permute-done | bytes 25120 | tf_op jit(solution)/shard_map/ppermute | solution.py:94
  39.5 0.8 %pad_maximum_fusion.3 = bf16[4,6272]{1,0:T(4,128)(2,1)S(1)} fusion(bf16[2,6272]{1,0:T(2,128)(2,1)} %collective-permute-done, bf16[2,128]{1,0:T(2,128)(2,1)S(1)} %scatter.9, bf16[2,3072]{1,0:T(2,128)(2,1)S(1)} %copy-done.4, bf16[2,3072]{1,0:T(2,128)(2,1)S(1)} %copy-done.5), kind=kLoop, calls=%fused_computation.3 | loop fusion | flops 200704 | bytes 100352 | tf_op jit(solution)/shard_map/concatenate | solution.py:95
  40.3 0.1 collective-permute-start.1
  40.4 7.4 %collective-permute-start.4 = (bf16[2,128,3072]{2,1,0:T(8,128)(2,1)S(1)}, bf16[2,128,3072]{2,1,0:T(8,128)(2,1)}, u32[]{:S(2)}, u32[]{:S(2)}) collective-permute-start(bf16[2,128,3072]{2,1,0:T(8,128)(2,1)S(1)} %pad_maximum_fusion.k0.v0), channel_id=1, source_target_pairs={{0,1},{2,3},{4,5},{6,7},{8,9},{10,11},{12,13},{14,15},{1,4},{3,6},... | collective-permute-start | bytes 4718600 | tf_op jit(solution)/shard_map/ppermute | solution.py:119
  47.9 0.0 collective-permute-done.5.k2.v2
  47.9 0.0 copy-start.1
  47.9 0.1 collective-permute-start.6
  48.0 0.0 collective-permute-done.1
  48.0 1.0 %pad_maximum_fusion.2 = bf16[8,6272]{1,0:T(8,128)(2,1)S(1)} fusion(bf16[4,6272]{1,0:T(4,128)(2,1)} %collective-permute-done.1, bf16[2,6272]{1,0:T(2,128)(2,1)} %collective-permute-done, bf16[2,128]{1,0:T(2,128)(2,1)S(1)} %scatter.9, bf16[2,3072]{1,0:T(2,128)(2,1)S(1)} %copy-done.4, bf16[2,3072]{1,0:T(2,128)(2,1)S(1)} %copy-done.5), kind=kLoop, calls=%fused_computation.2 | loop fusion | flops 501760 | bytes 200704 | tf_op jit(solution)/shard_map/concatenate | solution.py:95
  48.9 0.1 collective-permute-start.2
  49.7 3.4 %collective-permute-done.2 = bf16[8,6272]{1,0:T(8,128)(2,1)} collective-permute-done((bf16[8,6272]{1,0:T(8,128)(2,1)S(1)}, bf16[8,6272]{1,0:T(8,128)(2,1)}, u32[]{:S(2)}, u32[]{:S(2)}) %collective-permute-start.2) | collective-permute-done | bytes 100384 | tf_op jit(solution)/shard_map/ppermute | solution.py:94
  53.1 1.1 %pad_maximum_fusion.1 = bf16[16,6272]{1,0:T(8,128)(2,1)S(1)} fusion(bf16[8,6272]{1,0:T(8,128)(2,1)} %collective-permute-done.2, bf16[4,6272]{1,0:T(4,128)(2,1)} %collective-permute-done.1, bf16[2,6272]{1,0:T(2,128)(2,1)} %collective-permute-done, bf16[2,128]{1,0:T(2,128)(2,1)S(1)} %scatter.9, bf16[2,3072]{1,0:T(2,128)(2,1)S(1)} %copy-done.4, ...), kind=kLoop, calls=%fused_computation.1 | loop fusion | flops 1204224 | bytes 401408 | tf_op jit(solution)/shard_map/concatenate | solution.py:95
  54.1 1.3 %collective-permute-start.3 = (bf16[16,6272]{1,0:T(8,128)(2,1)S(1)}, bf16[16,6272]{1,0:T(8,128)(2,1)}, u32[]{:S(2)}, u32[]{:S(2)}) collective-permute-start(bf16[16,6272]{1,0:T(8,128)(2,1)S(1)} %pad_maximum_fusion.1), channel_id=1, source_target_pairs={{0,1},{1,0},{2,3},{3,2},{4,5},{5,4},{6,7},{7,6},{8,9},{9,8},{10,11... | collective-permute-start | bytes 602120 | tf_op jit(solution)/shard_map/ppermute | solution.py:94
  55.5 0.0 copy-done.6
  55.5 0.0 copy-done.7
  55.5 1.2 %collective-permute-done.3 = bf16[16,6272]{1,0:T(8,128)(2,1)} collective-permute-done((bf16[16,6272]{1,0:T(8,128)(2,1)S(1)}, bf16[16,6272]{1,0:T(8,128)(2,1)}, u32[]{:S(2)}, u32[]{:S(2)}) %collective-permute-start.3) | collective-permute-done | bytes 200736 | tf_op jit(solution)/shard_map/ppermute | solution.py:94
  56.7 2.8 %concatenate.29.ck.cv = bf16[32,6272]{1,0:T(8,128)(2,1)S(1)} concatenate(bf16[2,6272]{1,0:T(2,128)(2,1)} %pad_maximum_fusion.4, bf16[2,6272]{1,0:T(2,128)(2,1)} %collective-permute-done, bf16[4,6272]{1,0:T(4,128)(2,1)} %collective-permute-done.1, bf16[8,6272]{1,0:T(8,128)(2,1)} %collective-permute-done.2, bf16[16,6272]{1,0:T(8,128)(2,1)} %collective-permute-done.3), dimensions={0} | concatenate | bytes 802816 | tf_op jit(solution)/shard_map/concatenate | solution.py:95
  59.5 0.0 copy-start.2
  59.5 0.2 convert_reduce_fusion.1
  59.7 0.2 select_reduce_fusion
  59.9 0.7 pad_add_fusion.table_ref
  60.5 4.7 %collective-permute-done.4.k1.v1 = bf16[2,128,3072]{2,1,0:T(8,128)(2,1)} collective-permute-done((bf16[2,128,3072]{2,1,0:T(8,128)(2,1)S(1)}, bf16[2,128,3072]{2,1,0:T(8,128)(2,1)}, u32[]{:S(2)}, u32[]{:S(2)}) %collective-permute-start.4) | collective-permute-done | bytes 1572896 | tf_op jit(solution)/shard_map/ppermute | solution.py:119
  65.2 0.0 collective-permute-done.6.k3.v3
  65.2 0.0 copy-done
  65.2 0.0 copy-done.1
  65.2 0.0 copy-done.2
  65.2 7.7 %shard_map.100 = bf16[128,3072]{1,0:T(8,128)(2,1)} custom-call(s32[5]{0:T(128)} %pad_add_fusion.table_ref, bf16[128,3072]{1,0:T(8,128)(2,1)} %q_ref.1, bf16[2,128,3072]{2,1,0:T(8,128)(2,1)} %copy-done, bf16[2,128,3072]{2,1,0:T(8,128)(2,1)} %copy-done, bf16[2,128,3072]{2,1,0:T(8,128)(2,1)} %collective-permute-done.4.k1.v1, ...), custom_call_target="tpu_custom_call" | custom-call | flops 855638016 | bytes 8454144 | tf_op jit(solution)/shard_map/pallas_call | solution.py:80
  (3 shorter events, 0.0 us)
Async XLA Ops:
  1.3 1.1 %copy-start.3 = (bf16[128,3072]{1,0:T(8,128)(2,1)S(1)}, bf16[128,3072]{1,0:T(8,128)(2,1)}, u32[]{:S(2)}) copy-start(bf16[128,3072]{1,0:T(8,128)(2,1)} %param.16) | copy-start | bytes 2359300
  2.4 6.0 %copy-start.4 = (bf16[2,3072]{1,0:T(2,128)(2,1)S(1)}, bf16[2,3072]{1,0:T(2,128)(2,1)}, u32[]{:S(2)}) copy-start(bf16[2,3072]{1,0:T(2,128)(2,1)} %param.18) | copy-start | bytes 36868
  2.4 6.0 %copy-start.5 = (bf16[2,3072]{1,0:T(2,128)(2,1)S(1)}, bf16[2,3072]{1,0:T(2,128)(2,1)}, u32[]{:S(2)}) copy-start(bf16[2,3072]{1,0:T(2,128)(2,1)} %param.17) | copy-start | bytes 36868
  2.4 53.1 %copy-start.6 = (s32[3]{0:T(128)S(1)}, s32[3]{0:T(128)}, u32[]{:S(2)}) copy-start(s32[3]{0:T(128)} %constant.76.clone) | copy-start | bytes 40
  2.4 53.1 %copy-start.7 = (s32[3]{0:T(128)S(1)}, s32[3]{0:T(128)}, u32[]{:S(2)}) copy-start(s32[3]{0:T(128)} %constant.75.clone) | copy-start | bytes 40
  2.6 62.6 %copy-start = (bf16[2,128,3072]{2,1,0:T(8,128)(2,1)}, bf16[2,128,3072]{2,1,0:T(8,128)(2,1)S(1)}, u32[]{:S(2)}) copy-start(bf16[2,128,3072]{2,1,0:T(8,128)(2,1)S(1)} %pad_maximum_fusion.k0.v0) | copy-start | bytes 4718596
  2.6 45.3 %collective-permute-start.5 = (bf16[2,128,3072]{2,1,0:T(8,128)(2,1)S(1)}, bf16[2,128,3072]{2,1,0:T(8,128)(2,1)S(1)}, u32[]{:S(2)}, u32[]{:S(2)}) collective-permute-start(bf16[2,128,3072]{2,1,0:T(8,128)(2,1)S(1)} %pad_maximum_fusion.k0.v0), channel_id=1, source_target_pairs={{0,2},{1,3},{2,4},{3,5},{4,6},{5,7},{6,8},{7,9},{8,10},{9,11},{10,... | collective-permute-start | bytes 4718600 | tf_op jit(solution)/shard_map/ppermute | solution.py:118
  9.1 30.4 %collective-permute-start = (bf16[2,6272]{1,0:T(2,128)(2,1)}, bf16[2,6272]{1,0:T(2,128)(2,1)}, u32[]{:S(2)}, u32[]{:S(2)}) collective-permute-start(bf16[2,6272]{1,0:T(2,128)(2,1)} %pad_maximum_fusion.4), channel_id=1, source_target_pairs={{0,8},{1,9},{2,10},{3,11},{4,12},{5,13},{6,14},{7,15},{8,0},{9,1},... | collective-permute-start | bytes 75272 | tf_op jit(solution)/shard_map/ppermute | solution.py:94
  40.3 7.7 %collective-permute-start.1 = (bf16[4,6272]{1,0:T(4,128)(2,1)S(1)}, bf16[4,6272]{1,0:T(4,128)(2,1)}, u32[]{:S(2)}, u32[]{:S(2)}) collective-permute-start(bf16[4,6272]{1,0:T(4,128)(2,1)S(1)} %pad_maximum_fusion.3), channel_id=1, source_target_pairs={{0,4},{1,5},{2,6},{3,7},{4,0},{5,1},{6,2},{7,3},{8,12},{9,13},{10,... | collective-permute-start | bytes 150536 | tf_op jit(solution)/shard_map/ppermute | solution.py:94
  40.4 24.8 %collective-permute-start.4 = (bf16[2,128,3072]{2,1,0:T(8,128)(2,1)S(1)}, bf16[2,128,3072]{2,1,0:T(8,128)(2,1)}, u32[]{:S(2)}, u32[]{:S(2)}) collective-permute-start(bf16[2,128,3072]{2,1,0:T(8,128)(2,1)S(1)} %pad_maximum_fusion.k0.v0), channel_id=1, source_target_pairs={{0,1},{2,3},{4,5},{6,7},{8,9},{10,11},{12,13},{14,15},{1,4},{3,6},... | collective-permute-start | bytes 4718600 | tf_op jit(solution)/shard_map/ppermute | solution.py:119
  47.9 17.3 %copy-start.1 = (bf16[2,128,3072]{2,1,0:T(8,128)(2,1)}, bf16[2,128,3072]{2,1,0:T(8,128)(2,1)S(1)}, u32[]{:S(2)}) copy-start(bf16[2,128,3072]{2,1,0:T(8,128)(2,1)S(1)} %collective-permute-done.5.k2.v2) | copy-start | bytes 4718596
  47.9 17.3 %collective-permute-start.6 = (bf16[2,128,3072]{2,1,0:T(8,128)(2,1)S(1)}, bf16[2,128,3072]{2,1,0:T(8,128)(2,1)}, u32[]{:S(2)}, u32[]{:S(2)}) collective-permute-start(bf16[2,128,3072]{2,1,0:T(8,128)(2,1)S(1)} %collective-permute-done.5.k2.v2), channel_id=1, source_target_pairs={{0,1},{1,0},{2,3},{3,2},{4,5},{5,4},{6,7},{7,6},{8,9},{9,8},{10,11... | collective-permute-start | bytes 4718600 | tf_op jit(solution)/shard_map/ppermute | solution.py:121
  48.9 4.1 %collective-permute-start.2 = (bf16[8,6272]{1,0:T(8,128)(2,1)S(1)}, bf16[8,6272]{1,0:T(8,128)(2,1)}, u32[]{:S(2)}, u32[]{:S(2)}) collective-permute-start(bf16[8,6272]{1,0:T(8,128)(2,1)S(1)} %pad_maximum_fusion.2), channel_id=1, source_target_pairs={{0,2},{1,3},{2,0},{3,1},{4,6},{5,7},{6,4},{7,5},{8,10},{9,11},{10,... | collective-permute-start | bytes 301064 | tf_op jit(solution)/shard_map/ppermute | solution.py:94
  54.1 2.6 %collective-permute-start.3 = (bf16[16,6272]{1,0:T(8,128)(2,1)S(1)}, bf16[16,6272]{1,0:T(8,128)(2,1)}, u32[]{:S(2)}, u32[]{:S(2)}) collective-permute-start(bf16[16,6272]{1,0:T(8,128)(2,1)S(1)} %pad_maximum_fusion.1), channel_id=1, source_target_pairs={{0,1},{1,0},{2,3},{3,2},{4,5},{5,4},{6,7},{7,6},{8,9},{9,8},{10,11... | collective-permute-start | bytes 602120 | tf_op jit(solution)/shard_map/ppermute | solution.py:94
  59.5 5.7 %copy-start.2 = (bf16[32,6272]{1,0:T(8,128)(2,1)}, bf16[32,6272]{1,0:T(8,128)(2,1)S(1)}, u32[]{:S(2)}) copy-start(bf16[32,6272]{1,0:T(8,128)(2,1)S(1)} %concatenate.29.ck.cv) | copy-start | bytes 1204228

commit v15 on v14

--- a/solution.py
+++ b/solution.py
@@ -10,7 +10,7 @@
 
 HEAD_DIM = 128
 WIN = 4
-HEADS_PER_STEP = 8
+HEADS_PER_STEP = 12
 
 
 def attention_kernel(table_ref, q_ref, k0, v0, k1, v1, k2, v2, k3, v3, ck, cv, gate_ref, o_ref, *, heads):

time: 74.3 us -> 73.8 us (level)
  no operation moved by 1% of the time
where the time goes in v15:
time: 73.8 us; the launch traced here: 72.5 us
  waiting for transfers between devices  39.3 us (53%)
  starting transfers between devices  12.7 us (17%)
  Pallas kernels  7.25 us (10%)
  local copies, waits for them, and re-layouts  7.2 us (10%)
  other arithmetic  4.61 us (6%)
  between operations  1.5 us (2%)
    ppermute x4, waiting for transfers between devices, gather_pieces(): other = lax.ppermute(held, 'group', [(i, i ^ step) for i in range(size)])  34.6 us
    ppermute x1, starting transfers between devices, body(): from_mixed = lax.ppermute(kv, 'group', pairs_mixed)  7.45 us
    pallas_call x1, Pallas kernels, attend(): pl.pallas_call(functools.partial(attention_kernel, heads=HEADS_PER_STEP),...  7.25 us
    ppermute x1, waiting for transfers between devices, body(): from_mixed = lax.ppermute(kv, 'group', pairs_mixed)  4.68 us
    ppermute x1, starting transfers between devices, body(): from_two = lax.ppermute(kv, 'group', pairs_two)  3.18 us
    concatenate x3, other arithmetic, gather_pieces(): held = jnp.concatenate([held, other], 0)  2.81 us
    concatenate x1, local copies, waits for them, and re-layouts, gather_pieces(): held = jnp.concatenate([held, other], 0)  2.79 us
    ppermute x4, starting transfers between devices, gather_pieces(): other = lax.ppermute(held, 'group', [(i, i ^ step) for i in range(size)])  1.95 us
  transfers between devices with their start and end apart: 7, of which 4 were waited for; matrix products, arithmetic and copies ran while one was open for 13% of the time, Pallas kernels for 0%

profile of v15, /device:TPU:15, one launch (start us, length us, event | category | flops | bytes accessed | tf_op | source)
XLA Modules:
  0.0 72.5 jit_solution(8680148711049049628)
XLA Ops:
  0.0 1.3 %copy.14 = bf16[16,8,24,128]{3,2,1,0:T(8,128)(2,1)S(1)} copy(bf16[16,8,24,128]{3,1,2,0:T(8,128)(2,1)} %bitcast.10) | data formatting | bytes 1572864
  1.3 0.0 copy-start.3
  1.3 0.7 copy.13
  2.0 0.3 stack_reshape.3
  2.3 0.1 copy-done.3
  2.4 0.0 copy-start.4
  2.4 0.0 copy-start.5
  2.4 0.0 copy-start.6
  2.4 0.0 copy-start.7
  2.4 0.1 pad_maximum_fusion.k0.v0
  2.6 0.0 copy-start
  2.6 3.2 %collective-permute-start.5 = (bf16[2,128,3072]{2,1,0:T(8,128)(2,1)S(1)}, bf16[2,128,3072]{2,1,0:T(8,128)(2,1)S(1)}, u32[]{:S(2)}, u32[]{:S(2)}) collective-permute-start(bf16[2,128,3072]{2,1,0:T(8,128)(2,1)S(1)} %pad_maximum_fusion.k0.v0), channel_id=1, source_target_pairs={{0,2},{1,3},{2,4},{3,5},{4,6},{5,7},{6,8},{7,9},{8,10},{9,11},{10,... | collective-permute-start | bytes 4718600 | tf_op jit(solution)/shard_map/ppermute | solution.py:118
  6.5 0.6 fusion.1
  7.1 1.3 %scatter.9 = bf16[2,128]{1,0:T(2,128)(2,1)S(1)} dynamic-update-slice(bf16[2,128]{1,0:T(2,128)(2,1)S(1)} %scatter.6, bf16[1,1]{1,0:T(2,128)(2,1)} %bitcast.1, s32[]{:T(128)} %bitcast.2, s32[]{:T(128)} %bitcast.3) | dynamic-update-slice | bytes 8 | tf_op jit(solution)/shard_map/scatter | solution.py:107
  8.5 0.0 copy-done.4
  8.5 0.0 copy-done.5
  8.5 0.6 pad_maximum_fusion.4
  9.1 0.4 collective-permute-start
  9.5 30.0 %collective-permute-done = bf16[2,6272]{1,0:T(2,128)(2,1)} collective-permute-done((bf16[2,6272]{1,0:T(2,128)(2,1)}, bf16[2,6272]{1,0:T(2,128)(2,1)}, u32[]{:S(2)}, u32[]{:S(2)}) %collective-permute-start) | collective-permute-done | bytes 25120 | tf_op jit(solution)/shard_map/ppermute | solution.py:94
  39.5 0.8 %pad_maximum_fusion.3 = bf16[4,6272]{1,0:T(4,128)(2,1)S(1)} fusion(bf16[2,6272]{1,0:T(2,128)(2,1)} %collective-permute-done, bf16[2,128]{1,0:T(2,128)(2,1)S(1)} %scatter.9, bf16[2,3072]{1,0:T(2,128)(2,1)S(1)} %copy-done.4, bf16[2,3072]{1,0:T(2,128)(2,1)S(1)} %copy-done.5), kind=kLoop, calls=%fused_computation.3 | loop fusion | flops 200704 | bytes 100352 | tf_op jit(solution)/shard_map/concatenate | solution.py:95
  40.3 0.1 collective-permute-start.1
  40.4 7.4 %collective-permute-start.4 = (bf16[2,128,3072]{2,1,0:T(8,128)(2,1)S(1)}, bf16[2,128,3072]{2,1,0:T(8,128)(2,1)}, u32[]{:S(2)}, u32[]{:S(2)}) collective-permute-start(bf16[2,128,3072]{2,1,0:T(8,128)(2,1)S(1)} %pad_maximum_fusion.k0.v0), channel_id=1, source_target_pairs={{0,1},{2,3},{4,5},{6,7},{8,9},{10,11},{12,13},{14,15},{1,4},{3,6},... | collective-permute-start | bytes 4718600 | tf_op jit(solution)/shard_map/ppermute | solution.py:119
  47.9 0.0 collective-permute-done.5.k2.v2
  47.9 0.0 copy-start.1
  47.9 0.1 collective-permute-start.6
  48.0 0.0 collective-permute-done.1
  48.0 1.0 %pad_maximum_fusion.2 = bf16[8,6272]{1,0:T(8,128)(2,1)S(1)} fusion(bf16[4,6272]{1,0:T(4,128)(2,1)} %collective-permute-done.1, bf16[2,6272]{1,0:T(2,128)(2,1)} %collective-permute-done, bf16[2,128]{1,0:T(2,128)(2,1)S(1)} %scatter.9, bf16[2,3072]{1,0:T(2,128)(2,1)S(1)} %copy-done.4, bf16[2,3072]{1,0:T(2,128)(2,1)S(1)} %copy-done.5), kind=kLoop, calls=%fused_computation.2 | loop fusion | flops 501760 | bytes 200704 | tf_op jit(solution)/shard_map/concatenate | solution.py:95
  48.9 0.1 collective-permute-start.2
  49.7 3.4 %collective-permute-done.2 = bf16[8,6272]{1,0:T(8,128)(2,1)} collective-permute-done((bf16[8,6272]{1,0:T(8,128)(2,1)S(1)}, bf16[8,6272]{1,0:T(8,128)(2,1)}, u32[]{:S(2)}, u32[]{:S(2)}) %collective-permute-start.2) | collective-permute-done | bytes 100384 | tf_op jit(solution)/shard_map/ppermute | solution.py:94
  53.1 1.1 %pad_maximum_fusion.1 = bf16[16,6272]{1,0:T(8,128)(2,1)S(1)} fusion(bf16[8,6272]{1,0:T(8,128)(2,1)} %collective-permute-done.2, bf16[4,6272]{1,0:T(4,128)(2,1)} %collective-permute-done.1, bf16[2,6272]{1,0:T(2,128)(2,1)} %collective-permute-done, bf16[2,128]{1,0:T(2,128)(2,1)S(1)} %scatter.9, bf16[2,3072]{1,0:T(2,128)(2,1)S(1)} %copy-done.4, ...), kind=kLoop, calls=%fused_computation.1 | loop fusion | flops 1204224 | bytes 401408 | tf_op jit(solution)/shard_map/concatenate | solution.py:95
  54.1 1.3 %collective-permute-start.3 = (bf16[16,6272]{1,0:T(8,128)(2,1)S(1)}, bf16[16,6272]{1,0:T(8,128)(2,1)}, u32[]{:S(2)}, u32[]{:S(2)}) collective-permute-start(bf16[16,6272]{1,0:T(8,128)(2,1)S(1)} %pad_maximum_fusion.1), channel_id=1, source_target_pairs={{0,1},{1,0},{2,3},{3,2},{4,5},{5,4},{6,7},{7,6},{8,9},{9,8},{10,11... | collective-permute-start | bytes 602120 | tf_op jit(solution)/shard_map/ppermute | solution.py:94
  55.5 0.0 copy-done.6
  55.5 0.0 copy-done.7
  55.5 1.2 %collective-permute-done.3 = bf16[16,6272]{1,0:T(8,128)(2,1)} collective-permute-done((bf16[16,6272]{1,0:T(8,128)(2,1)S(1)}, bf16[16,6272]{1,0:T(8,128)(2,1)}, u32[]{:S(2)}, u32[]{:S(2)}) %collective-permute-start.3) | collective-permute-done | bytes 200736 | tf_op jit(solution)/shard_map/ppermute | solution.py:94
  56.7 2.8 %concatenate.29.ck.cv = bf16[32,6272]{1,0:T(8,128)(2,1)S(1)} concatenate(bf16[2,6272]{1,0:T(2,128)(2,1)} %pad_maximum_fusion.4, bf16[2,6272]{1,0:T(2,128)(2,1)} %collective-permute-done, bf16[4,6272]{1,0:T(4,128)(2,1)} %collective-permute-done.1, bf16[8,6272]{1,0:T(8,128)(2,1)} %collective-permute-done.2, bf16[16,6272]{1,0:T(8,128)(2,1)} %collective-permute-done.3), dimensions={0} | concatenate | bytes 802816 | tf_op jit(solution)/shard_map/concatenate | solution.py:95
  59.5 0.0 copy-start.2
  59.5 0.2 convert_reduce_fusion.1
  59.7 0.2 select_reduce_fusion
  59.9 0.7 pad_add_fusion.table_ref
  60.5 4.7 %collective-permute-done.4.k1.v1 = bf16[2,128,3072]{2,1,0:T(8,128)(2,1)} collective-permute-done((bf16[2,128,3072]{2,1,0:T(8,128)(2,1)S(1)}, bf16[2,128,3072]{2,1,0:T(8,128)(2,1)}, u32[]{:S(2)}, u32[]{:S(2)}) %collective-permute-start.4) | collective-permute-done | bytes 1572896 | tf_op jit(solution)/shard_map/ppermute | solution.py:119
  65.2 0.0 collective-permute-done.6.k3.v3
  65.2 0.0 copy-done
  65.2 0.0 copy-done.1
  65.2 0.0 copy-done.2
  65.2 7.3 %shard_map.100 = bf16[128,3072]{1,0:T(8,128)(2,1)} custom-call(s32[5]{0:T(128)} %pad_add_fusion.table_ref, bf16[128,3072]{1,0:T(8,128)(2,1)} %q_ref.1, bf16[2,128,3072]{2,1,0:T(8,128)(2,1)} %copy-done, bf16[2,128,3072]{2,1,0:T(8,128)(2,1)} %copy-done, bf16[2,128,3072]{2,1,0:T(8,128)(2,1)} %collective-permute-done.4.k1.v1, ...), custom_call_target="tpu_custom_call" | custom-call | flops 855638016 | bytes 8454144 | tf_op jit(solution)/shard_map/pallas_call | solution.py:80
  (3 shorter events, 0.0 us)
Async XLA Ops:
  1.3 1.1 %copy-start.3 = (bf16[128,3072]{1,0:T(8,128)(2,1)S(1)}, bf16[128,3072]{1,0:T(8,128)(2,1)}, u32[]{:S(2)}) copy-start(bf16[128,3072]{1,0:T(8,128)(2,1)} %param.16) | copy-start | bytes 2359300
  2.4 6.0 %copy-start.4 = (bf16[2,3072]{1,0:T(2,128)(2,1)S(1)}, bf16[2,3072]{1,0:T(2,128)(2,1)}, u32[]{:S(2)}) copy-start(bf16[2,3072]{1,0:T(2,128)(2,1)} %param.18) | copy-start | bytes 36868
  2.4 6.0 %copy-start.5 = (bf16[2,3072]{1,0:T(2,128)(2,1)S(1)}, bf16[2,3072]{1,0:T(2,128)(2,1)}, u32[]{:S(2)}) copy-start(bf16[2,3072]{1,0:T(2,128)(2,1)} %param.17) | copy-start | bytes 36868
  2.4 53.1 %copy-start.6 = (s32[3]{0:T(128)S(1)}, s32[3]{0:T(128)}, u32[]{:S(2)}) copy-start(s32[3]{0:T(128)} %constant.76.clone) | copy-start | bytes 40
  2.4 53.1 %copy-start.7 = (s32[3]{0:T(128)S(1)}, s32[3]{0:T(128)}, u32[]{:S(2)}) copy-start(s32[3]{0:T(128)} %constant.75.clone) | copy-start | bytes 40
  2.6 62.6 %copy-start = (bf16[2,128,3072]{2,1,0:T(8,128)(2,1)}, bf16[2,128,3072]{2,1,0:T(8,128)(2,1)S(1)}, u32[]{:S(2)}) copy-start(bf16[2,128,3072]{2,1,0:T(8,128)(2,1)S(1)} %pad_maximum_fusion.k0.v0) | copy-start | bytes 4718596
  2.6 45.3 %collective-permute-start.5 = (bf16[2,128,3072]{2,1,0:T(8,128)(2,1)S(1)}, bf16[2,128,3072]{2,1,0:T(8,128)(2,1)S(1)}, u32[]{:S(2)}, u32[]{:S(2)}) collective-permute-start(bf16[2,128,3072]{2,1,0:T(8,128)(2,1)S(1)} %pad_maximum_fusion.k0.v0), channel_id=1, source_target_pairs={{0,2},{1,3},{2,4},{3,5},{4,6},{5,7},{6,8},{7,9},{8,10},{9,11},{10,... | collective-permute-start | bytes 4718600 | tf_op jit(solution)/shard_map/ppermute | solution.py:118
  9.1 30.4 %collective-permute-start = (bf16[2,6272]{1,0:T(2,128)(2,1)}, bf16[2,6272]{1,0:T(2,128)(2,1)}, u32[]{:S(2)}, u32[]{:S(2)}) collective-permute-start(bf16[2,6272]{1,0:T(2,128)(2,1)} %pad_maximum_fusion.4), channel_id=1, source_target_pairs={{0,8},{1,9},{2,10},{3,11},{4,12},{5,13},{6,14},{7,15},{8,0},{9,1},... | collective-permute-start | bytes 75272 | tf_op jit(solution)/shard_map/ppermute | solution.py:94
  40.3 7.7 %collective-permute-start.1 = (bf16[4,6272]{1,0:T(4,128)(2,1)S(1)}, bf16[4,6272]{1,0:T(4,128)(2,1)}, u32[]{:S(2)}, u32[]{:S(2)}) collective-permute-start(bf16[4,6272]{1,0:T(4,128)(2,1)S(1)} %pad_maximum_fusion.3), channel_id=1, source_target_pairs={{0,4},{1,5},{2,6},{3,7},{4,0},{5,1},{6,2},{7,3},{8,12},{9,13},{10,... | collective-permute-start | bytes 150536 | tf_op jit(solution)/shard_map/ppermute | solution.py:94
  40.4 24.8 %collective-permute-start.4 = (bf16[2,128,3072]{2,1,0:T(8,128)(2,1)S(1)}, bf16[2,128,3072]{2,1,0:T(8,128)(2,1)}, u32[]{:S(2)}, u32[]{:S(2)}) collective-permute-start(bf16[2,128,3072]{2,1,0:T(8,128)(2,1)S(1)} %pad_maximum_fusion.k0.v0), channel_id=1, source_target_pairs={{0,1},{2,3},{4,5},{6,7},{8,9},{10,11},{12,13},{14,15},{1,4},{3,6},... | collective-permute-start | bytes 4718600 | tf_op jit(solution)/shard_map/ppermute | solution.py:119
  47.9 17.3 %copy-start.1 = (bf16[2,128,3072]{2,1,0:T(8,128)(2,1)}, bf16[2,128,3072]{2,1,0:T(8,128)(2,1)S(1)}, u32[]{:S(2)}) copy-start(bf16[2,128,3072]{2,1,0:T(8,128)(2,1)S(1)} %collective-permute-done.5.k2.v2) | copy-start | bytes 4718596
  47.9 17.3 %collective-permute-start.6 = (bf16[2,128,3072]{2,1,0:T(8,128)(2,1)S(1)}, bf16[2,128,3072]{2,1,0:T(8,128)(2,1)}, u32[]{:S(2)}, u32[]{:S(2)}) collective-permute-start(bf16[2,128,3072]{2,1,0:T(8,128)(2,1)S(1)} %collective-permute-done.5.k2.v2), channel_id=1, source_target_pairs={{0,1},{1,0},{2,3},{3,2},{4,5},{5,4},{6,7},{7,6},{8,9},{9,8},{10,11... | collective-permute-start | bytes 4718600 | tf_op jit(solution)/shard_map/ppermute | solution.py:121
  48.9 4.1 %collective-permute-start.2 = (bf16[8,6272]{1,0:T(8,128)(2,1)S(1)}, bf16[8,6272]{1,0:T(8,128)(2,1)}, u32[]{:S(2)}, u32[]{:S(2)}) collective-permute-start(bf16[8,6272]{1,0:T(8,128)(2,1)S(1)} %pad_maximum_fusion.2), channel_id=1, source_target_pairs={{0,2},{1,3},{2,0},{3,1},{4,6},{5,7},{6,4},{7,5},{8,10},{9,11},{10,... | collective-permute-start | bytes 301064 | tf_op jit(solution)/shard_map/ppermute | solution.py:94
  54.1 2.6 %collective-permute-start.3 = (bf16[16,6272]{1,0:T(8,128)(2,1)S(1)}, bf16[16,6272]{1,0:T(8,128)(2,1)}, u32[]{:S(2)}, u32[]{:S(2)}) collective-permute-start(bf16[16,6272]{1,0:T(8,128)(2,1)S(1)} %pad_maximum_fusion.1), channel_id=1, source_target_pairs={{0,1},{1,0},{2,3},{3,2},{4,5},{5,4},{6,7},{7,6},{8,9},{9,8},{10,11... | collective-permute-start | bytes 602120 | tf_op jit(solution)/shard_map/ppermute | solution.py:94
  59.5 5.7 %copy-start.2 = (bf16[32,6272]{1,0:T(8,128)(2,1)}, bf16[32,6272]{1,0:T(8,128)(2,1)S(1)}, u32[]{:S(2)}) copy-start(bf16[32,6272]{1,0:T(8,128)(2,1)S(1)} %concatenate.29.ck.cv) | copy-start | bytes 1204228

commit v16 on v15

--- a/solution.py
+++ b/solution.py
@@ -10,7 +10,7 @@
 
 HEAD_DIM = 128
 WIN = 4
-HEADS_PER_STEP = 12
+HEADS_PER_STEP = 24
 
 
 def attention_kernel(table_ref, q_ref, k0, v0, k1, v1, k2, v2, k3, v3, ck, cv, gate_ref, o_ref, *, heads):

time: 73.8 us -> 75.3 us (1.020)
  Pallas kernels: 7.25 us -> 8.77 us
    pallas_call x1, Pallas kernels: 7.25 us -> 8.77 us  [attend(): pl.pallas_call(functools.partial(attention_kernel, heads=HEADS_PER_STEP),...]
  transfers between devices with their start and end apart: 7 -> 7, of which waited for: 4 -> 4; matrix products, arithmetic and copies ran while one was open for 13% -> 12% of each run, Pallas kernels for 0% -> 0%
where the time goes in v16:
time: 75.3 us; the launch traced here: 74 us
  waiting for transfers between devices  39.3 us (52%)
  starting transfers between devices  12.7 us (17%)
  Pallas kernels  8.77 us (12%)
  local copies, waits for them, and re-layouts  7.2 us (10%)
  other arithmetic  4.61 us (6%)
  between operations  1.5 us (2%)
    ppermute x4, waiting for transfers between devices, gather_pieces(): other = lax.ppermute(held, 'group', [(i, i ^ step) for i in range(size)])  34.6 us
    pallas_call x1, Pallas kernels, attend(): pl.pallas_call(functools.partial(attention_kernel, heads=HEADS_PER_STEP),...  8.77 us
    ppermute x1, starting transfers between devices, body(): from_mixed = lax.ppermute(kv, 'group', pairs_mixed)  7.45 us
    ppermute x1, waiting for transfers between devices, body(): from_mixed = lax.ppermute(kv, 'group', pairs_mixed)  4.68 us
    ppermute x1, starting transfers between devices, body(): from_two = lax.ppermute(kv, 'group', pairs_two)  3.18 us
    concatenate x3, other arithmetic, gather_pieces(): held = jnp.concatenate([held, other], 0)  2.81 us
    concatenate x1, local copies, waits for them, and re-layouts, gather_pieces(): held = jnp.concatenate([held, other], 0)  2.79 us
    ppermute x4, starting transfers between devices, gather_pieces(): other = lax.ppermute(held, 'group', [(i, i ^ step) for i in range(size)])  1.95 us
  transfers between devices with their start and end apart: 7, of which 4 were waited for; matrix products, arithmetic and copies ran while one was open for 12% of the time, Pallas kernels for 0%

profile of v16, /device:TPU:15, one launch (start us, length us, event | category | flops | bytes accessed | tf_op | source)
XLA Modules:
  0.0 74.0 jit_solution(8776378733263239853)
XLA Ops:
  0.0 1.3 %copy.14 = bf16[16,8,24,128]{3,2,1,0:T(8,128)(2,1)S(1)} copy(bf16[16,8,24,128]{3,1,2,0:T(8,128)(2,1)} %bitcast.10) | data formatting | bytes 1572864
  1.3 0.0 copy-start.3
  1.3 0.7 copy.13
  2.0 0.3 stack_reshape.3
  2.3 0.1 copy-done.3
  2.4 0.0 copy-start.4
  2.4 0.0 copy-start.5
  2.4 0.0 copy-start.6
  2.4 0.0 copy-start.7
  2.4 0.1 pad_maximum_fusion.k0.v0
  2.6 0.0 copy-start
  2.6 3.2 %collective-permute-start.5 = (bf16[2,128,3072]{2,1,0:T(8,128)(2,1)S(1)}, bf16[2,128,3072]{2,1,0:T(8,128)(2,1)S(1)}, u32[]{:S(2)}, u32[]{:S(2)}) collective-permute-start(bf16[2,128,3072]{2,1,0:T(8,128)(2,1)S(1)} %pad_maximum_fusion.k0.v0), channel_id=1, source_target_pairs={{0,2},{1,3},{2,4},{3,5},{4,6},{5,7},{6,8},{7,9},{8,10},{9,11},{10,... | collective-permute-start | bytes 4718600 | tf_op jit(solution)/shard_map/ppermute | solution.py:118
  6.5 0.6 fusion.1
  7.1 1.3 %scatter.9 = bf16[2,128]{1,0:T(2,128)(2,1)S(1)} dynamic-update-slice(bf16[2,128]{1,0:T(2,128)(2,1)S(1)} %scatter.6, bf16[1,1]{1,0:T(2,128)(2,1)} %bitcast.1, s32[]{:T(128)} %bitcast.2, s32[]{:T(128)} %bitcast.3) | dynamic-update-slice | bytes 8 | tf_op jit(solution)/shard_map/scatter | solution.py:107
  8.5 0.0 copy-done.4
  8.5 0.0 copy-done.5
  8.5 0.6 pad_maximum_fusion.4
  9.1 0.4 collective-permute-start
  9.5 30.0 %collective-permute-done = bf16[2,6272]{1,0:T(2,128)(2,1)} collective-permute-done((bf16[2,6272]{1,0:T(2,128)(2,1)}, bf16[2,6272]{1,0:T(2,128)(2,1)}, u32[]{:S(2)}, u32[]{:S(2)}) %collective-permute-start) | collective-permute-done | bytes 25120 | tf_op jit(solution)/shard_map/ppermute | solution.py:94
  39.5 0.8 %pad_maximum_fusion.3 = bf16[4,6272]{1,0:T(4,128)(2,1)S(1)} fusion(bf16[2,6272]{1,0:T(2,128)(2,1)} %collective-permute-done, bf16[2,128]{1,0:T(2,128)(2,1)S(1)} %scatter.9, bf16[2,3072]{1,0:T(2,128)(2,1)S(1)} %copy-done.4, bf16[2,3072]{1,0:T(2,128)(2,1)S(1)} %copy-done.5), kind=kLoop, calls=%fused_computation.3 | loop fusion | flops 200704 | bytes 100352 | tf_op jit(solution)/shard_map/concatenate | solution.py:95
  40.3 0.1 collective-permute-start.1
  40.4 7.4 %collective-permute-start.4 = (bf16[2,128,3072]{2,1,0:T(8,128)(2,1)S(1)}, bf16[2,128,3072]{2,1,0:T(8,128)(2,1)}, u32[]{:S(2)}, u32[]{:S(2)}) collective-permute-start(bf16[2,128,3072]{2,1,0:T(8,128)(2,1)S(1)} %pad_maximum_fusion.k0.v0), channel_id=1, source_target_pairs={{0,1},{2,3},{4,5},{6,7},{8,9},{10,11},{12,13},{14,15},{1,4},{3,6},... | collective-permute-start | bytes 4718600 | tf_op jit(solution)/shard_map/ppermute | solution.py:119
  47.9 0.0 collective-permute-done.5.k2.v2
  47.9 0.0 copy-start.1
  47.9 0.1 collective-permute-start.6
  48.0 0.0 collective-permute-done.1
  48.0 1.0 %pad_maximum_fusion.2 = bf16[8,6272]{1,0:T(8,128)(2,1)S(1)} fusion(bf16[4,6272]{1,0:T(4,128)(2,1)} %collective-permute-done.1, bf16[2,6272]{1,0:T(2,128)(2,1)} %collective-permute-done, bf16[2,128]{1,0:T(2,128)(2,1)S(1)} %scatter.9, bf16[2,3072]{1,0:T(2,128)(2,1)S(1)} %copy-done.4, bf16[2,3072]{1,0:T(2,128)(2,1)S(1)} %copy-done.5), kind=kLoop, calls=%fused_computation.2 | loop fusion | flops 501760 | bytes 200704 | tf_op jit(solution)/shard_map/concatenate | solution.py:95
  48.9 0.1 collective-permute-start.2
  49.7 3.4 %collective-permute-done.2 = bf16[8,6272]{1,0:T(8,128)(2,1)} collective-permute-done((bf16[8,6272]{1,0:T(8,128)(2,1)S(1)}, bf16[8,6272]{1,0:T(8,128)(2,1)}, u32[]{:S(2)}, u32[]{:S(2)}) %collective-permute-start.2) | collective-permute-done | bytes 100384 | tf_op jit(solution)/shard_map/ppermute | solution.py:94
  53.1 1.1 %pad_maximum_fusion.1 = bf16[16,6272]{1,0:T(8,128)(2,1)S(1)} fusion(bf16[8,6272]{1,0:T(8,128)(2,1)} %collective-permute-done.2, bf16[4,6272]{1,0:T(4,128)(2,1)} %collective-permute-done.1, bf16[2,6272]{1,0:T(2,128)(2,1)} %collective-permute-done, bf16[2,128]{1,0:T(2,128)(2,1)S(1)} %scatter.9, bf16[2,3072]{1,0:T(2,128)(2,1)S(1)} %copy-done.4, ...), kind=kLoop, calls=%fused_computation.1 | loop fusion | flops 1204224 | bytes 401408 | tf_op jit(solution)/shard_map/concatenate | solution.py:95
  54.1 1.3 %collective-permute-start.3 = (bf16[16,6272]{1,0:T(8,128)(2,1)S(1)}, bf16[16,6272]{1,0:T(8,128)(2,1)}, u32[]{:S(2)}, u32[]{:S(2)}) collective-permute-start(bf16[16,6272]{1,0:T(8,128)(2,1)S(1)} %pad_maximum_fusion.1), channel_id=1, source_target_pairs={{0,1},{1,0},{2,3},{3,2},{4,5},{5,4},{6,7},{7,6},{8,9},{9,8},{10,11... | collective-permute-start | bytes 602120 | tf_op jit(solution)/shard_map/ppermute | solution.py:94
  55.5 0.0 copy-done.6
  55.5 0.0 copy-done.7
  55.5 1.2 %collective-permute-done.3 = bf16[16,6272]{1,0:T(8,128)(2,1)} collective-permute-done((bf16[16,6272]{1,0:T(8,128)(2,1)S(1)}, bf16[16,6272]{1,0:T(8,128)(2,1)}, u32[]{:S(2)}, u32[]{:S(2)}) %collective-permute-start.3) | collective-permute-done | bytes 200736 | tf_op jit(solution)/shard_map/ppermute | solution.py:94
  56.7 2.8 %concatenate.29.ck.cv = bf16[32,6272]{1,0:T(8,128)(2,1)S(1)} concatenate(bf16[2,6272]{1,0:T(2,128)(2,1)} %pad_maximum_fusion.4, bf16[2,6272]{1,0:T(2,128)(2,1)} %collective-permute-done, bf16[4,6272]{1,0:T(4,128)(2,1)} %collective-permute-done.1, bf16[8,6272]{1,0:T(8,128)(2,1)} %collective-permute-done.2, bf16[16,6272]{1,0:T(8,128)(2,1)} %collective-permute-done.3), dimensions={0} | concatenate | bytes 802816 | tf_op jit(solution)/shard_map/concatenate | solution.py:95
  59.5 0.0 copy-start.2
  59.5 0.2 convert_reduce_fusion.1
  59.7 0.2 select_reduce_fusion
  59.9 0.7 pad_add_fusion.table_ref
  60.5 4.7 %collective-permute-done.4.k1.v1 = bf16[2,128,3072]{2,1,0:T(8,128)(2,1)} collective-permute-done((bf16[2,128,3072]{2,1,0:T(8,128)(2,1)S(1)}, bf16[2,128,3072]{2,1,0:T(8,128)(2,1)}, u32[]{:S(2)}, u32[]{:S(2)}) %collective-permute-start.4) | collective-permute-done | bytes 1572896 | tf_op jit(solution)/shard_map/ppermute | solution.py:119
  65.2 0.0 collective-permute-done.6.k3.v3
  65.2 0.0 copy-done
  65.2 0.0 copy-done.1
  65.2 0.0 copy-done.2
  65.2 8.8 %shard_map.100 = bf16[128,3072]{1,0:T(8,128)(2,1)} custom-call(s32[5]{0:T(128)} %pad_add_fusion.table_ref, bf16[128,3072]{1,0:T(8,128)(2,1)} %q_ref.1, bf16[2,128,3072]{2,1,0:T(8,128)(2,1)} %copy-done, bf16[2,128,3072]{2,1,0:T(8,128)(2,1)} %copy-done, bf16[2,128,3072]{2,1,0:T(8,128)(2,1)} %collective-permute-done.4.k1.v1, ...), custom_call_target="tpu_custom_call" | custom-call | flops 855638016 | bytes 8454144 | tf_op jit(solution)/shard_map/pallas_call | solution.py:80
  (3 shorter events, 0.0 us)
Async XLA Ops:
  1.3 1.1 %copy-start.3 = (bf16[128,3072]{1,0:T(8,128)(2,1)S(1)}, bf16[128,3072]{1,0:T(8,128)(2,1)}, u32[]{:S(2)}) copy-start(bf16[128,3072]{1,0:T(8,128)(2,1)} %param.16) | copy-start | bytes 2359300
  2.4 6.0 %copy-start.4 = (bf16[2,3072]{1,0:T(2,128)(2,1)S(1)}, bf16[2,3072]{1,0:T(2,128)(2,1)}, u32[]{:S(2)}) copy-start(bf16[2,3072]{1,0:T(2,128)(2,1)} %param.18) | copy-start | bytes 36868
  2.4 6.0 %copy-start.5 = (bf16[2,3072]{1,0:T(2,128)(2,1)S(1)}, bf16[2,3072]{1,0:T(2,128)(2,1)}, u32[]{:S(2)}) copy-start(bf16[2,3072]{1,0:T(2,128)(2,1)} %param.17) | copy-start | bytes 36868
  2.4 53.1 %copy-start.6 = (s32[3]{0:T(128)S(1)}, s32[3]{0:T(128)}, u32[]{:S(2)}) copy-start(s32[3]{0:T(128)} %constant.76.clone) | copy-start | bytes 40
  2.4 53.1 %copy-start.7 = (s32[3]{0:T(128)S(1)}, s32[3]{0:T(128)}, u32[]{:S(2)}) copy-start(s32[3]{0:T(128)} %constant.75.clone) | copy-start | bytes 40
  2.6 62.6 %copy-start = (bf16[2,128,3072]{2,1,0:T(8,128)(2,1)}, bf16[2,128,3072]{2,1,0:T(8,128)(2,1)S(1)}, u32[]{:S(2)}) copy-start(bf16[2,128,3072]{2,1,0:T(8,128)(2,1)S(1)} %pad_maximum_fusion.k0.v0) | copy-start | bytes 4718596
  2.6 45.3 %collective-permute-start.5 = (bf16[2,128,3072]{2,1,0:T(8,128)(2,1)S(1)}, bf16[2,128,3072]{2,1,0:T(8,128)(2,1)S(1)}, u32[]{:S(2)}, u32[]{:S(2)}) collective-permute-start(bf16[2,128,3072]{2,1,0:T(8,128)(2,1)S(1)} %pad_maximum_fusion.k0.v0), channel_id=1, source_target_pairs={{0,2},{1,3},{2,4},{3,5},{4,6},{5,7},{6,8},{7,9},{8,10},{9,11},{10,... | collective-permute-start | bytes 4718600 | tf_op jit(solution)/shard_map/ppermute | solution.py:118
  9.1 30.4 %collective-permute-start = (bf16[2,6272]{1,0:T(2,128)(2,1)}, bf16[2,6272]{1,0:T(2,128)(2,1)}, u32[]{:S(2)}, u32[]{:S(2)}) collective-permute-start(bf16[2,6272]{1,0:T(2,128)(2,1)} %pad_maximum_fusion.4), channel_id=1, source_target_pairs={{0,8},{1,9},{2,10},{3,11},{4,12},{5,13},{6,14},{7,15},{8,0},{9,1},... | collective-permute-start | bytes 75272 | tf_op jit(solution)/shard_map/ppermute | solution.py:94
  40.3 7.7 %collective-permute-start.1 = (bf16[4,6272]{1,0:T(4,128)(2,1)S(1)}, bf16[4,6272]{1,0:T(4,128)(2,1)}, u32[]{:S(2)}, u32[]{:S(2)}) collective-permute-start(bf16[4,6272]{1,0:T(4,128)(2,1)S(1)} %pad_maximum_fusion.3), channel_id=1, source_target_pairs={{0,4},{1,5},{2,6},{3,7},{4,0},{5,1},{6,2},{7,3},{8,12},{9,13},{10,... | collective-permute-start | bytes 150536 | tf_op jit(solution)/shard_map/ppermute | solution.py:94
  40.4 24.8 %collective-permute-start.4 = (bf16[2,128,3072]{2,1,0:T(8,128)(2,1)S(1)}, bf16[2,128,3072]{2,1,0:T(8,128)(2,1)}, u32[]{:S(2)}, u32[]{:S(2)}) collective-permute-start(bf16[2,128,3072]{2,1,0:T(8,128)(2,1)S(1)} %pad_maximum_fusion.k0.v0), channel_id=1, source_target_pairs={{0,1},{2,3},{4,5},{6,7},{8,9},{10,11},{12,13},{14,15},{1,4},{3,6},... | collective-permute-start | bytes 4718600 | tf_op jit(solution)/shard_map/ppermute | solution.py:119
  47.9 17.3 %copy-start.1 = (bf16[2,128,3072]{2,1,0:T(8,128)(2,1)}, bf16[2,128,3072]{2,1,0:T(8,128)(2,1)S(1)}, u32[]{:S(2)}) copy-start(bf16[2,128,3072]{2,1,0:T(8,128)(2,1)S(1)} %collective-permute-done.5.k2.v2) | copy-start | bytes 4718596
  47.9 17.3 %collective-permute-start.6 = (bf16[2,128,3072]{2,1,0:T(8,128)(2,1)S(1)}, bf16[2,128,3072]{2,1,0:T(8,128)(2,1)}, u32[]{:S(2)}, u32[]{:S(2)}) collective-permute-start(bf16[2,128,3072]{2,1,0:T(8,128)(2,1)S(1)} %collective-permute-done.5.k2.v2), channel_id=1, source_target_pairs={{0,1},{1,0},{2,3},{3,2},{4,5},{5,4},{6,7},{7,6},{8,9},{9,8},{10,11... | collective-permute-start | bytes 4718600 | tf_op jit(solution)/shard_map/ppermute | solution.py:121
  48.9 4.1 %collective-permute-start.2 = (bf16[8,6272]{1,0:T(8,128)(2,1)S(1)}, bf16[8,6272]{1,0:T(8,128)(2,1)}, u32[]{:S(2)}, u32[]{:S(2)}) collective-permute-start(bf16[8,6272]{1,0:T(8,128)(2,1)S(1)} %pad_maximum_fusion.2), channel_id=1, source_target_pairs={{0,2},{1,3},{2,0},{3,1},{4,6},{5,7},{6,4},{7,5},{8,10},{9,11},{10,... | collective-permute-start | bytes 301064 | tf_op jit(solution)/shard_map/ppermute | solution.py:94
  54.1 2.6 %collective-permute-start.3 = (bf16[16,6272]{1,0:T(8,128)(2,1)S(1)}, bf16[16,6272]{1,0:T(8,128)(2,1)}, u32[]{:S(2)}, u32[]{:S(2)}) collective-permute-start(bf16[16,6272]{1,0:T(8,128)(2,1)S(1)} %pad_maximum_fusion.1), channel_id=1, source_target_pairs={{0,1},{1,0},{2,3},{3,2},{4,5},{5,4},{6,7},{7,6},{8,9},{9,8},{10,11... | collective-permute-start | bytes 602120 | tf_op jit(solution)/shard_map/ppermute | solution.py:94
  59.5 5.7 %copy-start.2 = (bf16[32,6272]{1,0:T(8,128)(2,1)}, bf16[32,6272]{1,0:T(8,128)(2,1)S(1)}, u32[]{:S(2)}) copy-start(bf16[32,6272]{1,0:T(8,128)(2,1)S(1)} %concatenate.29.ck.cv) | copy-start | bytes 1204228

commit v17 on v16

--- a/solution.py
+++ b/solution.py
@@ -10,7 +10,7 @@
 
 HEAD_DIM = 128
 WIN = 4
-HEADS_PER_STEP = 24
+HEADS_PER_STEP = 6
 
 
 def attention_kernel(table_ref, q_ref, k0, v0, k1, v1, k2, v2, k3, v3, ck, cv, gate_ref, o_ref, *, heads):

time: 75.3 us -> 74.1 us (0.984)
  Pallas kernels: 8.77 us -> 7.51 us
    pallas_call x1, Pallas kernels: 8.77 us -> 7.51 us  [attend(): pl.pallas_call(functools.partial(attention_kernel, heads=HEADS_PER_STEP),...]
  transfers between devices with their start and end apart: 7 -> 7, of which waited for: 4 -> 4; matrix products, arithmetic and copies ran while one was open for 12% -> 13% of each run, Pallas kernels for 0% -> 0%
where the time goes in v17:
time: 74.1 us; the launch traced here: 72.7 us
  waiting for transfers between devices  39.3 us (53%)
  starting transfers between devices  12.7 us (17%)
  Pallas kernels  7.51 us (10%)
  local copies, waits for them, and re-layouts  7.2 us (10%)
  other arithmetic  4.61 us (6%)
  between operations  1.5 us (2%)
    ppermute x4, waiting for transfers between devices, gather_pieces(): other = lax.ppermute(held, 'group', [(i, i ^ step) for i in range(size)])  34.6 us
    pallas_call x1, Pallas kernels, attend(): pl.pallas_call(functools.partial(attention_kernel, heads=HEADS_PER_STEP),...  7.51 us
    ppermute x1, starting transfers between devices, body(): from_mixed = lax.ppermute(kv, 'group', pairs_mixed)  7.45 us
    ppermute x1, waiting for transfers between devices, body(): from_mixed = lax.ppermute(kv, 'group', pairs_mixed)  4.68 us
    ppermute x1, starting transfers between devices, body(): from_two = lax.ppermute(kv, 'group', pairs_two)  3.18 us
    concatenate x3, other arithmetic, gather_pieces(): held = jnp.concatenate([held, other], 0)  2.81 us
    concatenate x1, local copies, waits for them, and re-layouts, gather_pieces(): held = jnp.concatenate([held, other], 0)  2.79 us
    ppermute x4, starting transfers between devices, gather_pieces(): other = lax.ppermute(held, 'group', [(i, i ^ step) for i in range(size)])  1.95 us
  transfers between devices with their start and end apart: 7, of which 4 were waited for; matrix products, arithmetic and copies ran while one was open for 13% of the time, Pallas kernels for 0%

profile of v17, /device:TPU:15, one launch (start us, length us, event | category | flops | bytes accessed | tf_op | source)
XLA Modules:
  0.0 72.7 jit_solution(15848026140357615932)
XLA Ops:
  0.0 1.3 %copy.14 = bf16[16,8,24,128]{3,2,1,0:T(8,128)(2,1)S(1)} copy(bf16[16,8,24,128]{3,1,2,0:T(8,128)(2,1)} %bitcast.10) | data formatting | bytes 1572864
  1.3 0.0 copy-start.3
  1.3 0.7 copy.13
  2.0 0.3 stack_reshape.3
  2.3 0.1 copy-done.3
  2.4 0.0 copy-start.4
  2.4 0.0 copy-start.5
  2.4 0.0 copy-start.6
  2.4 0.0 copy-start.7
  2.4 0.1 pad_maximum_fusion.k0.v0
  2.6 0.0 copy-start
  2.6 3.2 %collective-permute-start.5 = (bf16[2,128,3072]{2,1,0:T(8,128)(2,1)S(1)}, bf16[2,128,3072]{2,1,0:T(8,128)(2,1)S(1)}, u32[]{:S(2)}, u32[]{:S(2)}) collective-permute-start(bf16[2,128,3072]{2,1,0:T(8,128)(2,1)S(1)} %pad_maximum_fusion.k0.v0), channel_id=1, source_target_pairs={{0,2},{1,3},{2,4},{3,5},{4,6},{5,7},{6,8},{7,9},{8,10},{9,11},{10,... | collective-permute-start | bytes 4718600 | tf_op jit(solution)/shard_map/ppermute | solution.py:118
  6.5 0.6 fusion.1
  7.1 1.3 %scatter.9 = bf16[2,128]{1,0:T(2,128)(2,1)S(1)} dynamic-update-slice(bf16[2,128]{1,0:T(2,128)(2,1)S(1)} %scatter.6, bf16[1,1]{1,0:T(2,128)(2,1)} %bitcast.1, s32[]{:T(128)} %bitcast.2, s32[]{:T(128)} %bitcast.3) | dynamic-update-slice | bytes 8 | tf_op jit(solution)/shard_map/scatter | solution.py:107
  8.5 0.0 copy-done.4
  8.5 0.0 copy-done.5
  8.5 0.6 pad_maximum_fusion.4
  9.1 0.4 collective-permute-start
  9.5 30.0 %collective-permute-done = bf16[2,6272]{1,0:T(2,128)(2,1)} collective-permute-done((bf16[2,6272]{1,0:T(2,128)(2,1)}, bf16[2,6272]{1,0:T(2,128)(2,1)}, u32[]{:S(2)}, u32[]{:S(2)}) %collective-permute-start) | collective-permute-done | bytes 25120 | tf_op jit(solution)/shard_map/ppermute | solution.py:94
  39.5 0.8 %pad_maximum_fusion.3 = bf16[4,6272]{1,0:T(4,128)(2,1)S(1)} fusion(bf16[2,6272]{1,0:T(2,128)(2,1)} %collective-permute-done, bf16[2,128]{1,0:T(2,128)(2,1)S(1)} %scatter.9, bf16[2,3072]{1,0:T(2,128)(2,1)S(1)} %copy-done.4, bf16[2,3072]{1,0:T(2,128)(2,1)S(1)} %copy-done.5), kind=kLoop, calls=%fused_computation.3 | loop fusion | flops 200704 | bytes 100352 | tf_op jit(solution)/shard_map/concatenate | solution.py:95
  40.3 0.1 collective-permute-start.1
  40.4 7.4 %collective-permute-start.4 = (bf16[2,128,3072]{2,1,0:T(8,128)(2,1)S(1)}, bf16[2,128,3072]{2,1,0:T(8,128)(2,1)}, u32[]{:S(2)}, u32[]{:S(2)}) collective-permute-start(bf16[2,128,3072]{2,1,0:T(8,128)(2,1)S(1)} %pad_maximum_fusion.k0.v0), channel_id=1, source_target_pairs={{0,1},{2,3},{4,5},{6,7},{8,9},{10,11},{12,13},{14,15},{1,4},{3,6},... | collective-permute-start | bytes 4718600 | tf_op jit(solution)/shard_map/ppermute | solution.py:119
  47.9 0.0 collective-permute-done.5.k2.v2
  47.9 0.0 copy-start.1
  47.9 0.1 collective-permute-start.6
  48.0 0.0 collective-permute-done.1
  48.0 1.0 %pad_maximum_fusion.2 = bf16[8,6272]{1,0:T(8,128)(2,1)S(1)} fusion(bf16[4,6272]{1,0:T(4,128)(2,1)} %collective-permute-done.1, bf16[2,6272]{1,0:T(2,128)(2,1)} %collective-permute-done, bf16[2,128]{1,0:T(2,128)(2,1)S(1)} %scatter.9, bf16[2,3072]{1,0:T(2,128)(2,1)S(1)} %copy-done.4, bf16[2,3072]{1,0:T(2,128)(2,1)S(1)} %copy-done.5), kind=kLoop, calls=%fused_computation.2 | loop fusion | flops 501760 | bytes 200704 | tf_op jit(solution)/shard_map/concatenate | solution.py:95
  48.9 0.1 collective-permute-start.2
  49.7 3.4 %collective-permute-done.2 = bf16[8,6272]{1,0:T(8,128)(2,1)} collective-permute-done((bf16[8,6272]{1,0:T(8,128)(2,1)S(1)}, bf16[8,6272]{1,0:T(8,128)(2,1)}, u32[]{:S(2)}, u32[]{:S(2)}) %collective-permute-start.2) | collective-permute-done | bytes 100384 | tf_op jit(solution)/shard_map/ppermute | solution.py:94
  53.1 1.1 %pad_maximum_fusion.1 = bf16[16,6272]{1,0:T(8,128)(2,1)S(1)} fusion(bf16[8,6272]{1,0:T(8,128)(2,1)} %collective-permute-done.2, bf16[4,6272]{1,0:T(4,128)(2,1)} %collective-permute-done.1, bf16[2,6272]{1,0:T(2,128)(2,1)} %collective-permute-done, bf16[2,128]{1,0:T(2,128)(2,1)S(1)} %scatter.9, bf16[2,3072]{1,0:T(2,128)(2,1)S(1)} %copy-done.4, ...), kind=kLoop, calls=%fused_computation.1 | loop fusion | flops 1204224 | bytes 401408 | tf_op jit(solution)/shard_map/concatenate | solution.py:95
  54.1 1.3 %collective-permute-start.3 = (bf16[16,6272]{1,0:T(8,128)(2,1)S(1)}, bf16[16,6272]{1,0:T(8,128)(2,1)}, u32[]{:S(2)}, u32[]{:S(2)}) collective-permute-start(bf16[16,6272]{1,0:T(8,128)(2,1)S(1)} %pad_maximum_fusion.1), channel_id=1, source_target_pairs={{0,1},{1,0},{2,3},{3,2},{4,5},{5,4},{6,7},{7,6},{8,9},{9,8},{10,11... | collective-permute-start | bytes 602120 | tf_op jit(solution)/shard_map/ppermute | solution.py:94
  55.5 0.0 copy-done.6
  55.5 0.0 copy-done.7
  55.5 1.2 %collective-permute-done.3 = bf16[16,6272]{1,0:T(8,128)(2,1)} collective-permute-done((bf16[16,6272]{1,0:T(8,128)(2,1)S(1)}, bf16[16,6272]{1,0:T(8,128)(2,1)}, u32[]{:S(2)}, u32[]{:S(2)}) %collective-permute-start.3) | collective-permute-done | bytes 200736 | tf_op jit(solution)/shard_map/ppermute | solution.py:94
  56.7 2.8 %concatenate.29.ck.cv = bf16[32,6272]{1,0:T(8,128)(2,1)S(1)} concatenate(bf16[2,6272]{1,0:T(2,128)(2,1)} %pad_maximum_fusion.4, bf16[2,6272]{1,0:T(2,128)(2,1)} %collective-permute-done, bf16[4,6272]{1,0:T(4,128)(2,1)} %collective-permute-done.1, bf16[8,6272]{1,0:T(8,128)(2,1)} %collective-permute-done.2, bf16[16,6272]{1,0:T(8,128)(2,1)} %collective-permute-done.3), dimensions={0} | concatenate | bytes 802816 | tf_op jit(solution)/shard_map/concatenate | solution.py:95
  59.5 0.0 copy-start.2
  59.5 0.2 convert_reduce_fusion.1
  59.7 0.2 select_reduce_fusion
  59.9 0.7 pad_add_fusion.table_ref
  60.5 4.7 %collective-permute-done.4.k1.v1 = bf16[2,128,3072]{2,1,0:T(8,128)(2,1)} collective-permute-done((bf16[2,128,3072]{2,1,0:T(8,128)(2,1)S(1)}, bf16[2,128,3072]{2,1,0:T(8,128)(2,1)}, u32[]{:S(2)}, u32[]{:S(2)}) %collective-permute-start.4) | collective-permute-done | bytes 1572896 | tf_op jit(solution)/shard_map/ppermute | solution.py:119
  65.2 0.0 collective-permute-done.6.k3.v3
  65.2 0.0 copy-done
  65.2 0.0 copy-done.1
  65.2 0.0 copy-done.2
  65.2 7.5 %shard_map.100 = bf16[128,3072]{1,0:T(8,128)(2,1)} custom-call(s32[5]{0:T(128)} %pad_add_fusion.table_ref, bf16[128,3072]{1,0:T(8,128)(2,1)} %q_ref.1, bf16[2,128,3072]{2,1,0:T(8,128)(2,1)} %copy-done, bf16[2,128,3072]{2,1,0:T(8,128)(2,1)} %copy-done, bf16[2,128,3072]{2,1,0:T(8,128)(2,1)} %collective-permute-done.4.k1.v1, ...), custom_call_target="tpu_custom_call" | custom-call | flops 855638016 | bytes 8454144 | tf_op jit(solution)/shard_map/pallas_call | solution.py:80
  (3 shorter events, 0.0 us)
Async XLA Ops:
  1.3 1.1 %copy-start.3 = (bf16[128,3072]{1,0:T(8,128)(2,1)S(1)}, bf16[128,3072]{1,0:T(8,128)(2,1)}, u32[]{:S(2)}) copy-start(bf16[128,3072]{1,0:T(8,128)(2,1)} %param.16) | copy-start | bytes 2359300
  2.4 6.0 %copy-start.4 = (bf16[2,3072]{1,0:T(2,128)(2,1)S(1)}, bf16[2,3072]{1,0:T(2,128)(2,1)}, u32[]{:S(2)}) copy-start(bf16[2,3072]{1,0:T(2,128)(2,1)} %param.18) | copy-start | bytes 36868
  2.4 6.0 %copy-start.5 = (bf16[2,3072]{1,0:T(2,128)(2,1)S(1)}, bf16[2,3072]{1,0:T(2,128)(2,1)}, u32[]{:S(2)}) copy-start(bf16[2,3072]{1,0:T(2,128)(2,1)} %param.17) | copy-start | bytes 36868
  2.4 53.1 %copy-start.6 = (s32[3]{0:T(128)S(1)}, s32[3]{0:T(128)}, u32[]{:S(2)}) copy-start(s32[3]{0:T(128)} %constant.76.clone) | copy-start | bytes 40
  2.4 53.1 %copy-start.7 = (s32[3]{0:T(128)S(1)}, s32[3]{0:T(128)}, u32[]{:S(2)}) copy-start(s32[3]{0:T(128)} %constant.75.clone) | copy-start | bytes 40
  2.6 62.6 %copy-start = (bf16[2,128,3072]{2,1,0:T(8,128)(2,1)}, bf16[2,128,3072]{2,1,0:T(8,128)(2,1)S(1)}, u32[]{:S(2)}) copy-start(bf16[2,128,3072]{2,1,0:T(8,128)(2,1)S(1)} %pad_maximum_fusion.k0.v0) | copy-start | bytes 4718596
  2.6 45.3 %collective-permute-start.5 = (bf16[2,128,3072]{2,1,0:T(8,128)(2,1)S(1)}, bf16[2,128,3072]{2,1,0:T(8,128)(2,1)S(1)}, u32[]{:S(2)}, u32[]{:S(2)}) collective-permute-start(bf16[2,128,3072]{2,1,0:T(8,128)(2,1)S(1)} %pad_maximum_fusion.k0.v0), channel_id=1, source_target_pairs={{0,2},{1,3},{2,4},{3,5},{4,6},{5,7},{6,8},{7,9},{8,10},{9,11},{10,... | collective-permute-start | bytes 4718600 | tf_op jit(solution)/shard_map/ppermute | solution.py:118
  9.1 30.4 %collective-permute-start = (bf16[2,6272]{1,0:T(2,128)(2,1)}, bf16[2,6272]{1,0:T(2,128)(2,1)}, u32[]{:S(2)}, u32[]{:S(2)}) collective-permute-start(bf16[2,6272]{1,0:T(2,128)(2,1)} %pad_maximum_fusion.4), channel_id=1, source_target_pairs={{0,8},{1,9},{2,10},{3,11},{4,12},{5,13},{6,14},{7,15},{8,0},{9,1},... | collective-permute-start | bytes 75272 | tf_op jit(solution)/shard_map/ppermute | solution.py:94
  40.3 7.7 %collective-permute-start.1 = (bf16[4,6272]{1,0:T(4,128)(2,1)S(1)}, bf16[4,6272]{1,0:T(4,128)(2,1)}, u32[]{:S(2)}, u32[]{:S(2)}) collective-permute-start(bf16[4,6272]{1,0:T(4,128)(2,1)S(1)} %pad_maximum_fusion.3), channel_id=1, source_target_pairs={{0,4},{1,5},{2,6},{3,7},{4,0},{5,1},{6,2},{7,3},{8,12},{9,13},{10,... | collective-permute-start | bytes 150536 | tf_op jit(solution)/shard_map/ppermute | solution.py:94
  40.4 24.8 %collective-permute-start.4 = (bf16[2,128,3072]{2,1,0:T(8,128)(2,1)S(1)}, bf16[2,128,3072]{2,1,0:T(8,128)(2,1)}, u32[]{:S(2)}, u32[]{:S(2)}) collective-permute-start(bf16[2,128,3072]{2,1,0:T(8,128)(2,1)S(1)} %pad_maximum_fusion.k0.v0), channel_id=1, source_target_pairs={{0,1},{2,3},{4,5},{6,7},{8,9},{10,11},{12,13},{14,15},{1,4},{3,6},... | collective-permute-start | bytes 4718600 | tf_op jit(solution)/shard_map/ppermute | solution.py:119
  47.9 17.3 %copy-start.1 = (bf16[2,128,3072]{2,1,0:T(8,128)(2,1)}, bf16[2,128,3072]{2,1,0:T(8,128)(2,1)S(1)}, u32[]{:S(2)}) copy-start(bf16[2,128,3072]{2,1,0:T(8,128)(2,1)S(1)} %collective-permute-done.5.k2.v2) | copy-start | bytes 4718596
  47.9 17.3 %collective-permute-start.6 = (bf16[2,128,3072]{2,1,0:T(8,128)(2,1)S(1)}, bf16[2,128,3072]{2,1,0:T(8,128)(2,1)}, u32[]{:S(2)}, u32[]{:S(2)}) collective-permute-start(bf16[2,128,3072]{2,1,0:T(8,128)(2,1)S(1)} %collective-permute-done.5.k2.v2), channel_id=1, source_target_pairs={{0,1},{1,0},{2,3},{3,2},{4,5},{5,4},{6,7},{7,6},{8,9},{9,8},{10,11... | collective-permute-start | bytes 4718600 | tf_op jit(solution)/shard_map/ppermute | solution.py:121
  48.9 4.1 %collective-permute-start.2 = (bf16[8,6272]{1,0:T(8,128)(2,1)S(1)}, bf16[8,6272]{1,0:T(8,128)(2,1)}, u32[]{:S(2)}, u32[]{:S(2)}) collective-permute-start(bf16[8,6272]{1,0:T(8,128)(2,1)S(1)} %pad_maximum_fusion.2), channel_id=1, source_target_pairs={{0,2},{1,3},{2,0},{3,1},{4,6},{5,7},{6,4},{7,5},{8,10},{9,11},{10,... | collective-permute-start | bytes 301064 | tf_op jit(solution)/shard_map/ppermute | solution.py:94
  54.1 2.6 %collective-permute-start.3 = (bf16[16,6272]{1,0:T(8,128)(2,1)S(1)}, bf16[16,6272]{1,0:T(8,128)(2,1)}, u32[]{:S(2)}, u32[]{:S(2)}) collective-permute-start(bf16[16,6272]{1,0:T(8,128)(2,1)S(1)} %pad_maximum_fusion.1), channel_id=1, source_target_pairs={{0,1},{1,0},{2,3},{3,2},{4,5},{5,4},{6,7},{7,6},{8,9},{9,8},{10,11... | collective-permute-start | bytes 602120 | tf_op jit(solution)/shard_map/ppermute | solution.py:94
  59.5 5.7 %copy-start.2 = (bf16[32,6272]{1,0:T(8,128)(2,1)}, bf16[32,6272]{1,0:T(8,128)(2,1)S(1)}, u32[]{:S(2)}) copy-start(bf16[32,6272]{1,0:T(8,128)(2,1)S(1)} %concatenate.29.ck.cv) | copy-start | bytes 1204228
